TPU v7x, 256 devices: a whole 4x4x8 slice. The times are simulated.
256 devices in a mesh: dp: 32 (over x, y, core), expert: 8 (over z).
Axes of the slice: x: 4, y: 4, z: 8, core: 2. Of those that a mesh axis runs over, the one named last changes fastest.
Arguments:
- tokens: bfloat16 [32768, 2048], P(('dp', 'expert')), may hold values from -6 to 6
- expert_ids: int32 [32768, 3], P(('dp', 'expert')), may hold values from 0 to 7, as said below
- slot_index: int32 [32768, 3], P(('dp', 'expert')), may hold values from -1 to 47, as said below
- w_router: float32 [2048, 8], replicated, may hold values from -0.125 to 0.125
- w_gate: bfloat16 [8, 2048, 768], P('expert'), may hold values from -0.125 to 0.125
- w_up: bfloat16 [8, 2048, 768], P('expert'), may hold values from -0.125 to 0.125
- w_down: bfloat16 [8, 2048, 768], P('expert'), may hold values from -0.21875 to 0.21875
- grad_out: bfloat16 [32768, 2048], P(('dp', 'expert')), may hold values from -0.59765625 to 0.59765625
Outputs:
- layer_output: bfloat16 [32768, 2048], P(('dp', 'expert'))
- grad_tokens: bfloat16 [32768, 2048], P(('dp', 'expert'))
- grad_router: float32 [2048, 8], replicated
- grad_gate: float32 [8, 2048, 768], P('expert', 'dp')
- grad_up: float32 [8, 2048, 768], P('expert', 'dp')
- grad_down: float32 [8, 2048, 768], P('expert', 'dp')
Inputs may be any that keep to these rules, and one draw needn't show every extreme that they name: `expert_ids`: each token names 3 different experts. `slot_index`: the live choices of one device's 128 tokens to one expert take the slots 0, 1, 2, ... in the order of tokens and then choices, and choices past 48 of them get -1; in every draw some expert gets all 48 slots from every device.
All inputs are finite; a program needn't handle non-finite values.
Results may differ from a plain program's by a relative error of at most 0.025.
Values may be sent and summed in bfloat16 or wider, within the bound.
No kernel may reach another device: no remote copies, remote signals or barrier semaphores. Data moves between devices by JAX's collectives and lax.ppermute only.
A program may use at most 128 MiB of HBM per device.

v0:
```python
import jax
import jax.numpy as jnp
from jax import lax
from jax.sharding import PartitionSpec as P


def silu_parts(hidden):
    sigmoid_val = jax.nn.sigmoid(hidden)
    return (hidden * sigmoid_val, sigmoid_val * (1.0 + hidden * (1.0 - sigmoid_val)))


def on_device(tokens, expert_ids, slot_index, w_router, w_gate, w_up, w_down, grad_out):
    tok_count, width = tokens.shape
    choice_count = expert_ids.shape[1]
    expert_count = w_router.shape[1]
    local_count = w_gate.shape[0]
    hidden_width = w_gate.shape[2]
    sender_count = lax.axis_size("expert")
    own_rows = width // lax.axis_size("dp")
    slot_count = tok_count * choice_count // expert_count
    highest = lax.Precision.HIGHEST
    tokens_wide = tokens.astype(jnp.float32)
    scores = jax.nn.sigmoid(jnp.dot(tokens_wide, w_router, precision=highest))
    picker = (
        expert_ids[:, :, None] == jnp.arange(expert_count, dtype=jnp.int32)[None, None, :]
    ).astype(jnp.float32)
    picked = jnp.sum(picker * scores[:, None, :], axis=2)
    pick_sum = jnp.sum(picked, axis=1, keepdims=True)
    gate_value = picked / pick_sum
    is_live = slot_index >= 0
    live_gate = jnp.where(is_live, gate_value, 0.0)
    position = jnp.where(is_live, expert_ids * slot_count + slot_index, expert_count * slot_count)
    owner_table = jnp.full((expert_count * slot_count + 1,), tok_count * choice_count, jnp.int32)
    owner_table = owner_table.at[position.reshape(-1)].set(
        jnp.arange(tok_count * choice_count, dtype=jnp.int32)
    )
    owner_table = owner_table[: expert_count * slot_count]
    zero_row = jnp.zeros((1, width), jnp.bfloat16)
    token_pad = jnp.concatenate([tokens, zero_row], axis=0)
    outgoing = token_pad[owner_table // choice_count].reshape(expert_count, slot_count, width)
    received = lax.all_to_all(outgoing, "expert", split_axis=0, concat_axis=0, tiled=True)
    item_count = received.shape[1]
    expert_row_block = received.reshape(sender_count, local_count, item_count, width)
    hidden_gate = jnp.einsum(
        "slnd,ldf->slnf", expert_row_block, w_gate, preferred_element_type=jnp.float32
    )
    hidden_up = jnp.einsum(
        "slnd,ldf->slnf", expert_row_block, w_up, preferred_element_type=jnp.float32
    )
    expert_activated = (silu_parts(hidden_gate)[0] * hidden_up).astype(jnp.bfloat16)
    expert_out = jnp.einsum(
        "slnf,ldf->slnd", expert_activated, w_down, preferred_element_type=jnp.float32
    ).astype(jnp.bfloat16)
    returned = lax.all_to_all(
        expert_out.reshape(sender_count * local_count, item_count, width),
        "expert",
        split_axis=0,
        concat_axis=0,
        tiled=True,
    )
    flat_shape = (sender_count * local_count, item_count, hidden_width)
    results = (
        returned,
        received,
        hidden_gate.reshape(flat_shape),
        hidden_up.reshape(flat_shape),
        expert_activated.reshape(flat_shape),
    )
    returned = results[0]
    received = results[1]
    out_pad = jnp.concatenate([returned.reshape(-1, width), zero_row], axis=0)
    dy_wide = grad_out.astype(jnp.float32)
    mixed = jnp.zeros((tok_count, width), jnp.float32)
    gate_grads = []
    for which in range(choice_count):
        got_row = out_pad[position[:, which]].astype(jnp.float32)
        mixed = mixed + live_gate[:, which : which + 1] * got_row
        gate_grads.append(jnp.sum(dy_wide * got_row, axis=1))
    layer_output = mixed.astype(jnp.bfloat16)
    gate_grad = jnp.stack(gate_grads, axis=1)
    gate_pad = jnp.concatenate([live_gate.reshape(-1), jnp.zeros((1,), jnp.float32)])
    grad_pad = jnp.concatenate([grad_out, zero_row], axis=0)
    grad_rows = (
        gate_pad[owner_table][:, None] * grad_pad[owner_table // choice_count].astype(jnp.float32)
    ).astype(jnp.bfloat16)
    grad_rows = grad_rows.reshape(expert_count, slot_count, width)
    block_shape = (sender_count, local_count, slot_count, width)
    arrived = lax.all_to_all(grad_rows, "expert", split_axis=0, concat_axis=0, tiled=True).reshape(
        block_shape
    )
    row_block = received.reshape(block_shape)
    hidden_shape = (sender_count, local_count, slot_count, hidden_width)
    hidden_gate = results[2].reshape(hidden_shape)
    hidden_up = results[3].reshape(hidden_shape)
    activated = results[4].reshape(hidden_shape)
    silu_value, silu_slope = silu_parts(hidden_gate)
    grad_act = jnp.einsum("slnd,ldf->slnf", arrived, w_down, preferred_element_type=jnp.float32)
    gate_delta = (grad_act * hidden_up * silu_slope).astype(jnp.bfloat16)
    up_delta = (grad_act * silu_value).astype(jnp.bfloat16)
    row_grad = (
        jnp.einsum("slnf,ldf->slnd", gate_delta, w_gate, preferred_element_type=jnp.float32)
        + jnp.einsum("slnf,ldf->slnd", up_delta, w_up, preferred_element_type=jnp.float32)
    ).astype(jnp.bfloat16)
    sent_back = lax.all_to_all(
        row_grad.reshape(sender_count * local_count, slot_count, width),
        "expert",
        split_axis=0,
        concat_axis=0,
        tiled=True,
    )
    piece = row_block
    gate_part = jnp.einsum("slnd,slnf->dlf", piece, gate_delta, preferred_element_type=jnp.float32)
    up_part = jnp.einsum("slnd,slnf->dlf", piece, up_delta, preferred_element_type=jnp.float32)
    gate_part, up_part = (gate_part, up_part)
    piece = arrived
    down_part = (
        jnp.einsum("slnd,slnf->dlf", piece, activated, preferred_element_type=jnp.float32)
        .reshape(lax.axis_size("dp") * own_rows, local_count * hidden_width)
        .reshape(lax.axis_size("dp") * own_rows, local_count, hidden_width)
    )
    joined = lax.psum_scatter(
        jnp.concatenate([gate_part, up_part, down_part], axis=2)
        .reshape(lax.axis_size("dp") * own_rows, local_count * 3 * hidden_width)
        .astype(jnp.bfloat16),
        "dp",
        scatter_dimension=0,
        tiled=True,
    ).astype(jnp.float32)
    triple_view = joined.reshape(-1, local_count, 3, hidden_width)
    grad_gate = jnp.transpose(triple_view[:, :, 0, :], (1, 0, 2))
    grad_up = jnp.transpose(triple_view[:, :, 1, :], (1, 0, 2))
    grad_down = jnp.transpose(triple_view[:, :, 2, :], (1, 0, 2))
    back_pad = jnp.concatenate([sent_back.reshape(-1, width), zero_row], axis=0)
    row_sum = jnp.zeros((tok_count, width), jnp.float32)
    for which in range(choice_count):
        row_sum = row_sum + back_pad[position[:, which]].astype(jnp.float32)
    cross_term = jnp.sum(gate_grad * gate_value, axis=1, keepdims=True)
    pick_delta = (gate_grad - cross_term) / pick_sum * picked * (1.0 - picked)
    logit_grad = jnp.sum(picker * pick_delta[:, :, None], axis=1)
    grad_tokens = (row_sum + jnp.dot(logit_grad, w_router.T, precision=highest)).astype(
        jnp.bfloat16
    )
    grad_router = lax.psum(jnp.dot(tokens_wide.T, logit_grad, precision=highest), ("dp", "expert"))
    return (layer_output, grad_tokens, grad_router, grad_gate, grad_up, grad_down)


def solution(mesh):
    return jax.shard_map(
        on_device,
        mesh=mesh,
        in_specs=(
            P(("dp", "expert"), None),
            P(("dp", "expert"), None),
            P(("dp", "expert"), None),
            P(),
            P("expert", None, None),
            P("expert", None, None),
            P("expert", None, None),
            P(("dp", "expert"), None),
        ),
        out_specs=(
            P(("dp", "expert"), None),
            P(("dp", "expert"), None),
            P(),
            P("expert", "dp", None),
            P("expert", "dp", None),
            P("expert", "dp", None),
        ),
        check_vma=False,
    )
```

profile of v0, /device:TPU:1, one launch (start us, length us, event | category | flops | bytes accessed | tf_op | source)
XLA Modules:
  0.0 503.2 jit_solution(17069465970971020080)
XLA Ops:
  9.2 2.9 scatter_custom_fusion
  14.1 6.2 %gather_fusion = bf16[384,2048]{1,0:T(8,128)(2,1)} fusion(bf16[129,2048]{1,0:T(8,128)(2,1)} %concatenate.23, s32[1024]{0:T(1024)S(1)} %get-tuple-element.27), kind=kCustom, calls=%fused_computation | custom fusion | bytes 3147264 | tf_op jit(solution)/shard_map/gather | solution.py:40
  20.3 9.0 %all-to-all-start = ((bf16[8,48,2048]{2,1,0:T(8,128)(2,1)}), bf16[8,48,2048]{2,1,0:T(8,128)(2,1)}, u32[]{:S(2)}, u32[]{:S(2)}) async-start(bf16[8,48,2048]{2,1,0:T(8,128)(2,1)} %bitcast.129), calls=%async_computation | async-start | bytes 3145728 | tf_op jit(solution)/shard_map/all_to_all | solution.py:41
  31.2 6.2 %gather_fusion.5 = bf16[384,2048]{1,0:T(8,128)(2,1)} fusion(bf16[129,2048]{1,0:T(8,128)(2,1)} %concatenate.26, s32[1024]{0:T(1024)S(1)} %get-tuple-element.27), kind=kCustom, calls=%fused_computation.5 | custom fusion | bytes 3147264 | tf_op jit(solution)/shard_map/gather | solution.py:84
  39.3 2.8 gather_fusion.4
  42.2 2.9 fusion
  45.1 24.7 %all-to-all-done = bf16[8,48,2048]{2,1,0:T(8,128)(2,1)} async-done(((bf16[8,48,2048]{2,1,0:T(8,128)(2,1)}), bf16[8,48,2048]{2,1,0:T(8,128)(2,1)}, u32[]{:S(2)}, u32[]{:S(2)}) %all-to-all-start) | async-done | bytes 1572896 | tf_op jit(solution)/shard_map/all_to_all | solution.py:41
  69.8 4.3 all-to-all-start.2
  74.4 5.0 fusion.22
  79.3 3.8 fusion.25
  83.1 29.2 %all-to-all-done.2 = bf16[8,48,2048]{2,1,0:T(8,128)(2,1)} async-done(((bf16[8,48,2048]{2,1,0:T(8,128)(2,1)}), bf16[8,48,2048]{2,1,0:T(8,128)(2,1)}, u32[]{:S(2)}, u32[]{:S(2)}) %all-to-all-start.2) | async-done | bytes 1572896 | tf_op jit(solution)/shard_map/all_to_all | solution.py:88
  112.4 3.7 multiply_convert_fusion.1
  116.1 3.9 fusion.15
  120.0 3.3 fusion.14
  123.3 3.2 fusion.13
  126.6 4.5 maximum_bitcast_fusion
  131.0 12.4 %copy.41 = bf16[2048,2304]{1,0:T(8,128)(2,1)} copy(bf16[2048,2304]{0,1:T(8,128)(2,1)} %maximum_bitcast_fusion) | data formatting | bytes 18874368
  143.4 3.7 fusion.18
  147.1 4.5 all-to-all-start.1
  151.7 3.8 fusion.5
  158.1 31.7 %all-to-all-done.1 = bf16[8,48,2048]{2,1,0:T(8,128)(2,1)} async-done(((bf16[8,48,2048]{2,1,0:T(8,128)(2,1)}), bf16[8,48,2048]{2,1,0:T(8,128)(2,1)}, u32[]{:S(2)}, u32[]{:S(2)}) %all-to-all-start.1) | async-done | bytes 1572896 | tf_op jit(solution)/shard_map/all_to_all | solution.py:54
  189.8 4.3 all-to-all-start.3
  197.0 4.3 gather_fusion.2
  201.3 3.9 gather_fusion.3
  205.2 27.1 %all-to-all-done.3 = bf16[8,48,2048]{2,1,0:T(8,128)(2,1)} async-done(((bf16[8,48,2048]{2,1,0:T(8,128)(2,1)}), bf16[8,48,2048]{2,1,0:T(8,128)(2,1)}, u32[]{:S(2)}, u32[]{:S(2)}) %all-to-all-start.3) | async-done | bytes 1572896 | tf_op jit(solution)/shard_map/all_to_all | solution.py:104
  235.1 3.9 gather_fusion.8
  239.0 3.9 gather_fusion.7
  242.9 3.9 gather_fusion.1
  246.8 3.9 gather_fusion.6
  250.6 3.0 fusion.38
  254.7 3.3 fusion.21
  266.6 227.7 %all-reduce.6.cloned.1.call-done = f32[2048,8]{0,1:T(8,128)} async-done(((f32[2048,8]{0,1:T(8,128)}), f32[2048,8]{0,1:T(8,128)}) %all-reduce.6.cloned.1.call-update) | async-done | bytes 65552 | tf_op jit(solution)/shard_map/psum | solution.py:143
  (60 shorter events, 26.5 us)
Async XLA Ops:
  8.0 104.4 %copy-start = (bf16[1,2048,768]{2,1,0:T(8,128)(2,1)S(1)}, bf16[1,2048,768]{2,1,0:T(8,128)(2,1)}, u32[]{:S(2)}) copy-start(bf16[1,2048,768]{2,1,0:T(8,128)(2,1)} %param.14) | copy-start | bytes 9437188
  20.3 49.5 %all-to-all-start = ((bf16[8,48,2048]{2,1,0:T(8,128)(2,1)}), bf16[8,48,2048]{2,1,0:T(8,128)(2,1)}, u32[]{:S(2)}, u32[]{:S(2)}) async-start(bf16[8,48,2048]{2,1,0:T(8,128)(2,1)} %bitcast.129), calls=%async_computation | async-start | bytes 3145728 | tf_op jit(solution)/shard_map/all_to_all | solution.py:41
  31.2 6.2 %copy-start.2 = (f32[2048,8]{0,1:T(8,128)S(1)}, f32[2048,8]{0,1:T(8,128)}, u32[]{:S(2)}) copy-start(f32[2048,8]{0,1:T(8,128)} %param.11) | copy-start | bytes 196612
  31.2 7.8 %copy-start.3 = (s32[128,3]{0,1:T(4,128)S(1)}, s32[128,3]{0,1:T(4,128)}, u32[]{:S(2)}) copy-start(s32[128,3]{0,1:T(4,128)} %param.9) | copy-start | bytes 4612
  31.2 7.8 %copy-start.4 = (s32[128,3]{0,1:T(4,128)S(1)}, s32[128,3]{0,1:T(4,128)}, u32[]{:S(2)}) copy-start(s32[128,3]{0,1:T(4,128)} %param.10) | copy-start | bytes 4612
  69.8 42.6 %all-to-all-start.2 = ((bf16[8,48,2048]{2,1,0:T(8,128)(2,1)}), bf16[8,48,2048]{2,1,0:T(8,128)(2,1)}, u32[]{:S(2)}, u32[]{:S(2)}) async-start(bf16[8,48,2048]{2,1,0:T(8,128)(2,1)} %fusion), calls=%async_computation.2 | async-start | bytes 3145728 | tf_op jit(solution)/shard_map/all_to_all | solution.py:88
  74.1 183.9 %reduce-scatter.4.cloned.1.call-start = ((), (), s32[]{:S(2)}) async-start(), calls=%async_computation.6 | async-start | bytes 9732096
  74.3 5.0 copy-start.5
  116.1 3.9 copy-start.10
  116.1 3.9 copy-start.9
  116.1 7.2 %copy-start.7 = (bf16[8,1,48,768]{3,2,0,1:T(8,128)(2,1)}, bf16[8,1,48,768]{3,2,0,1:T(8,128)(2,1)S(1)}, u32[]{:S(2)}) copy-start(bf16[8,1,48,768]{3,2,0,1:T(8,128)(2,1)S(1)} %get-tuple-element.11) | copy-start | bytes 1769476
  147.1 42.7 %all-to-all-start.1 = ((bf16[8,48,2048]{2,1,0:T(8,128)(2,1)}), bf16[8,48,2048]{2,1,0:T(8,128)(2,1)}, u32[]{:S(2)}, u32[]{:S(2)}) async-start(bf16[8,48,2048]{2,1,0:T(8,128)(2,1)} %fusion.18), calls=%async_computation.1 | async-start | bytes 3145728 | tf_op jit(solution)/shard_map/all_to_all | solution.py:54
  151.6 3.9 copy-start.6
  151.7 3.9 copy-start.8
  189.8 42.5 %all-to-all-start.3 = ((bf16[8,48,2048]{2,1,0:T(8,128)(2,1)}), bf16[8,48,2048]{2,1,0:T(8,128)(2,1)}, u32[]{:S(2)}, u32[]{:S(2)}) async-start(bf16[8,48,2048]{2,1,0:T(8,128)(2,1)} %add_convert_fusion), calls=%async_computation.3 | async-start | bytes 3145728 | tf_op jit(solution)/shard_map/all_to_all | solution.py:104
  194.1 300.2 %all-reduce.6.cloned.1.call-start = ((), (), s32[]{:S(2)}) async-start(), calls=%async_computation.5 | async-start | bytes 131072 | tf_op jit(solution)/shard_map/psum | solution.py:143
  250.6 3.1 copy-start.1
Sparse Core Ops, SparseCore 0:
  143.6 99.7 reduce-scatter.3
Sparse Core Ops, SparseCore 1:
  254.8 239.4 all-reduce.5
where the time goes:
time: 505 us; the launch traced here: 503 us
  waiting for transfers between devices  340 us (67%)
  local copies, waits for them, and re-layouts  74.4 us (15%)
  matrix products  38.8 us (8%)
  starting transfers between devices  22.4 us (4%)
  between operations  15.8 us (3%)
  other arithmetic  11.4 us (2%)
    psum x1, waiting for transfers between devices, on_device(): lax.psum(jnp.dot(tokens_wide.T, logit_grad, precision=highest), ('dp', 'e...  228 us
    all_to_all x1, waiting for transfers between devices, on_device(): lax.all_to_all(expert_out.reshape(sender_count * local_count, item_count,...  31.7 us
    all_to_all x1, waiting for transfers between devices, on_device(): lax.all_to_all(grad_rows, 'expert', split_axis=0, concat_axis=0, tiled=True)  29.2 us
    all_to_all x1, waiting for transfers between devices, on_device(): lax.all_to_all(row_grad.reshape(sender_count * local_count, slot_count, w...  27.1 us
    all_to_all x1, waiting for transfers between devices, on_device(): lax.all_to_all(outgoing, 'expert', split_axis=0, concat_axis=0, tiled=True)  24.7 us
    unnamed x28, local copies, waits for them, and re-layouts  20.4 us
    gather x3, local copies, waits for them, and re-layouts, on_device(): got_row = out_pad[position[:, which]].astype(jnp.float32)  12.1 us
    gather x3, local copies, waits for them, and re-layouts, on_device(): row_sum = row_sum + back_pad[position[:, which]].astype(jnp.float32)  11.7 us
  transfers between devices with their start and end apart: 6, of which 5 were waited for; matrix products, arithmetic and copies ran while one was open for 16% of the time, Pallas kernels for 0%

commit v1 on v0

v1 whole, which is shorter than its diff:
```python
import jax
import jax.numpy as jnp
from jax import lax
from jax.sharding import PartitionSpec as P


def silu_parts(hidden):
    sigmoid_val = jax.nn.sigmoid(hidden)
    return (hidden * sigmoid_val, sigmoid_val * (1.0 + hidden * (1.0 - sigmoid_val)))


def butterfly_sum(value, axis):
    size = lax.axis_size(axis)
    step = 1
    while step < size:
        pairs = [(i, i ^ step) for i in range(size)]
        value = value + lax.ppermute(value, axis, pairs)
        step *= 2
    return value


def on_device(tokens, expert_ids, slot_index, w_router, w_gate, w_up, w_down, grad_out):
    tok_count, width = tokens.shape
    choice_count = expert_ids.shape[1]
    expert_count = w_router.shape[1]
    local_count = w_gate.shape[0]
    hidden_width = w_gate.shape[2]
    sender_count = lax.axis_size("expert")
    own_rows = width // lax.axis_size("dp")
    slot_count = tok_count * choice_count // expert_count
    highest = lax.Precision.HIGHEST
    tokens_wide = tokens.astype(jnp.float32)
    scores = jax.nn.sigmoid(jnp.dot(tokens_wide, w_router, precision=highest))
    picker = (
        expert_ids[:, :, None] == jnp.arange(expert_count, dtype=jnp.int32)[None, None, :]
    ).astype(jnp.float32)
    picked = jnp.sum(picker * scores[:, None, :], axis=2)
    pick_sum = jnp.sum(picked, axis=1, keepdims=True)
    gate_value = picked / pick_sum
    is_live = slot_index >= 0
    live_gate = jnp.where(is_live, gate_value, 0.0)
    position = jnp.where(is_live, expert_ids * slot_count + slot_index, expert_count * slot_count)
    owner_table = jnp.full((expert_count * slot_count + 1,), tok_count * choice_count, jnp.int32)
    owner_table = owner_table.at[position.reshape(-1)].set(
        jnp.arange(tok_count * choice_count, dtype=jnp.int32)
    )
    owner_table = owner_table[: expert_count * slot_count]
    zero_row = jnp.zeros((1, width), jnp.bfloat16)
    token_pad = jnp.concatenate([tokens, zero_row], axis=0)
    outgoing = token_pad[owner_table // choice_count].reshape(expert_count, slot_count, width)
    gate_pad = jnp.concatenate([live_gate.reshape(-1), jnp.zeros((1,), jnp.float32)])
    grad_pad = jnp.concatenate([grad_out, zero_row], axis=0)
    grad_rows = (
        gate_pad[owner_table][:, None] * grad_pad[owner_table // choice_count].astype(jnp.float32)
    ).astype(jnp.bfloat16)
    grad_rows = grad_rows.reshape(expert_count, slot_count, width)
    both_in = lax.all_to_all(
        jnp.concatenate([outgoing, grad_rows], axis=1), "expert", split_axis=0, concat_axis=0, tiled=True
    )
    block_shape = (sender_count, local_count, slot_count, width)
    row_block = both_in[:, :slot_count].reshape(block_shape)
    arrived = both_in[:, slot_count:].reshape(block_shape)
    hidden_gate = jnp.einsum(
        "slnd,ldf->slnf", row_block, w_gate, preferred_element_type=jnp.float32
    )
    hidden_up = jnp.einsum(
        "slnd,ldf->slnf", row_block, w_up, preferred_element_type=jnp.float32
    )
    silu_value, silu_slope = silu_parts(hidden_gate)
    activated = (silu_value * hidden_up).astype(jnp.bfloat16)
    expert_out = jnp.einsum(
        "slnf,ldf->slnd", activated, w_down, preferred_element_type=jnp.float32
    ).astype(jnp.bfloat16)
    grad_act = jnp.einsum("slnd,ldf->slnf", arrived, w_down, preferred_element_type=jnp.float32)
    gate_delta = (grad_act * hidden_up * silu_slope).astype(jnp.bfloat16)
    up_delta = (grad_act * silu_value).astype(jnp.bfloat16)
    row_grad = (
        jnp.einsum("slnf,ldf->slnd", gate_delta, w_gate, preferred_element_type=jnp.float32)
        + jnp.einsum("slnf,ldf->slnd", up_delta, w_up, preferred_element_type=jnp.float32)
    ).astype(jnp.bfloat16)
    flat_rows = (sender_count * local_count, slot_count, width)
    both_out = lax.all_to_all(
        jnp.concatenate([expert_out.reshape(flat_rows), row_grad.reshape(flat_rows)], axis=1),
        "expert",
        split_axis=0,
        concat_axis=0,
        tiled=True,
    )
    returned = both_out[:, :slot_count]
    sent_back = both_out[:, slot_count:]
    gate_part = jnp.einsum("slnd,slnf->dlf", row_block, gate_delta, preferred_element_type=jnp.float32)
    up_part = jnp.einsum("slnd,slnf->dlf", row_block, up_delta, preferred_element_type=jnp.float32)
    down_part = jnp.einsum("slnd,slnf->dlf", arrived, activated, preferred_element_type=jnp.float32)
    joined = lax.psum_scatter(
        jnp.concatenate([gate_part, up_part, down_part], axis=2)
        .reshape(lax.axis_size("dp") * own_rows, local_count * 3 * hidden_width)
        .astype(jnp.bfloat16),
        "dp",
        scatter_dimension=0,
        tiled=True,
    ).astype(jnp.float32)
    triple_view = joined.reshape(-1, local_count, 3, hidden_width)
    grad_gate = jnp.transpose(triple_view[:, :, 0, :], (1, 0, 2))
    grad_up = jnp.transpose(triple_view[:, :, 1, :], (1, 0, 2))
    grad_down = jnp.transpose(triple_view[:, :, 2, :], (1, 0, 2))
    out_pad = jnp.concatenate([returned.reshape(-1, width), zero_row], axis=0)
    back_pad = jnp.concatenate([sent_back.reshape(-1, width), zero_row], axis=0)
    dy_wide = grad_out.astype(jnp.float32)
    mixed = jnp.zeros((tok_count, width), jnp.float32)
    row_sum = jnp.zeros((tok_count, width), jnp.float32)
    gate_grads = []
    for which in range(choice_count):
        got_row = out_pad[position[:, which]].astype(jnp.float32)
        mixed = mixed + live_gate[:, which : which + 1] * got_row
        gate_grads.append(jnp.sum(dy_wide * got_row, axis=1))
        row_sum = row_sum + back_pad[position[:, which]].astype(jnp.float32)
    layer_output = mixed.astype(jnp.bfloat16)
    gate_grad = jnp.stack(gate_grads, axis=1)
    cross_term = jnp.sum(gate_grad * gate_value, axis=1, keepdims=True)
    pick_delta = (gate_grad - cross_term) / pick_sum * picked * (1.0 - picked)
    logit_grad = jnp.sum(picker * pick_delta[:, :, None], axis=1)
    grad_tokens = (row_sum + jnp.dot(logit_grad, w_router.T, precision=highest)).astype(
        jnp.bfloat16
    )
    router_part = jnp.dot(tokens_wide.T, logit_grad, precision=highest)
    grad_router = butterfly_sum(butterfly_sum(router_part, "expert"), "dp")
    return (layer_output, grad_tokens, grad_router, grad_gate, grad_up, grad_down)


def solution(mesh):
    return jax.shard_map(
        on_device,
        mesh=mesh,
        in_specs=(
            P(("dp", "expert"), None),
            P(("dp", "expert"), None),
            P(("dp", "expert"), None),
            P(),
            P("expert", None, None),
            P("expert", None, None),
            P("expert", None, None),
            P(("dp", "expert"), None),
        ),
        out_specs=(
            P(("dp", "expert"), None),
            P(("dp", "expert"), None),
            P(),
            P("expert", "dp", None),
            P("expert", "dp", None),
            P("expert", "dp", None),
        ),
        check_vma=False,
    )
```

time: 505 us -> 321 us (0.64)
  waiting for transfers between devices: 340 us -> 93 us
  blocking collectives: 0 us -> 81.4 us
  matrix products: 38.8 us -> 21.7 us
    psum x1 -> x0, waiting for transfers between devices: 228 us -> none  [on_device(): lax.psum(jnp.dot(tokens_wide.T, logit_grad, precision=highest), ('dp', 'e...]
    all_to_all x0 -> x1, blocking collectives: none -> 81.4 us  [on_device(): lax.all_to_all(jnp.concatenate([outgoing, grad_rows], axis=1), 'expert',...]
    all_to_all x4 -> x1, waiting for transfers between devices: 113 us -> 74.1 us  [on_device(): lax.all_to_all(jnp.concatenate([expert_out.reshape(flat_rows), row_grad.r...]
    ppermute x0 -> x8, waiting for transfers between devices: none -> 18.8 us  [butterfly_sum(): value = value + lax.ppermute(value, axis, pairs)]
    all_to_all x4 -> x1, starting transfers between devices: 22.1 us -> 4.46 us  [on_device(): lax.all_to_all(jnp.concatenate([expert_out.reshape(flat_rows), row_grad.r...]
    ppermute x0 -> x8, starting transfers between devices: none -> 13.8 us  [butterfly_sum(): value = value + lax.ppermute(value, axis, pairs)]
    dot_general x7, matrix products: 23.8 us -> 12.3 us  [the longest x1 2.63 us: on_device(): jnp.einsum('slnf,ldf->slnd', activated, w_down, preferred_element_type=jn...]
    unnamed x28 -> x33, local copies, waits for them, and re-layouts: 20.4 us -> 19.8 us
  transfers between devices with their start and end apart: 6 -> 10, of which waited for: 5 -> 7; matrix products, arithmetic and copies ran while one was open for 16% -> 14% of each run, Pallas kernels for 0% -> 0%
where the time goes in v1:
time: 321 us; the launch traced here: 318 us
  waiting for transfers between devices  93 us (29%)
  blocking collectives  81.4 us (25%)
  local copies, waits for them, and re-layouts  74 us (23%)
  matrix products  21.7 us (7%)
  starting transfers between devices  18.2 us (6%)
  other arithmetic  14.9 us (5%)
  between operations  14.4 us (4%)
    all_to_all x1, blocking collectives, on_device(): lax.all_to_all(jnp.concatenate([outgoing, grad_rows], axis=1), 'expert',...  81.4 us
    all_to_all x1, waiting for transfers between devices, on_device(): lax.all_to_all(jnp.concatenate([expert_out.reshape(flat_rows), row_grad.r...  74.1 us
    unnamed x33, local copies, waits for them, and re-layouts  19.8 us
    ppermute x8, waiting for transfers between devices, butterfly_sum(): value = value + lax.ppermute(value, axis, pairs)  18.8 us
    ppermute x8, starting transfers between devices, butterfly_sum(): value = value + lax.ppermute(value, axis, pairs)  13.8 us
    gather x3, local copies, waits for them, and re-layouts, on_device(): got_row = out_pad[position[:, which]].astype(jnp.float32)  11.7 us
    gather x3, local copies, waits for them, and re-layouts, on_device(): row_sum = row_sum + back_pad[position[:, which]].astype(jnp.float32)  11.6 us
  transfers between devices with their start and end apart: 10, of which 7 were waited for; matrix products, arithmetic and copies ran while one was open for 14% of the time, Pallas kernels for 0%

profile of v1, /device:TPU:1, one launch (start us, length us, event | category | flops | bytes accessed | tf_op | source)
XLA Modules:
  0.0 317.7 jit_solution(13984881418568510303)
XLA Ops:
  8.4 2.9 scatter_custom_fusion
  11.4 1.9 concatenate.31
  13.3 1.9 concatenate.29
  18.5 2.8 gather_fusion.1
  21.4 6.2 %gather_fusion.2 = bf16[384,2048]{1,0:T(8,128)(2,1)} fusion(bf16[129,2048]{1,0:T(8,128)(2,1)} %concatenate.31, s32[1024]{0:T(1024)S(1)} %get-tuple-element.29), kind=kCustom, calls=%fused_computation.2 | custom fusion | bytes 3147264 | tf_op jit(solution)/shard_map/gather | solution.py:54
  27.6 6.2 %gather_fusion = bf16[384,2048]{1,0:T(8,128)(2,1)} fusion(bf16[129,2048]{1,0:T(8,128)(2,1)} %concatenate.29, s32[1024]{0:T(1024)S(1)} %get-tuple-element.29), kind=kCustom, calls=%fused_computation | custom fusion | bytes 3147264 | tf_op jit(solution)/shard_map/gather | solution.py:50
  33.8 1.8 fusion
  36.1 81.4 %all_to_all.10 = bf16[8,96,2048]{2,1,0:T(8,128)(2,1)S(1)} all-to-all(bf16[8,96,2048]{2,1,0:T(8,128)(2,1)S(1)} %pad_maximum_fusion), channel_id=1, replica_groups=mesh['dp'=32,'expert'=8] {'expert'}, dimensions={0} | all-to-all | bytes 6291456 | tf_op jit(solution)/shard_map/all_to_all | solution.py:57
  122.5 1.8 fusion.15
  128.1 4.5 %maximum_bitcast_fusion = bf16[2048,2304]{0,1:T(8,128)(2,1)} fusion(bf16[2048,1,768]{0,2,1:T(8,128)(2,1)S(1)} %fusion.15, bf16[2048,1,768]{0,2,1:T(8,128)(2,1)S(1)} %fusion.14, bf16[2048,1,768]{0,2,1:T(8,128)(2,1)S(1)} %fusion.13), kind=kLoop, calls=%fused_computation.10 | loop fusion | flops 28311552 | bytes 18874368 | tf_op jit(solution)/shard_map/convert_element_type | solution.py:97
  132.6 12.2 %copy.41 = bf16[2048,2304]{1,0:T(8,128)(2,1)} copy(bf16[2048,2304]{0,1:T(8,128)(2,1)} %maximum_bitcast_fusion) | data formatting | bytes 18874368
  144.8 2.6 fusion.18
  150.9 2.0 pad_maximum_fusion.1
  152.9 4.5 %all-to-all-start.1 = ((bf16[8,96,2048]{2,1,0:T(8,128)(2,1)}), bf16[8,96,2048]{2,1,0:T(8,128)(2,1)}, u32[]{:S(2)}, u32[]{:S(2)}) async-start(bf16[8,96,2048]{2,1,0:T(8,128)(2,1)} %pad_maximum_fusion.1), calls=%async_computation.1 | async-start | bytes 6291456 | tf_op jit(solution)/shard_map/all_to_all | solution.py:82
  157.4 74.1 %all-to-all-done.1 = bf16[8,96,2048]{2,1,0:T(8,128)(2,1)} async-done(((bf16[8,96,2048]{2,1,0:T(8,128)(2,1)}), bf16[8,96,2048]{2,1,0:T(8,128)(2,1)}, u32[]{:S(2)}, u32[]{:S(2)}) %all-to-all-start.1) | async-done | bytes 3145760 | tf_op jit(solution)/shard_map/all_to_all | solution.py:82
  231.6 3.7 %fusion.59 = (bf16[8,48,2048]{2,1,0:T(8,128)(2,1)}, bf16[8,48,2048]{2,1,0:T(8,128)(2,1)S(1)}) fusion(bf16[8,96,2048]{2,1,0:T(8,128)(2,1)} %all-to-all-done.1), kind=kLoop, calls=%fused_computation.109 | loop fusion | bytes 6291456 | tf_op jit(solution)/shard_map/slice | solution.py:90
  236.5 3.9 %gather_fusion.3 = bf16[128,2048]{1,0:T(8,128)(2,1)} fusion(bf16[385,2048]{1,0:T(8,128)(2,1)} %concatenate.34, s32[1024]{0:T(1024)S(1)} %pad_clamp_fusion.2), kind=kCustom, calls=%fused_computation.3 | custom fusion | bytes 1049088 | tf_op jit(solution)/shard_map/gather | solution.py:113
  240.4 3.9 %gather_fusion.4 = bf16[128,2048]{1,0:T(8,128)(2,1)} fusion(bf16[385,2048]{1,0:T(8,128)(2,1)} %concatenate.34, s32[1024]{0:T(1024)S(1)} %get-tuple-element.31), kind=kCustom, calls=%fused_computation.4 | custom fusion | bytes 1049088 | tf_op jit(solution)/shard_map/gather | solution.py:113
  244.3 3.9 %gather_fusion.5 = bf16[128,2048]{1,0:T(8,128)(2,1)} fusion(bf16[385,2048]{1,0:T(8,128)(2,1)} %concatenate.34, s32[1024]{0:T(1024)S(1)} %get-tuple-element.30), kind=kCustom, calls=%fused_computation.5 | custom fusion | bytes 1049088 | tf_op jit(solution)/shard_map/gather | solution.py:113
  248.2 3.1 fusion.40
  252.8 3.1 collective-permute-done
  256.0 4.4 %collective-permute-done.1 = f32[2048,8]{0,1:T(8,128)S(1)} collective-permute-done((f32[2048,8]{0,1:T(8,128)S(1)}, f32[2048,8]{0,1:T(8,128)S(1)}, u32[]{:S(2)}, u32[]{:S(2)}) %collective-permute-start.1) | collective-permute-done | bytes 65568 | tf_op jit(solution)/shard_map/ppermute | solution.py:17
  260.5 7.0 %collective-permute-done.2 = f32[2048,8]{0,1:T(8,128)S(1)} collective-permute-done((f32[2048,8]{0,1:T(8,128)S(1)}, f32[2048,8]{0,1:T(8,128)S(1)}, u32[]{:S(2)}, u32[]{:S(2)}) %collective-permute-start.2) | collective-permute-done | bytes 65568 | tf_op jit(solution)/shard_map/ppermute | solution.py:17
  267.6 4.7 %collective-permute-start.3 = (f32[2048,8]{0,1:T(8,128)S(1)}, f32[2048,8]{0,1:T(8,128)S(1)}, u32[]{:S(2)}, u32[]{:S(2)}) collective-permute-start(f32[2048,8]{0,1:T(8,128)S(1)} %add.118), channel_id=1, source_target_pairs={{0,8},{8,0},{16,24},{24,16},{32,40},{40,32},{48,56},{56,48},{64,72... | collective-permute-start | bytes 196616 | tf_op jit(solution)/shard_map/ppermute | solution.py:17
  276.4 3.1 collective-permute-start.5
  284.1 3.9 %gather_fusion.8 = bf16[128,2048]{1,0:T(8,128)(2,1)} fusion(bf16[385,2048]{1,0:T(8,128)(2,1)} %concatenate.35, s32[1024]{0:T(1024)S(1)} %get-tuple-element.30), kind=kCustom, calls=%fused_computation.8 | custom fusion | bytes 1049088 | tf_op jit(solution)/shard_map/gather | solution.py:116
  287.9 3.9 %gather_fusion.7 = bf16[128,2048]{1,0:T(8,128)(2,1)} fusion(bf16[385,2048]{1,0:T(8,128)(2,1)} %concatenate.35, s32[1024]{0:T(1024)S(1)} %get-tuple-element.31), kind=kCustom, calls=%fused_computation.7 | custom fusion | bytes 1049088 | tf_op jit(solution)/shard_map/gather | solution.py:116
  291.8 3.9 %gather_fusion.6 = bf16[128,2048]{1,0:T(8,128)(2,1)} fusion(bf16[385,2048]{1,0:T(8,128)(2,1)} %concatenate.35, s32[1024]{0:T(1024)S(1)} %pad_clamp_fusion.2), kind=kCustom, calls=%fused_computation.6 | custom fusion | bytes 1049088 | tf_op jit(solution)/shard_map/gather | solution.py:116
  295.7 2.6 collective-permute-start.7
  298.3 3.3 %fusion.21 = bf16[128,2048]{1,0:T(8,128)(2,1)} fusion(f32[128,8]{0,1:T(8,128)S(1)} %select_reduce_fusion.2, f32[2048,8]{0,1:T(8,128)S(1)} %copy-done.3, bf16[128,2048]{1,0:T(8,128)(2,1)} %gather_fusion.8, bf16[128,2048]{1,0:T(8,128)(2,1)} %gather_fusion.7, bf16[128,2048]{1,0:T(8,128)(2,1)} %gather_fusion.6), kind=kOutput, calls=%fused_computation.36 | convolution fusion | flops 27000832 | bytes 2166784 | tf_op jit(solution)/shard_map/dot_general | solution.py:122
  302.2 2.0 copy.42
  304.2 2.1 fusion.60
  (84 shorter events, 34.0 us)
Async XLA Ops:
  7.2 113.6 %copy-start = (bf16[1,2048,768]{2,1,0:T(8,128)(2,1)S(1)}, bf16[1,2048,768]{2,1,0:T(8,128)(2,1)}, u32[]{:S(2)}) copy-start(bf16[1,2048,768]{2,1,0:T(8,128)(2,1)} %param.14) | copy-start | bytes 9437188
  7.2 295.0 %reduce-scatter.4.cloned.1.call-start = ((), (), s32[]{:S(2)}) async-start(), calls=%async_computation.3 | async-start | bytes 9732096
  33.8 1.9 copy-start.2
  36.1 81.4 %copy-start.5 = (bf16[1,2048,768]{2,1,0:T(8,128)(2,1)S(1)}, bf16[1,2048,768]{2,1,0:T(8,128)(2,1)}, u32[]{:S(2)}) copy-start(bf16[1,2048,768]{2,1,0:T(8,128)(2,1)} %param.13) | copy-start | bytes 9437188
  117.4 1.9 copy-start.7
  122.5 1.9 copy-start.13
  122.5 1.9 copy-start.11
  122.5 3.7 %copy-start.9 = (bf16[8,1,48,768]{3,2,0,1:T(8,128)(2,1)}, bf16[8,1,48,768]{3,2,0,1:T(8,128)(2,1)S(1)}, u32[]{:S(2)}) copy-start(bf16[8,1,48,768]{3,2,0,1:T(8,128)(2,1)S(1)} %get-tuple-element.14) | copy-start | bytes 1769476
  144.8 2.7 copy-start.6
  144.8 2.7 copy-start.12
  147.4 1.9 copy-start.8
  147.5 2.0 copy-start.10
  152.9 78.6 %all-to-all-start.1 = ((bf16[8,96,2048]{2,1,0:T(8,128)(2,1)}), bf16[8,96,2048]{2,1,0:T(8,128)(2,1)}, u32[]{:S(2)}, u32[]{:S(2)}) async-start(bf16[8,96,2048]{2,1,0:T(8,128)(2,1)} %pad_maximum_fusion.1), calls=%async_computation.1 | async-start | bytes 6291456 | tf_op jit(solution)/shard_map/all_to_all | solution.py:82
  244.3 7.0 %copy-start.4 = (s32[128,3]{0,1:T(4,128)S(1)}, s32[128,3]{0,1:T(4,128)}, u32[]{:S(2)}) copy-start(s32[128,3]{0,1:T(4,128)} %param.9) | copy-start | bytes 4612
  248.2 34.6 %copy-start.1 = (bf16[8,48,2048]{2,1,0:T(8,128)(2,1)S(1)}, bf16[8,48,2048]{2,1,0:T(8,128)(2,1)}, u32[]{:S(2)}) copy-start(bf16[8,48,2048]{2,1,0:T(8,128)(2,1)} %get-tuple-element.11) | copy-start | bytes 4718596
  252.7 3.2 %collective-permute-start = (f32[2048,8]{0,1:T(8,128)S(1)}, f32[2048,8]{0,1:T(8,128)S(1)}, u32[]{:S(2)}, u32[]{:S(2)}) collective-permute-start(f32[2048,8]{0,1:T(8,128)S(1)} %convolution_bitcast_fusion), channel_id=1, source_target_pairs={{0,1},{1,0},{2,3},{3,2},{4,5},{5,4},{6,7},{7,6},{8,9},{9,8},{10,11... | collective-permute-start | bytes 196616 | tf_op jit(solution)/shard_map/ppermute | solution.py:17
  255.9 4.5 %collective-permute-start.1 = (f32[2048,8]{0,1:T(8,128)S(1)}, f32[2048,8]{0,1:T(8,128)S(1)}, u32[]{:S(2)}, u32[]{:S(2)}) collective-permute-start(f32[2048,8]{0,1:T(8,128)S(1)} %add.116), channel_id=1, source_target_pairs={{0,2},{1,3},{2,0},{3,1},{4,6},{5,7},{6,4},{7,5},{8,10},{9,11},{10,... | collective-permute-start | bytes 196616 | tf_op jit(solution)/shard_map/ppermute | solution.py:17
  260.4 7.1 %collective-permute-start.2 = (f32[2048,8]{0,1:T(8,128)S(1)}, f32[2048,8]{0,1:T(8,128)S(1)}, u32[]{:S(2)}, u32[]{:S(2)}) collective-permute-start(f32[2048,8]{0,1:T(8,128)S(1)} %add.117), channel_id=1, source_target_pairs={{0,4},{1,5},{2,6},{3,7},{4,0},{5,1},{6,2},{7,3},{8,12},{9,13},{10,... | collective-permute-start | bytes 196616 | tf_op jit(solution)/shard_map/ppermute | solution.py:17
  267.6 5.6 %collective-permute-start.3 = (f32[2048,8]{0,1:T(8,128)S(1)}, f32[2048,8]{0,1:T(8,128)S(1)}, u32[]{:S(2)}, u32[]{:S(2)}) collective-permute-start(f32[2048,8]{0,1:T(8,128)S(1)} %add.118), channel_id=1, source_target_pairs={{0,8},{8,0},{16,24},{24,16},{32,40},{40,32},{48,56},{56,48},{64,72... | collective-permute-start | bytes 196616 | tf_op jit(solution)/shard_map/ppermute | solution.py:17
  273.2 3.2 %collective-permute-start.4 = (f32[2048,8]{0,1:T(8,128)S(1)}, f32[2048,8]{0,1:T(8,128)S(1)}, u32[]{:S(2)}, u32[]{:S(2)}) collective-permute-start(f32[2048,8]{0,1:T(8,128)S(1)} %add.119), channel_id=1, source_target_pairs={{0,16},{8,24},{16,0},{24,8},{32,48},{40,56},{48,32},{56,40},{64,80... | collective-permute-start | bytes 196616 | tf_op jit(solution)/shard_map/ppermute | solution.py:17
  276.4 4.8 %collective-permute-start.5 = (f32[2048,8]{0,1:T(8,128)S(1)}, f32[2048,8]{0,1:T(8,128)S(1)}, u32[]{:S(2)}, u32[]{:S(2)}) collective-permute-start(f32[2048,8]{0,1:T(8,128)S(1)} %add.120), channel_id=1, source_target_pairs={{0,32},{8,40},{16,48},{24,56},{32,0},{40,8},{48,16},{56,24},{64,96... | collective-permute-start | bytes 196616 | tf_op jit(solution)/shard_map/ppermute | solution.py:17
  281.2 14.5 %collective-permute-start.6 = (f32[2048,8]{0,1:T(8,128)S(1)}, f32[2048,8]{0,1:T(8,128)S(1)}, u32[]{:S(2)}, u32[]{:S(2)}) collective-permute-start(f32[2048,8]{0,1:T(8,128)S(1)} %add.121), channel_id=1, source_target_pairs={{0,64},{8,72},{16,80},{24,88},{32,96},{40,104},{48,112},{56,120},{... | collective-permute-start | bytes 196616 | tf_op jit(solution)/shard_map/ppermute | solution.py:17
  291.8 6.5 %copy-start.3 = (f32[2048,8]{0,1:T(8,128)S(1)}, f32[2048,8]{0,1:T(8,128)}, u32[]{:S(2)}) copy-start(f32[2048,8]{0,1:T(8,128)} %param.11) | copy-start | bytes 196612
  295.7 5.9 %collective-permute-start.7 = (f32[2048,8]{0,1:T(8,128)S(1)}, f32[2048,8]{0,1:T(8,128)S(1)}, u32[]{:S(2)}, u32[]{:S(2)}) collective-permute-start(f32[2048,8]{0,1:T(8,128)S(1)} %add.122), channel_id=1, source_target_pairs={{0,128},{8,136},{16,144},{24,152},{32,160},{40,168},{48,176},{56,1... | collective-permute-start | bytes 196616 | tf_op jit(solution)/shard_map/ppermute | solution.py:17
Sparse Core Ops, SparseCore 0:
  144.9 99.3 reduce-scatter.3

commit v2 on v1

--- a/solution.py
+++ b/solution.py
@@ -9,13 +9,25 @@
     return (hidden * sigmoid_val, sigmoid_val * (1.0 + hidden * (1.0 - sigmoid_val)))
 
 
-def butterfly_sum(value, axis):
+def group_sum(value, axis, low_bit, bits):
     size = lax.axis_size(axis)
-    step = 1
-    while step < size:
+    got = [value]
+    for offset in range(1, 2**bits):
+        step = offset << low_bit
         pairs = [(i, i ^ step) for i in range(size)]
-        value = value + lax.ppermute(value, axis, pairs)
-        step *= 2
+        got.append(lax.ppermute(value, axis, pairs))
+    while len(got) > 1:
+        got = [got[i] + got[i + 1] for i in range(0, len(got), 2)]
+    return got[0]
+
+
+def all_sum(value, axis):
+    size = lax.axis_size(axis)
+    low_bit = 0
+    while (1 << low_bit) < size:
+        bits = min(3, (size - 1).bit_length() - low_bit)
+        value = group_sum(value, axis, low_bit, bits)
+        low_bit += bits
     return value
 
 
@@ -40,19 +52,15 @@
     is_live = slot_index >= 0
     live_gate = jnp.where(is_live, gate_value, 0.0)
     position = jnp.where(is_live, expert_ids * slot_count + slot_index, expert_count * slot_count)
-    owner_table = jnp.full((expert_count * slot_count + 1,), tok_count * choice_count, jnp.int32)
-    owner_table = owner_table.at[position.reshape(-1)].set(
-        jnp.arange(tok_count * choice_count, dtype=jnp.int32)
-    )
-    owner_table = owner_table[: expert_count * slot_count]
-    zero_row = jnp.zeros((1, width), jnp.bfloat16)
-    token_pad = jnp.concatenate([tokens, zero_row], axis=0)
-    outgoing = token_pad[owner_table // choice_count].reshape(expert_count, slot_count, width)
-    gate_pad = jnp.concatenate([live_gate.reshape(-1), jnp.zeros((1,), jnp.float32)])
-    grad_pad = jnp.concatenate([grad_out, zero_row], axis=0)
-    grad_rows = (
-        gate_pad[owner_table][:, None] * grad_pad[owner_table // choice_count].astype(jnp.float32)
-    ).astype(jnp.bfloat16)
+    slot_total = expert_count * slot_count
+    chosen = position[:, :, None] == jnp.arange(slot_total, dtype=jnp.int32)[None, None, :]
+    slot_of_token = jnp.any(chosen, axis=1)
+    gate_of_slot = jnp.sum(jnp.where(chosen, live_gate[:, :, None], 0.0), axis=(0, 1))
+    pick_rows = slot_of_token.astype(jnp.bfloat16)
+    outgoing = jnp.dot(pick_rows.T, tokens, preferred_element_type=jnp.float32).astype(jnp.bfloat16)
+    picked_grad = jnp.dot(pick_rows.T, grad_out, preferred_element_type=jnp.float32)
+    grad_rows = (gate_of_slot[:, None] * picked_grad).astype(jnp.bfloat16)
+    outgoing = outgoing.reshape(expert_count, slot_count, width)
     grad_rows = grad_rows.reshape(expert_count, slot_count, width)
     both_in = lax.all_to_all(
         jnp.concatenate([outgoing, grad_rows], axis=1), "expert", split_axis=0, concat_axis=0, tiled=True
@@ -71,6 +79,10 @@
     expert_out = jnp.einsum(
         "slnf,ldf->slnd", activated, w_down, preferred_element_type=jnp.float32
     ).astype(jnp.bfloat16)
+    flat_rows = (sender_count * local_count, slot_count, width)
+    returned = lax.all_to_all(
+        expert_out.reshape(flat_rows), "expert", split_axis=0, concat_axis=0, tiled=True
+    )
     grad_act = jnp.einsum("slnd,ldf->slnf", arrived, w_down, preferred_element_type=jnp.float32)
     gate_delta = (grad_act * hidden_up * silu_slope).astype(jnp.bfloat16)
     up_delta = (grad_act * silu_value).astype(jnp.bfloat16)
@@ -78,16 +90,9 @@
         jnp.einsum("slnf,ldf->slnd", gate_delta, w_gate, preferred_element_type=jnp.float32)
         + jnp.einsum("slnf,ldf->slnd", up_delta, w_up, preferred_element_type=jnp.float32)
     ).astype(jnp.bfloat16)
-    flat_rows = (sender_count * local_count, slot_count, width)
-    both_out = lax.all_to_all(
-        jnp.concatenate([expert_out.reshape(flat_rows), row_grad.reshape(flat_rows)], axis=1),
-        "expert",
-        split_axis=0,
-        concat_axis=0,
-        tiled=True,
+    sent_back = lax.all_to_all(
+        row_grad.reshape(flat_rows), "expert", split_axis=0, concat_axis=0, tiled=True
     )
-    returned = both_out[:, :slot_count]
-    sent_back = both_out[:, slot_count:]
     gate_part = jnp.einsum("slnd,slnf->dlf", row_block, gate_delta, preferred_element_type=jnp.float32)
     up_part = jnp.einsum("slnd,slnf->dlf", row_block, up_delta, preferred_element_type=jnp.float32)
     down_part = jnp.einsum("slnd,slnf->dlf", arrived, activated, preferred_element_type=jnp.float32)
@@ -103,17 +108,23 @@
     grad_gate = jnp.transpose(triple_view[:, :, 0, :], (1, 0, 2))
     grad_up = jnp.transpose(triple_view[:, :, 1, :], (1, 0, 2))
     grad_down = jnp.transpose(triple_view[:, :, 2, :], (1, 0, 2))
-    out_pad = jnp.concatenate([returned.reshape(-1, width), zero_row], axis=0)
-    back_pad = jnp.concatenate([sent_back.reshape(-1, width), zero_row], axis=0)
+    choice_rows = jnp.transpose(chosen, (1, 0, 2)).reshape(choice_count * tok_count, slot_total)
+    choice_rows = choice_rows.astype(jnp.bfloat16)
+    got_rows = jnp.dot(
+        choice_rows, returned.reshape(slot_total, width), preferred_element_type=jnp.float32
+    ).reshape(choice_count, tok_count, width)
+    back_rows = jnp.dot(
+        choice_rows, sent_back.reshape(slot_total, width), preferred_element_type=jnp.float32
+    ).reshape(choice_count, tok_count, width)
     dy_wide = grad_out.astype(jnp.float32)
     mixed = jnp.zeros((tok_count, width), jnp.float32)
     row_sum = jnp.zeros((tok_count, width), jnp.float32)
     gate_grads = []
     for which in range(choice_count):
-        got_row = out_pad[position[:, which]].astype(jnp.float32)
+        got_row = got_rows[which]
         mixed = mixed + live_gate[:, which : which + 1] * got_row
         gate_grads.append(jnp.sum(dy_wide * got_row, axis=1))
-        row_sum = row_sum + back_pad[position[:, which]].astype(jnp.float32)
+        row_sum = row_sum + back_rows[which]
     layer_output = mixed.astype(jnp.bfloat16)
     gate_grad = jnp.stack(gate_grads, axis=1)
     cross_term = jnp.sum(gate_grad * gate_value, axis=1, keepdims=True)
@@ -123,7 +134,7 @@
         jnp.bfloat16
     )
     router_part = jnp.dot(tokens_wide.T, logit_grad, precision=highest)
-    grad_router = butterfly_sum(butterfly_sum(router_part, "expert"), "dp")
+    grad_router = all_sum(all_sum(router_part, "expert"), "dp")
     return (layer_output, grad_tokens, grad_router, grad_gate, grad_up, grad_down)
 
 

time: 321 us -> 268 us (0.83)
  local copies, waits for them, and re-layouts: 74 us -> 22 us
  waiting for transfers between devices: 93 us -> 67.9 us
  starting transfers between devices: 18.2 us -> 39.3 us
  matrix products: 21.7 us -> 31.6 us
  other arithmetic: 14.9 us -> 10.5 us
    all_to_all x1 -> x2, waiting for transfers between devices: 74.1 us -> 34 us  [the longest x1 34 us: on_device(): lax.all_to_all(expert_out.reshape(flat_rows), 'expert', split_axis=0, con...]
    gather x9 -> x0, local copies, waits for them, and re-layouts: 38.4 us -> none  [the longest x3 11.7 us: on_device(): got_row = out_pad[position[:, which]].astype(jnp.float32)]
    ppermute x8 -> x17, starting transfers between devices: 13.8 us -> 30.6 us  [group_sum(): got.append(lax.ppermute(value, axis, pairs))]
    ppermute x8 -> x17, waiting for transfers between devices: 18.8 us -> 34 us  [group_sum(): got.append(lax.ppermute(value, axis, pairs))]
    dot_general x0 -> x4, matrix products: none -> 7.65 us  [the longest x1 2.9 us: on_device(): jnp.dot(choice_rows, returned.reshape(slot_total, width), preferred_eleme...]
    concatenate x4 -> x0, local copies, waits for them, and re-layouts: 6.44 us -> none  [the longest x1 1.91 us: on_device(): token_pad = jnp.concatenate([tokens, zero_row], axis=0)]
    all_to_all x1 -> x2, starting transfers between devices: 4.46 us -> 8.76 us  [the longest x1 4.46 us: on_device(): lax.all_to_all(row_grad.reshape(flat_rows), 'expert', split_axis=0, conca...]
    slice x1 -> x0, local copies, waits for them, and re-layouts: 3.65 us -> none  [on_device(): sent_back = both_out[:, slot_count:]]
  transfers between devices with their start and end apart: 10 -> 20, of which waited for: 7 -> 5; matrix products, arithmetic and copies ran while one was open for 14% -> 8% of each run, Pallas kernels for 0% -> 0%
where the time goes in v2:
time: 268 us; the launch traced here: 267 us
  blocking collectives  81.3 us (30%)
  waiting for transfers between devices  67.9 us (25%)
  starting transfers between devices  39.3 us (15%)
  matrix products  31.6 us (12%)
  local copies, waits for them, and re-layouts  22 us (8%)
  between operations  14.4 us (5%)
  other arithmetic  10.5 us (4%)
    all_to_all x1, blocking collectives, on_device(): lax.all_to_all(jnp.concatenate([outgoing, grad_rows], axis=1), 'expert',...  81.3 us
    ppermute x17, waiting for transfers between devices, group_sum(): got.append(lax.ppermute(value, axis, pairs))  34 us
    all_to_all x1, waiting for transfers between devices, on_device(): lax.all_to_all(expert_out.reshape(flat_rows), 'expert', split_axis=0, con...  34 us
    ppermute x17, starting transfers between devices, group_sum(): got.append(lax.ppermute(value, axis, pairs))  30.6 us
    unnamed x31, local copies, waits for them, and re-layouts  19.9 us
  transfers between devices with their start and end apart: 20, of which 5 were waited for; matrix products, arithmetic and copies ran while one was open for 8% of the time, Pallas kernels for 0%

profile of v2, /device:TPU:1, one launch (start us, length us, event | category | flops | bytes accessed | tf_op | source)
XLA Modules:
  0.0 267.1 jit_solution(13781898975509733970)
XLA Ops:
  11.5 1.7 convolution_convert_fusion
  14.2 81.3 %all_to_all.15 = bf16[8,96,2048]{2,1,0:T(8,128)(2,1)S(1)} all-to-all(bf16[8,96,2048]{2,1,0:T(8,128)(2,1)S(1)} %pad_maximum_fusion), channel_id=1, replica_groups=mesh['dp'=32,'expert'=8] {'expert'}, dimensions={0} | all-to-all | bytes 6291456 | tf_op jit(solution)/shard_map/all_to_all | solution.py:65
  98.9 1.7 multiply_convert_fusion.2
  100.6 1.8 fusion.14
  102.5 1.8 fusion.13
  104.4 1.8 fusion.12
  106.2 4.5 %maximum_bitcast_fusion = bf16[2048,2304]{0,1:T(8,128)(2,1)} fusion(bf16[2048,1,768]{0,2,1:T(8,128)(2,1)S(1)} %fusion.14, bf16[2048,1,768]{0,2,1:T(8,128)(2,1)S(1)} %fusion.13, bf16[2048,1,768]{0,2,1:T(8,128)(2,1)S(1)} %fusion.12), kind=kLoop, calls=%fused_computation | loop fusion | flops 28311552 | bytes 18874368 | tf_op jit(solution)/shard_map/convert_element_type | solution.py:102
  110.7 12.8 %copy.33 = bf16[2048,2304]{1,0:T(8,128)(2,1)} copy(bf16[2048,2304]{0,1:T(8,128)(2,1)} %maximum_bitcast_fusion) | data formatting | bytes 18874368
  123.5 3.6 %fusion.17 = bf16[8,48,2048]{2,1,0:T(8,128)(2,1)} fusion(bf16[8,48,768]{2,1,0:T(8,128)(2,1)} %copy-done.12, bf16[1,2048,768]{2,1,0:T(8,128)(2,1)S(1)} %copy-done), kind=kOutput, calls=%fused_computation.22 | convolution fusion | flops 1208745984 | bytes 5308416 | tf_op jit(solution)/shard_map/slnf,ldf->slnd/dot_general | solution.py:79
  127.2 4.3 %all-to-all-start.1 = ((bf16[8,48,2048]{2,1,0:T(8,128)(2,1)}), bf16[8,48,2048]{2,1,0:T(8,128)(2,1)}, u32[]{:S(2)}, u32[]{:S(2)}) async-start(bf16[8,48,2048]{2,1,0:T(8,128)(2,1)} %fusion.17), calls=%async_computation.1 | async-start | bytes 3145728 | tf_op jit(solution)/shard_map/all_to_all | solution.py:83
  131.5 3.8 %fusion.4 = f32[8,48,2048]{2,1,0:T(8,128)S(1)} fusion(bf16[8,48,768]{2,1,0:T(8,128)(2,1)} %copy-done.11, bf16[1,2048,768]{2,1,0:T(8,128)(2,1)} %param.13), kind=kOutput, calls=%fused_computation.9 | convolution fusion | flops 1207959552 | bytes 6881280 | tf_op jit(solution)/shard_map/slnf,ldf->slnd/dot_general | solution.py:91
  135.4 2.6 add_convert_fusion
  138.0 34.0 %all-to-all-done.1 = bf16[8,48,2048]{2,1,0:T(8,128)(2,1)} async-done(((bf16[8,48,2048]{2,1,0:T(8,128)(2,1)}), bf16[8,48,2048]{2,1,0:T(8,128)(2,1)}, u32[]{:S(2)}, u32[]{:S(2)}) %all-to-all-start.1) | async-done | bytes 1572896 | tf_op jit(solution)/shard_map/all_to_all | solution.py:83
  171.9 4.5 %all-to-all-start.2 = ((bf16[8,48,2048]{2,1,0:T(8,128)(2,1)}), bf16[8,48,2048]{2,1,0:T(8,128)(2,1)}, u32[]{:S(2)}, u32[]{:S(2)}) async-start(bf16[8,48,2048]{2,1,0:T(8,128)(2,1)} %add_convert_fusion), calls=%async_computation.2 | async-start | bytes 3145728 | tf_op jit(solution)/shard_map/all_to_all | solution.py:93
  176.4 2.9 %fusion.49 = f32[384,2048]{1,0:T(8,128)S(1)} fusion(bf16[384,2048]{1,0:T(8,128)(2,1)} %bitcast.20, s32[384]{0:T(512)S(1)} %bitcast.128), kind=kOutput, calls=%fused_computation.63 | convolution fusion | flops 604127232 | bytes 4720128 | tf_op jit(solution)/shard_map/dot_general | solution.py:113
  181.1 3.1 %collective-permute-start.5 = (f32[2048,8]{0,1:T(8,128)S(1)}, f32[2048,8]{0,1:T(8,128)S(1)}, u32[]{:S(2)}, u32[]{:S(2)}) collective-permute-start(f32[2048,8]{0,1:T(8,128)S(1)} %convolution_bitcast_fusion), channel_id=1, source_target_pairs={{0,6},{1,7},{2,4},{3,5},{4,2},{5,3},{6,0},{7,1},{8,14},{9,15},{10,... | collective-permute-start | bytes 196616 | tf_op jit(solution)/shard_map/ppermute | solution.py:18
  184.8 3.9 %collective-permute-start.3 = (f32[2048,8]{0,1:T(8,128)S(1)}, f32[2048,8]{0,1:T(8,128)S(1)}, u32[]{:S(2)}, u32[]{:S(2)}) collective-permute-start(f32[2048,8]{0,1:T(8,128)S(1)} %convolution_bitcast_fusion), channel_id=1, source_target_pairs={{0,4},{1,5},{2,6},{3,7},{4,0},{5,1},{6,2},{7,3},{8,12},{9,13},{10,... | collective-permute-start | bytes 196616 | tf_op jit(solution)/shard_map/ppermute | solution.py:18
  191.3 26.9 %collective-permute-done.5 = f32[2048,8]{0,1:T(8,128)S(1)} collective-permute-done((f32[2048,8]{0,1:T(8,128)S(1)}, f32[2048,8]{0,1:T(8,128)S(1)}, u32[]{:S(2)}, u32[]{:S(2)}) %collective-permute-start.5) | collective-permute-done | bytes 65568 | tf_op jit(solution)/shard_map/ppermute | solution.py:18
  218.2 2.0 collective-permute-start.2
  221.8 4.3 %collective-permute-done.2 = f32[2048,8]{0,1:T(8,128)S(1)} collective-permute-done((f32[2048,8]{0,1:T(8,128)S(1)}, f32[2048,8]{0,1:T(8,128)S(1)}, u32[]{:S(2)}, u32[]{:S(2)}) %collective-permute-start.2) | collective-permute-done | bytes 65568 | tf_op jit(solution)/shard_map/ppermute | solution.py:18
  226.2 2.8 %collective-permute-start.12 = (f32[2048,8]{0,1:T(8,128)S(1)}, f32[2048,8]{0,1:T(8,128)S(1)}, u32[]{:S(2)}, u32[]{:S(2)}) collective-permute-start(f32[2048,8]{0,1:T(8,128)S(1)} %add_add_fusion.2), channel_id=1, source_target_pairs={{0,48},{8,56},{16,32},{24,40},{32,16},{40,24},{48,0},{56,8},{64,11... | collective-permute-start | bytes 196616 | tf_op jit(solution)/shard_map/ppermute | solution.py:18
  229.0 3.9 %collective-permute-start.13 = (f32[2048,8]{0,1:T(8,128)S(1)}, f32[2048,8]{0,1:T(8,128)S(1)}, u32[]{:S(2)}, u32[]{:S(2)}) collective-permute-start(f32[2048,8]{0,1:T(8,128)S(1)} %add_add_fusion.2), channel_id=1, source_target_pairs={{0,56},{8,48},{16,40},{24,32},{32,24},{40,16},{48,8},{56,0},{64,12... | collective-permute-start | bytes 196616 | tf_op jit(solution)/shard_map/ppermute | solution.py:18
  232.9 1.7 collective-permute-start.10
  236.2 1.7 collective-permute-start.9
  237.9 2.5 collective-permute-start.7
  240.4 2.5 fusion.48
  243.8 2.9 %collective-permute-start.15 = (f32[2048,8]{0,1:T(8,128)S(1)}, f32[2048,8]{0,1:T(8,128)S(1)}, u32[]{:S(2)}, u32[]{:S(2)}) collective-permute-start(f32[2048,8]{0,1:T(8,128)S(1)} %add_add_fusion.1), channel_id=1, source_target_pairs={{0,128},{8,136},{16,144},{24,152},{32,160},{40,168},{48,176},{56,1... | collective-permute-start | bytes 196616 | tf_op jit(solution)/shard_map/ppermute | solution.py:18
  247.5 1.9 fusion.20
  251.7 2.0 copy.34
  253.7 2.1 fusion.53
  255.8 1.8 copy.35
  257.6 1.8 copy.36
  (73 shorter events, 21.7 us)
Async XLA Ops:
  7.2 91.7 %copy-start = (bf16[1,2048,768]{2,1,0:T(8,128)(2,1)S(1)}, bf16[1,2048,768]{2,1,0:T(8,128)(2,1)}, u32[]{:S(2)}) copy-start(bf16[1,2048,768]{2,1,0:T(8,128)(2,1)} %param.14) | copy-start | bytes 9437188
  7.2 244.5 %reduce-scatter.4.cloned.1.call-start = ((), (), s32[]{:S(2)}) async-start(), calls=%async_computation.4 | async-start | bytes 9732096
  7.2 5.9 %copy-start.2 = (bf16[128,2048]{1,0:T(8,128)(2,1)S(1)}, bf16[128,2048]{1,0:T(8,128)(2,1)}, u32[]{:S(2)}) copy-start(bf16[128,2048]{1,0:T(8,128)(2,1)} %param.15) | copy-start | bytes 1572868
  14.2 81.4 %copy-start.7 = (bf16[1,2048,768]{2,1,0:T(8,128)(2,1)S(1)}, bf16[1,2048,768]{2,1,0:T(8,128)(2,1)}, u32[]{:S(2)}) copy-start(bf16[1,2048,768]{2,1,0:T(8,128)(2,1)} %param.12) | copy-start | bytes 9437188
  95.5 1.9 copy-start.6
  100.6 1.9 copy-start.12
  100.6 1.9 copy-start.11
  100.6 3.7 %copy-start.9 = (bf16[8,1,48,768]{3,2,0,1:T(8,128)(2,1)}, bf16[8,1,48,768]{3,2,0,1:T(8,128)(2,1)S(1)}, u32[]{:S(2)}) copy-start(bf16[8,1,48,768]{3,2,0,1:T(8,128)(2,1)S(1)} %get-tuple-element.12) | copy-start | bytes 1769476
  127.2 44.7 %all-to-all-start.1 = ((bf16[8,48,2048]{2,1,0:T(8,128)(2,1)}), bf16[8,48,2048]{2,1,0:T(8,128)(2,1)}, u32[]{:S(2)}, u32[]{:S(2)}) async-start(bf16[8,48,2048]{2,1,0:T(8,128)(2,1)} %fusion.17), calls=%async_computation.1 | async-start | bytes 3145728 | tf_op jit(solution)/shard_map/all_to_all | solution.py:83
  131.5 3.9 %copy-start.8 = (bf16[1,2048,768]{2,1,0:T(8,128)(2,1)S(1)}, bf16[1,2048,768]{2,1,0:T(8,128)(2,1)}, u32[]{:S(2)}) copy-start(bf16[1,2048,768]{2,1,0:T(8,128)(2,1)} %param.12) | copy-start | bytes 9437188
  131.5 3.9 %copy-start.10 = (bf16[8,1,48,768]{3,2,0,1:T(8,128)(2,1)S(1)}, bf16[8,1,48,768]{3,2,0,1:T(8,128)(2,1)}, u32[]{:S(2)}) copy-start(bf16[8,1,48,768]{3,2,0,1:T(8,128)(2,1)} %copy-done.9) | copy-start | bytes 1769476
  171.9 68.5 %all-to-all-start.2 = ((bf16[8,48,2048]{2,1,0:T(8,128)(2,1)}), bf16[8,48,2048]{2,1,0:T(8,128)(2,1)}, u32[]{:S(2)}, u32[]{:S(2)}) async-start(bf16[8,48,2048]{2,1,0:T(8,128)(2,1)} %add_convert_fusion), calls=%async_computation.2 | async-start | bytes 3145728 | tf_op jit(solution)/shard_map/all_to_all | solution.py:93
  176.4 3.0 %copy-start.3 = (bf16[128,2048]{1,0:T(8,128)(2,1)S(1)}, bf16[128,2048]{1,0:T(8,128)(2,1)}, u32[]{:S(2)}) copy-start(bf16[128,2048]{1,0:T(8,128)(2,1)} %param.15) | copy-start | bytes 1572868
  179.3 1.5 copy-start.1
  181.1 37.1 %collective-permute-start.5 = (f32[2048,8]{0,1:T(8,128)S(1)}, f32[2048,8]{0,1:T(8,128)S(1)}, u32[]{:S(2)}, u32[]{:S(2)}) collective-permute-start(f32[2048,8]{0,1:T(8,128)S(1)} %convolution_bitcast_fusion), channel_id=1, source_target_pairs={{0,6},{1,7},{2,4},{3,5},{4,2},{5,3},{6,0},{7,1},{8,14},{9,15},{10,... | collective-permute-start | bytes 196616 | tf_op jit(solution)/shard_map/ppermute | solution.py:18
  184.3 37.0 %collective-permute-start.6 = (f32[2048,8]{0,1:T(8,128)S(1)}, f32[2048,8]{0,1:T(8,128)S(1)}, u32[]{:S(2)}, u32[]{:S(2)}) collective-permute-start(f32[2048,8]{0,1:T(8,128)S(1)} %convolution_bitcast_fusion), channel_id=1, source_target_pairs={{0,7},{1,6},{2,5},{3,4},{4,3},{5,2},{6,1},{7,0},{8,15},{9,14},{10,... | collective-permute-start | bytes 196616 | tf_op jit(solution)/shard_map/ppermute | solution.py:18
  184.8 37.0 %collective-permute-start.3 = (f32[2048,8]{0,1:T(8,128)S(1)}, f32[2048,8]{0,1:T(8,128)S(1)}, u32[]{:S(2)}, u32[]{:S(2)}) collective-permute-start(f32[2048,8]{0,1:T(8,128)S(1)} %convolution_bitcast_fusion), channel_id=1, source_target_pairs={{0,4},{1,5},{2,6},{3,7},{4,0},{5,1},{6,2},{7,3},{8,12},{9,13},{10,... | collective-permute-start | bytes 196616 | tf_op jit(solution)/shard_map/ppermute | solution.py:18
  188.7 33.1 %collective-permute-start.4 = (f32[2048,8]{0,1:T(8,128)S(1)}, f32[2048,8]{0,1:T(8,128)S(1)}, u32[]{:S(2)}, u32[]{:S(2)}) collective-permute-start(f32[2048,8]{0,1:T(8,128)S(1)} %convolution_bitcast_fusion), channel_id=1, source_target_pairs={{0,5},{1,4},{2,7},{3,6},{4,1},{5,0},{6,3},{7,2},{8,13},{9,12},{10,... | collective-permute-start | bytes 196616 | tf_op jit(solution)/shard_map/ppermute | solution.py:18
  190.2 31.7 %collective-permute-start.1 = (f32[2048,8]{0,1:T(8,128)S(1)}, f32[2048,8]{0,1:T(8,128)S(1)}, u32[]{:S(2)}, u32[]{:S(2)}) collective-permute-start(f32[2048,8]{0,1:T(8,128)S(1)} %convolution_bitcast_fusion), channel_id=1, source_target_pairs={{0,2},{1,3},{2,0},{3,1},{4,6},{5,7},{6,4},{7,5},{8,10},{9,11},{10,... | collective-permute-start | bytes 196616 | tf_op jit(solution)/shard_map/ppermute | solution.py:18
  218.2 8.0 %collective-permute-start.2 = (f32[2048,8]{0,1:T(8,128)S(1)}, f32[2048,8]{0,1:T(8,128)S(1)}, u32[]{:S(2)}, u32[]{:S(2)}) collective-permute-start(f32[2048,8]{0,1:T(8,128)S(1)} %convolution_bitcast_fusion), channel_id=1, source_target_pairs={{0,3},{1,2},{2,1},{3,0},{4,7},{5,6},{6,5},{7,4},{8,11},{9,10},{10,... | collective-permute-start | bytes 196616 | tf_op jit(solution)/shard_map/ppermute | solution.py:18
  221.3 4.9 %collective-permute-start = (f32[2048,8]{0,1:T(8,128)S(1)}, f32[2048,8]{0,1:T(8,128)S(1)}, u32[]{:S(2)}, u32[]{:S(2)}) collective-permute-start(f32[2048,8]{0,1:T(8,128)S(1)} %convolution_bitcast_fusion), channel_id=1, source_target_pairs={{0,1},{1,0},{2,3},{3,2},{4,5},{5,4},{6,7},{7,6},{8,9},{9,8},{10,11... | collective-permute-start | bytes 196616 | tf_op jit(solution)/shard_map/ppermute | solution.py:18
  226.2 10.0 %collective-permute-start.12 = (f32[2048,8]{0,1:T(8,128)S(1)}, f32[2048,8]{0,1:T(8,128)S(1)}, u32[]{:S(2)}, u32[]{:S(2)}) collective-permute-start(f32[2048,8]{0,1:T(8,128)S(1)} %add_add_fusion.2), channel_id=1, source_target_pairs={{0,48},{8,56},{16,32},{24,40},{32,16},{40,24},{48,0},{56,8},{64,11... | collective-permute-start | bytes 196616 | tf_op jit(solution)/shard_map/ppermute | solution.py:18
  229.0 8.9 %collective-permute-start.13 = (f32[2048,8]{0,1:T(8,128)S(1)}, f32[2048,8]{0,1:T(8,128)S(1)}, u32[]{:S(2)}, u32[]{:S(2)}) collective-permute-start(f32[2048,8]{0,1:T(8,128)S(1)} %add_add_fusion.2), channel_id=1, source_target_pairs={{0,56},{8,48},{16,40},{24,32},{32,24},{40,16},{48,8},{56,0},{64,12... | collective-permute-start | bytes 196616 | tf_op jit(solution)/shard_map/ppermute | solution.py:18
  232.9 9.9 %collective-permute-start.10 = (f32[2048,8]{0,1:T(8,128)S(1)}, f32[2048,8]{0,1:T(8,128)S(1)}, u32[]{:S(2)}, u32[]{:S(2)}) collective-permute-start(f32[2048,8]{0,1:T(8,128)S(1)} %add_add_fusion.2), channel_id=1, source_target_pairs={{0,32},{8,40},{16,48},{24,56},{32,0},{40,8},{48,16},{56,24},{64,96... | collective-permute-start | bytes 196616 | tf_op jit(solution)/shard_map/ppermute | solution.py:18
  234.6 8.3 %collective-permute-start.11 = (f32[2048,8]{0,1:T(8,128)S(1)}, f32[2048,8]{0,1:T(8,128)S(1)}, u32[]{:S(2)}, u32[]{:S(2)}) collective-permute-start(f32[2048,8]{0,1:T(8,128)S(1)} %add_add_fusion.2), channel_id=1, source_target_pairs={{0,40},{8,32},{16,56},{24,48},{32,8},{40,0},{48,24},{56,16},{64,10... | collective-permute-start | bytes 196616 | tf_op jit(solution)/shard_map/ppermute | solution.py:18
  236.2 6.7 %collective-permute-start.8 = (f32[2048,8]{0,1:T(8,128)S(1)}, f32[2048,8]{0,1:T(8,128)S(1)}, u32[]{:S(2)}, u32[]{:S(2)}) collective-permute-start(f32[2048,8]{0,1:T(8,128)S(1)} %add_add_fusion.2), channel_id=1, source_target_pairs={{0,16},{8,24},{16,0},{24,8},{32,48},{40,56},{48,32},{56,40},{64,80... | collective-permute-start | bytes 196616 | tf_op jit(solution)/shard_map/ppermute | solution.py:18
  236.2 6.7 %collective-permute-start.9 = (f32[2048,8]{0,1:T(8,128)S(1)}, f32[2048,8]{0,1:T(8,128)}, u32[]{:S(2)}, u32[]{:S(2)}) collective-permute-start(f32[2048,8]{0,1:T(8,128)S(1)} %add_add_fusion.2), channel_id=1, source_target_pairs={{0,24},{8,16},{16,8},{24,0},{32,56},{40,48},{48,40},{56,32},{64,88... | collective-permute-start | bytes 196616 | tf_op jit(solution)/shard_map/ppermute | solution.py:18
  237.9 5.0 %collective-permute-start.7 = (f32[2048,8]{0,1:T(8,128)S(1)}, f32[2048,8]{0,1:T(8,128)}, u32[]{:S(2)}, u32[]{:S(2)}) collective-permute-start(f32[2048,8]{0,1:T(8,128)S(1)} %add_add_fusion.2), channel_id=1, source_target_pairs={{0,8},{8,0},{16,24},{24,16},{32,40},{40,32},{48,56},{56,48},{64,72... | collective-permute-start | bytes 196616 | tf_op jit(solution)/shard_map/ppermute | solution.py:18
  240.4 7.1 %copy-start.4 = (f32[2048,8]{0,1:T(8,128)S(1)}, f32[2048,8]{0,1:T(8,128)}, u32[]{:S(2)}) copy-start(f32[2048,8]{0,1:T(8,128)} %param.11) | copy-start | bytes 196612
  243.8 5.6 %collective-permute-start.15 = (f32[2048,8]{0,1:T(8,128)S(1)}, f32[2048,8]{0,1:T(8,128)S(1)}, u32[]{:S(2)}, u32[]{:S(2)}) collective-permute-start(f32[2048,8]{0,1:T(8,128)S(1)} %add_add_fusion.1), channel_id=1, source_target_pairs={{0,128},{8,136},{16,144},{24,152},{32,160},{40,168},{48,176},{56,1... | collective-permute-start | bytes 196616 | tf_op jit(solution)/shard_map/ppermute | solution.py:18
  246.7 4.3 %collective-permute-start.16 = (f32[2048,8]{0,1:T(8,128)S(1)}, f32[2048,8]{0,1:T(8,128)S(1)}, u32[]{:S(2)}, u32[]{:S(2)}) collective-permute-start(f32[2048,8]{0,1:T(8,128)S(1)} %add_add_fusion.1), channel_id=1, source_target_pairs={{0,192},{8,200},{16,208},{24,216},{32,224},{40,232},{48,240},{56,2... | collective-permute-start | bytes 196616 | tf_op jit(solution)/shard_map/ppermute | solution.py:18
  247.5 3.5 %collective-permute-start.14 = (f32[2048,8]{0,1:T(8,128)S(1)}, f32[2048,8]{0,1:T(8,128)S(1)}, u32[]{:S(2)}, u32[]{:S(2)}) collective-permute-start(f32[2048,8]{0,1:T(8,128)S(1)} %add_add_fusion.1), channel_id=1, source_target_pairs={{0,64},{8,72},{16,80},{24,88},{32,96},{40,104},{48,112},{56,120},{... | collective-permute-start | bytes 196616 | tf_op jit(solution)/shard_map/ppermute | solution.py:18
  (1 other events, 1.5 us)
Sparse Core Ops, SparseCore 0:
  123.7 99.5 reduce-scatter.3

commit v3 on v2

--- a/solution.py
+++ b/solution.py
@@ -134,7 +134,7 @@
         jnp.bfloat16
     )
     router_part = jnp.dot(tokens_wide.T, logit_grad, precision=highest)
-    grad_router = all_sum(all_sum(router_part, "expert"), "dp")
+    grad_router = all_sum(all_sum(router_part, "dp"), "expert")
     return (layer_output, grad_tokens, grad_router, grad_gate, grad_up, grad_down)
 
 

time: 268 us -> 250 us (0.933)
  waiting for transfers between devices: 67.9 us -> 56.3 us
  starting transfers between devices: 39.3 us -> 33.9 us
    ppermute x17, waiting for transfers between devices: 34 us -> 19.8 us  [group_sum(): got.append(lax.ppermute(value, axis, pairs))]
    ppermute x17, starting transfers between devices: 30.6 us -> 25.1 us  [group_sum(): got.append(lax.ppermute(value, axis, pairs))]
  transfers between devices with their start and end apart: 20 -> 20, of which waited for: 5 -> 10; matrix products, arithmetic and copies ran while one was open for 8% -> 8% of each run, Pallas kernels for 0% -> 0%
where the time goes in v3:
time: 250 us; the launch traced here: 249 us
  blocking collectives  81.3 us (33%)
  waiting for transfers between devices  56.3 us (23%)
  starting transfers between devices  33.9 us (14%)
  matrix products  31.5 us (13%)
  local copies, waits for them, and re-layouts  22 us (9%)
  between operations  14.4 us (6%)
  other arithmetic  9.66 us (4%)
    all_to_all x1, blocking collectives, on_device(): lax.all_to_all(jnp.concatenate([outgoing, grad_rows], axis=1), 'expert',...  81.3 us
    all_to_all x1, waiting for transfers between devices, on_device(): lax.all_to_all(expert_out.reshape(flat_rows), 'expert', split_axis=0, con...  34 us
    ppermute x17, starting transfers between devices, group_sum(): got.append(lax.ppermute(value, axis, pairs))  25.1 us
    unnamed x31, local copies, waits for them, and re-layouts  19.9 us
    ppermute x17, waiting for transfers between devices, group_sum(): got.append(lax.ppermute(value, axis, pairs))  19.8 us
  transfers between devices with their start and end apart: 20, of which 10 were waited for; matrix products, arithmetic and copies ran while one was open for 8% of the time, Pallas kernels for 0%

profile of v3, /device:TPU:1, one launch (start us, length us, event | category | flops | bytes accessed | tf_op | source)
XLA Modules:
  0.0 249.0 jit_solution(6360131780648026727)
XLA Ops:
  14.2 81.3 %all_to_all.15 = bf16[8,96,2048]{2,1,0:T(8,128)(2,1)S(1)} all-to-all(bf16[8,96,2048]{2,1,0:T(8,128)(2,1)S(1)} %pad_maximum_fusion), channel_id=1, replica_groups=mesh['dp'=32,'expert'=8] {'expert'}, dimensions={0} | all-to-all | bytes 6291456 | tf_op jit(solution)/shard_map/all_to_all | solution.py:65
  98.9 1.7 multiply_convert_fusion.2
  100.6 1.8 fusion.14
  102.5 1.8 fusion.13
  104.4 1.8 fusion.12
  106.2 4.5 %maximum_bitcast_fusion = bf16[2048,2304]{0,1:T(8,128)(2,1)} fusion(bf16[2048,1,768]{0,2,1:T(8,128)(2,1)S(1)} %fusion.14, bf16[2048,1,768]{0,2,1:T(8,128)(2,1)S(1)} %fusion.13, bf16[2048,1,768]{0,2,1:T(8,128)(2,1)S(1)} %fusion.12), kind=kLoop, calls=%fused_computation | loop fusion | flops 28311552 | bytes 18874368 | tf_op jit(solution)/shard_map/convert_element_type | solution.py:102
  110.7 12.8 %copy.33 = bf16[2048,2304]{1,0:T(8,128)(2,1)} copy(bf16[2048,2304]{0,1:T(8,128)(2,1)} %maximum_bitcast_fusion) | data formatting | bytes 18874368
  123.5 3.6 %fusion.17 = bf16[8,48,2048]{2,1,0:T(8,128)(2,1)} fusion(bf16[8,48,768]{2,1,0:T(8,128)(2,1)} %copy-done.12, bf16[1,2048,768]{2,1,0:T(8,128)(2,1)S(1)} %copy-done), kind=kOutput, calls=%fused_computation.22 | convolution fusion | flops 1208745984 | bytes 5308416 | tf_op jit(solution)/shard_map/slnf,ldf->slnd/dot_general | solution.py:79
  127.2 4.3 %all-to-all-start.1 = ((bf16[8,48,2048]{2,1,0:T(8,128)(2,1)}), bf16[8,48,2048]{2,1,0:T(8,128)(2,1)}, u32[]{:S(2)}, u32[]{:S(2)}) async-start(bf16[8,48,2048]{2,1,0:T(8,128)(2,1)} %fusion.17), calls=%async_computation.1 | async-start | bytes 3145728 | tf_op jit(solution)/shard_map/all_to_all | solution.py:83
  131.5 3.8 %fusion.4 = f32[8,48,2048]{2,1,0:T(8,128)S(1)} fusion(bf16[8,48,768]{2,1,0:T(8,128)(2,1)} %copy-done.11, bf16[1,2048,768]{2,1,0:T(8,128)(2,1)} %param.13), kind=kOutput, calls=%fused_computation.9 | convolution fusion | flops 1207959552 | bytes 6881280 | tf_op jit(solution)/shard_map/slnf,ldf->slnd/dot_general | solution.py:91
  135.4 2.6 %add_convert_fusion = bf16[8,48,2048]{2,1,0:T(8,128)(2,1)} fusion(f32[8,48,2048]{2,1,0:T(8,128)S(1)} %fusion.4, bf16[1,2048,768]{2,1,0:T(8,128)(2,1)S(1)} %copy-done.8, bf16[8,1,48,768]{3,2,0,1:T(8,128)(2,1)S(1)} %copy-done.10), kind=kOutput, calls=%fused_computation.17 | convolution fusion | flops 1209532416 | bytes 8454144 | tf_op jit(solution)/shard_map/slnf,ldf->slnd/dot_general | solution.py:90
  138.0 34.0 %all-to-all-done.1 = bf16[8,48,2048]{2,1,0:T(8,128)(2,1)} async-done(((bf16[8,48,2048]{2,1,0:T(8,128)(2,1)}), bf16[8,48,2048]{2,1,0:T(8,128)(2,1)}, u32[]{:S(2)}, u32[]{:S(2)}) %all-to-all-start.1) | async-done | bytes 1572896 | tf_op jit(solution)/shard_map/all_to_all | solution.py:83
  171.9 4.5 %all-to-all-start.2 = ((bf16[8,48,2048]{2,1,0:T(8,128)(2,1)}), bf16[8,48,2048]{2,1,0:T(8,128)(2,1)}, u32[]{:S(2)}, u32[]{:S(2)}) async-start(bf16[8,48,2048]{2,1,0:T(8,128)(2,1)} %add_convert_fusion), calls=%async_computation.2 | async-start | bytes 3145728 | tf_op jit(solution)/shard_map/all_to_all | solution.py:93
  176.4 2.9 %fusion.49 = f32[384,2048]{1,0:T(8,128)S(1)} fusion(bf16[384,2048]{1,0:T(8,128)(2,1)} %bitcast.20, s32[384]{0:T(512)S(1)} %bitcast.128), kind=kOutput, calls=%fused_computation.63 | convolution fusion | flops 604127232 | bytes 4720128 | tf_op jit(solution)/shard_map/dot_general | solution.py:113
  181.1 2.8 %collective-permute-start.5 = (f32[2048,8]{0,1:T(8,128)S(1)}, f32[2048,8]{0,1:T(8,128)S(1)}, u32[]{:S(2)}, u32[]{:S(2)}) collective-permute-start(f32[2048,8]{0,1:T(8,128)S(1)} %convolution_bitcast_fusion), channel_id=1, source_target_pairs={{0,48},{8,56},{16,32},{24,40},{32,16},{40,24},{48,0},{56,8},{64,11... | collective-permute-start | bytes 196616 | tf_op jit(solution)/shard_map/ppermute | solution.py:18
  184.5 1.8 collective-permute-start.3
  189.5 4.3 %collective-permute-done.6 = f32[2048,8]{0,1:T(8,128)S(1)} collective-permute-done((f32[2048,8]{0,1:T(8,128)S(1)}, f32[2048,8]{0,1:T(8,128)S(1)}, u32[]{:S(2)}, u32[]{:S(2)}) %collective-permute-start.6) | collective-permute-done | bytes 65568 | tf_op jit(solution)/shard_map/ppermute | solution.py:18
  195.0 2.6 %collective-permute-done.1 = f32[2048,8]{0,1:T(8,128)S(1)} collective-permute-done((f32[2048,8]{0,1:T(8,128)S(1)}, f32[2048,8]{0,1:T(8,128)S(1)}, u32[]{:S(2)}, u32[]{:S(2)}) %collective-permute-start.1) | collective-permute-done | bytes 65568 | tf_op jit(solution)/shard_map/ppermute | solution.py:18
  197.6 2.9 %collective-permute-done.2 = f32[2048,8]{0,1:T(8,128)S(1)} collective-permute-done((f32[2048,8]{0,1:T(8,128)S(1)}, f32[2048,8]{0,1:T(8,128)S(1)}, u32[]{:S(2)}, u32[]{:S(2)}) %collective-permute-start.2) | collective-permute-done | bytes 65568 | tf_op jit(solution)/shard_map/ppermute | solution.py:18
  200.5 2.8 %collective-permute-start.8 = (f32[2048,8]{0,1:T(8,128)S(1)}, f32[2048,8]{0,1:T(8,128)S(1)}, u32[]{:S(2)}, u32[]{:S(2)}) collective-permute-start(f32[2048,8]{0,1:T(8,128)S(1)} %add_add_fusion.2), channel_id=1, source_target_pairs={{0,128},{8,136},{16,144},{24,152},{32,160},{40,168},{48,176},{56,1... | collective-permute-start | bytes 196616 | tf_op jit(solution)/shard_map/ppermute | solution.py:18
  204.2 1.9 collective-permute-done.8
  207.7 3.9 %collective-permute-start.15 = (f32[2048,8]{0,1:T(8,128)S(1)}, f32[2048,8]{0,1:T(8,128)S(1)}, u32[]{:S(2)}, u32[]{:S(2)}) collective-permute-start(f32[2048,8]{0,1:T(8,128)S(1)} %add_add_fusion.1), channel_id=1, source_target_pairs={{0,6},{1,7},{2,4},{3,5},{4,2},{5,3},{6,0},{7,1},{8,14},{9,15},{10,... | collective-permute-start | bytes 196616 | tf_op jit(solution)/shard_map/ppermute | solution.py:18
  212.1 2.5 %all-to-all-done.2 = bf16[8,48,2048]{2,1,0:T(8,128)(2,1)} async-done(((bf16[8,48,2048]{2,1,0:T(8,128)(2,1)}), bf16[8,48,2048]{2,1,0:T(8,128)(2,1)}, u32[]{:S(2)}, u32[]{:S(2)}) %all-to-all-start.2) | async-done | bytes 1572896 | tf_op jit(solution)/shard_map/all_to_all | solution.py:93
  214.6 2.4 fusion.48
  218.7 4.2 %collective-permute-start.14 = (f32[2048,8]{0,1:T(8,128)S(1)}, f32[2048,8]{0,1:T(8,128)S(1)}, u32[]{:S(2)}, u32[]{:S(2)}) collective-permute-start(f32[2048,8]{0,1:T(8,128)S(1)} %add_add_fusion.1), channel_id=1, source_target_pairs={{0,5},{1,4},{2,7},{3,6},{4,1},{5,0},{6,3},{7,2},{8,13},{9,12},{10,... | collective-permute-start | bytes 196616 | tf_op jit(solution)/shard_map/ppermute | solution.py:18
  222.8 2.0 collective-permute-start.12
  225.5 1.8 fusion.20
  227.3 5.6 %collective-permute-done.11 = f32[2048,8]{0,1:T(8,128)S(1)} collective-permute-done((f32[2048,8]{0,1:T(8,128)S(1)}, f32[2048,8]{0,1:T(8,128)S(1)}, u32[]{:S(2)}, u32[]{:S(2)}) %collective-permute-start.11) | collective-permute-done | bytes 65568 | tf_op jit(solution)/shard_map/ppermute | solution.py:18
  233.6 2.0 copy.34
  235.6 2.1 fusion.53
  237.7 1.8 copy.35
  239.5 1.8 copy.36
  (73 shorter events, 23.8 us)
Async XLA Ops:
  7.2 91.7 %copy-start = (bf16[1,2048,768]{2,1,0:T(8,128)(2,1)S(1)}, bf16[1,2048,768]{2,1,0:T(8,128)(2,1)}, u32[]{:S(2)}) copy-start(bf16[1,2048,768]{2,1,0:T(8,128)(2,1)} %param.14) | copy-start | bytes 9437188
  7.2 226.4 %reduce-scatter.4.cloned.1.call-start = ((), (), s32[]{:S(2)}) async-start(), calls=%async_computation.4 | async-start | bytes 9732096
  7.2 5.9 %copy-start.2 = (bf16[128,2048]{1,0:T(8,128)(2,1)S(1)}, bf16[128,2048]{1,0:T(8,128)(2,1)}, u32[]{:S(2)}) copy-start(bf16[128,2048]{1,0:T(8,128)(2,1)} %param.15) | copy-start | bytes 1572868
  14.2 81.4 %copy-start.7 = (bf16[1,2048,768]{2,1,0:T(8,128)(2,1)S(1)}, bf16[1,2048,768]{2,1,0:T(8,128)(2,1)}, u32[]{:S(2)}) copy-start(bf16[1,2048,768]{2,1,0:T(8,128)(2,1)} %param.12) | copy-start | bytes 9437188
  95.5 1.9 copy-start.6
  100.6 1.9 copy-start.12
  100.6 1.9 copy-start.11
  100.6 3.7 %copy-start.9 = (bf16[8,1,48,768]{3,2,0,1:T(8,128)(2,1)}, bf16[8,1,48,768]{3,2,0,1:T(8,128)(2,1)S(1)}, u32[]{:S(2)}) copy-start(bf16[8,1,48,768]{3,2,0,1:T(8,128)(2,1)S(1)} %get-tuple-element.12) | copy-start | bytes 1769476
  127.2 44.7 %all-to-all-start.1 = ((bf16[8,48,2048]{2,1,0:T(8,128)(2,1)}), bf16[8,48,2048]{2,1,0:T(8,128)(2,1)}, u32[]{:S(2)}, u32[]{:S(2)}) async-start(bf16[8,48,2048]{2,1,0:T(8,128)(2,1)} %fusion.17), calls=%async_computation.1 | async-start | bytes 3145728 | tf_op jit(solution)/shard_map/all_to_all | solution.py:83
  131.5 3.9 %copy-start.8 = (bf16[1,2048,768]{2,1,0:T(8,128)(2,1)S(1)}, bf16[1,2048,768]{2,1,0:T(8,128)(2,1)}, u32[]{:S(2)}) copy-start(bf16[1,2048,768]{2,1,0:T(8,128)(2,1)} %param.12) | copy-start | bytes 9437188
  131.5 3.9 %copy-start.10 = (bf16[8,1,48,768]{3,2,0,1:T(8,128)(2,1)S(1)}, bf16[8,1,48,768]{3,2,0,1:T(8,128)(2,1)}, u32[]{:S(2)}) copy-start(bf16[8,1,48,768]{3,2,0,1:T(8,128)(2,1)} %copy-done.9) | copy-start | bytes 1769476
  171.9 42.7 %all-to-all-start.2 = ((bf16[8,48,2048]{2,1,0:T(8,128)(2,1)}), bf16[8,48,2048]{2,1,0:T(8,128)(2,1)}, u32[]{:S(2)}, u32[]{:S(2)}) async-start(bf16[8,48,2048]{2,1,0:T(8,128)(2,1)} %add_convert_fusion), calls=%async_computation.2 | async-start | bytes 3145728 | tf_op jit(solution)/shard_map/all_to_all | solution.py:93
  176.4 3.0 %copy-start.3 = (bf16[128,2048]{1,0:T(8,128)(2,1)S(1)}, bf16[128,2048]{1,0:T(8,128)(2,1)}, u32[]{:S(2)}) copy-start(bf16[128,2048]{1,0:T(8,128)(2,1)} %param.15) | copy-start | bytes 1572868
  179.3 1.5 copy-start.1
  181.1 6.9 %collective-permute-start.5 = (f32[2048,8]{0,1:T(8,128)S(1)}, f32[2048,8]{0,1:T(8,128)S(1)}, u32[]{:S(2)}, u32[]{:S(2)}) collective-permute-start(f32[2048,8]{0,1:T(8,128)S(1)} %convolution_bitcast_fusion), channel_id=1, source_target_pairs={{0,48},{8,56},{16,32},{24,40},{32,16},{40,24},{48,0},{56,8},{64,11... | collective-permute-start | bytes 196616 | tf_op jit(solution)/shard_map/ppermute | solution.py:18
  184.0 9.8 %collective-permute-start.6 = (f32[2048,8]{0,1:T(8,128)S(1)}, f32[2048,8]{0,1:T(8,128)S(1)}, u32[]{:S(2)}, u32[]{:S(2)}) collective-permute-start(f32[2048,8]{0,1:T(8,128)S(1)} %convolution_bitcast_fusion), channel_id=1, source_target_pairs={{0,56},{8,48},{16,40},{24,32},{32,24},{40,16},{48,8},{56,0},{64,12... | collective-permute-start | bytes 196616 | tf_op jit(solution)/shard_map/ppermute | solution.py:18
  184.5 9.7 %collective-permute-start.3 = (f32[2048,8]{0,1:T(8,128)S(1)}, f32[2048,8]{0,1:T(8,128)S(1)}, u32[]{:S(2)}, u32[]{:S(2)}) collective-permute-start(f32[2048,8]{0,1:T(8,128)S(1)} %convolution_bitcast_fusion), channel_id=1, source_target_pairs={{0,32},{8,40},{16,48},{24,56},{32,0},{40,8},{48,16},{56,24},{64,96... | collective-permute-start | bytes 196616 | tf_op jit(solution)/shard_map/ppermute | solution.py:18
  186.3 8.7 %collective-permute-start.4 = (f32[2048,8]{0,1:T(8,128)S(1)}, f32[2048,8]{0,1:T(8,128)S(1)}, u32[]{:S(2)}, u32[]{:S(2)}) collective-permute-start(f32[2048,8]{0,1:T(8,128)S(1)} %convolution_bitcast_fusion), channel_id=1, source_target_pairs={{0,40},{8,32},{16,56},{24,48},{32,8},{40,0},{48,24},{56,16},{64,10... | collective-permute-start | bytes 196616 | tf_op jit(solution)/shard_map/ppermute | solution.py:18
  187.9 9.7 %collective-permute-start.1 = (f32[2048,8]{0,1:T(8,128)S(1)}, f32[2048,8]{0,1:T(8,128)S(1)}, u32[]{:S(2)}, u32[]{:S(2)}) collective-permute-start(f32[2048,8]{0,1:T(8,128)S(1)} %convolution_bitcast_fusion), channel_id=1, source_target_pairs={{0,16},{8,24},{16,0},{24,8},{32,48},{40,56},{48,32},{56,40},{64,80... | collective-permute-start | bytes 196616 | tf_op jit(solution)/shard_map/ppermute | solution.py:18
  188.1 12.4 %collective-permute-start.2 = (f32[2048,8]{0,1:T(8,128)S(1)}, f32[2048,8]{0,1:T(8,128)S(1)}, u32[]{:S(2)}, u32[]{:S(2)}) collective-permute-start(f32[2048,8]{0,1:T(8,128)S(1)} %convolution_bitcast_fusion), channel_id=1, source_target_pairs={{0,24},{8,16},{16,8},{24,0},{32,56},{40,48},{48,40},{56,32},{64,88... | collective-permute-start | bytes 196616 | tf_op jit(solution)/shard_map/ppermute | solution.py:18
  193.8 6.7 %collective-permute-start = (f32[2048,8]{0,1:T(8,128)S(1)}, f32[2048,8]{0,1:T(8,128)S(1)}, u32[]{:S(2)}, u32[]{:S(2)}) collective-permute-start(f32[2048,8]{0,1:T(8,128)S(1)} %convolution_bitcast_fusion), channel_id=1, source_target_pairs={{0,8},{8,0},{16,24},{24,16},{32,40},{40,32},{48,56},{56,48},{64,72... | collective-permute-start | bytes 196616 | tf_op jit(solution)/shard_map/ppermute | solution.py:18
  200.5 25.0 %copy-start.4 = (f32[2048,8]{0,1:T(8,128)S(1)}, f32[2048,8]{0,1:T(8,128)}, u32[]{:S(2)}) copy-start(f32[2048,8]{0,1:T(8,128)} %param.11) | copy-start | bytes 196612
  200.5 5.6 %collective-permute-start.8 = (f32[2048,8]{0,1:T(8,128)S(1)}, f32[2048,8]{0,1:T(8,128)S(1)}, u32[]{:S(2)}, u32[]{:S(2)}) collective-permute-start(f32[2048,8]{0,1:T(8,128)S(1)} %add_add_fusion.2), channel_id=1, source_target_pairs={{0,128},{8,136},{16,144},{24,152},{32,160},{40,168},{48,176},{56,1... | collective-permute-start | bytes 196616 | tf_op jit(solution)/shard_map/ppermute | solution.py:18
  203.3 4.3 %collective-permute-start.9 = (f32[2048,8]{0,1:T(8,128)S(1)}, f32[2048,8]{0,1:T(8,128)S(1)}, u32[]{:S(2)}, u32[]{:S(2)}) collective-permute-start(f32[2048,8]{0,1:T(8,128)S(1)} %add_add_fusion.2), channel_id=1, source_target_pairs={{0,192},{8,200},{16,208},{24,216},{32,224},{40,232},{48,240},{56,2... | collective-permute-start | bytes 196616 | tf_op jit(solution)/shard_map/ppermute | solution.py:18
  204.2 3.5 %collective-permute-start.7 = (f32[2048,8]{0,1:T(8,128)S(1)}, f32[2048,8]{0,1:T(8,128)S(1)}, u32[]{:S(2)}, u32[]{:S(2)}) collective-permute-start(f32[2048,8]{0,1:T(8,128)S(1)} %add_add_fusion.2), channel_id=1, source_target_pairs={{0,64},{8,72},{16,80},{24,88},{32,96},{40,104},{48,112},{56,120},{... | collective-permute-start | bytes 196616 | tf_op jit(solution)/shard_map/ppermute | solution.py:18
  207.7 15.2 %collective-permute-start.15 = (f32[2048,8]{0,1:T(8,128)S(1)}, f32[2048,8]{0,1:T(8,128)S(1)}, u32[]{:S(2)}, u32[]{:S(2)}) collective-permute-start(f32[2048,8]{0,1:T(8,128)S(1)} %add_add_fusion.1), channel_id=1, source_target_pairs={{0,6},{1,7},{2,4},{3,5},{4,2},{5,3},{6,0},{7,1},{8,14},{9,15},{10,... | collective-permute-start | bytes 196616 | tf_op jit(solution)/shard_map/ppermute | solution.py:18
  211.6 13.3 %collective-permute-start.16 = (f32[2048,8]{0,1:T(8,128)S(1)}, f32[2048,8]{0,1:T(8,128)S(1)}, u32[]{:S(2)}, u32[]{:S(2)}) collective-permute-start(f32[2048,8]{0,1:T(8,128)S(1)} %add_add_fusion.1), channel_id=1, source_target_pairs={{0,7},{1,6},{2,5},{3,4},{4,3},{5,2},{6,1},{7,0},{8,15},{9,14},{10,... | collective-permute-start | bytes 196616 | tf_op jit(solution)/shard_map/ppermute | solution.py:18
  217.1 10.3 %collective-permute-start.13 = (f32[2048,8]{0,1:T(8,128)S(1)}, f32[2048,8]{0,1:T(8,128)S(1)}, u32[]{:S(2)}, u32[]{:S(2)}) collective-permute-start(f32[2048,8]{0,1:T(8,128)S(1)} %add_add_fusion.1), channel_id=1, source_target_pairs={{0,4},{1,5},{2,6},{3,7},{4,0},{5,1},{6,2},{7,3},{8,12},{9,13},{10,... | collective-permute-start | bytes 196616 | tf_op jit(solution)/shard_map/ppermute | solution.py:18
  218.7 8.7 %collective-permute-start.14 = (f32[2048,8]{0,1:T(8,128)S(1)}, f32[2048,8]{0,1:T(8,128)S(1)}, u32[]{:S(2)}, u32[]{:S(2)}) collective-permute-start(f32[2048,8]{0,1:T(8,128)S(1)} %add_add_fusion.1), channel_id=1, source_target_pairs={{0,5},{1,4},{2,7},{3,6},{4,1},{5,0},{6,3},{7,2},{8,13},{9,12},{10,... | collective-permute-start | bytes 196616 | tf_op jit(solution)/shard_map/ppermute | solution.py:18
  222.8 10.1 %collective-permute-start.11 = (f32[2048,8]{0,1:T(8,128)S(1)}, f32[2048,8]{0,1:T(8,128)S(1)}, u32[]{:S(2)}, u32[]{:S(2)}) collective-permute-start(f32[2048,8]{0,1:T(8,128)S(1)} %add_add_fusion.1), channel_id=1, source_target_pairs={{0,2},{1,3},{2,0},{3,1},{4,6},{5,7},{6,4},{7,5},{8,10},{9,11},{10,... | collective-permute-start | bytes 196616 | tf_op jit(solution)/shard_map/ppermute | solution.py:18
  222.8 10.1 %collective-permute-start.12 = (f32[2048,8]{0,1:T(8,128)S(1)}, f32[2048,8]{0,1:T(8,128)S(1)}, u32[]{:S(2)}, u32[]{:S(2)}) collective-permute-start(f32[2048,8]{0,1:T(8,128)S(1)} %add_add_fusion.1), channel_id=1, source_target_pairs={{0,3},{1,2},{2,1},{3,0},{4,7},{5,6},{6,5},{7,4},{8,11},{9,10},{10,... | collective-permute-start | bytes 196616 | tf_op jit(solution)/shard_map/ppermute | solution.py:18
  224.9 8.0 %collective-permute-start.10 = (f32[2048,8]{0,1:T(8,128)S(1)}, f32[2048,8]{0,1:T(8,128)S(1)}, u32[]{:S(2)}, u32[]{:S(2)}) collective-permute-start(f32[2048,8]{0,1:T(8,128)S(1)} %add_add_fusion.1), channel_id=1, source_target_pairs={{0,1},{1,0},{2,3},{3,2},{4,5},{5,4},{6,7},{7,6},{8,9},{9,8},{10,11... | collective-permute-start | bytes 196616 | tf_op jit(solution)/shard_map/ppermute | solution.py:18
  (1 other events, 1.5 us)
Sparse Core Ops, SparseCore 0:
  123.7 105.1 reduce-scatter.3

commit v4 on v3

--- a/solution.py
+++ b/solution.py
@@ -2,6 +2,7 @@
 import jax.numpy as jnp
 from jax import lax
 from jax.sharding import PartitionSpec as P
+from jax.experimental import pallas as pl
 
 
 def silu_parts(hidden):
@@ -29,6 +30,34 @@
         value = group_sum(value, axis, low_bit, bits)
         low_bit += bits
     return value
+
+
+def weight_grad_kernel(rows_t_ref, grads_t_ref, deltas_ref, act_ref, out_ref):
+    split = deltas_ref.shape[1]
+    both = jnp.dot(rows_t_ref[...], deltas_ref[...], preferred_element_type=jnp.float32)
+    down = jnp.dot(grads_t_ref[...], act_ref[...], preferred_element_type=jnp.float32)
+    out_ref[:, :split] = both.astype(out_ref.dtype)
+    out_ref[:, split:] = down.astype(out_ref.dtype)
+
+
+def weight_grads(rows, grads, gate_delta, up_delta, activated):
+    width = rows.shape[1]
+    count = rows.shape[0]
+    hidden = activated.shape[1]
+    deltas = jnp.concatenate([gate_delta, up_delta], axis=1)
+    tile = 256
+    return pl.pallas_call(
+        weight_grad_kernel,
+        grid=(width // tile,),
+        in_specs=[
+            pl.BlockSpec((tile, count), lambda i: (i, 0)),
+            pl.BlockSpec((tile, count), lambda i: (i, 0)),
+            pl.BlockSpec((count, 2 * hidden), lambda i: (0, 0)),
+            pl.BlockSpec((count, hidden), lambda i: (0, 0)),
+        ],
+        out_specs=pl.BlockSpec((tile, 3 * hidden), lambda i: (i, 0)),
+        out_shape=jax.ShapeDtypeStruct((width, 3 * hidden), jnp.bfloat16),
+    )(rows.T, grads.T, deltas, activated)
 
 
 def on_device(tokens, expert_ids, slot_index, w_router, w_gate, w_up, w_down, grad_out):
@@ -93,17 +122,25 @@
     sent_back = lax.all_to_all(
         row_grad.reshape(flat_rows), "expert", split_axis=0, concat_axis=0, tiled=True
     )
-    gate_part = jnp.einsum("slnd,slnf->dlf", row_block, gate_delta, preferred_element_type=jnp.float32)
-    up_part = jnp.einsum("slnd,slnf->dlf", row_block, up_delta, preferred_element_type=jnp.float32)
-    down_part = jnp.einsum("slnd,slnf->dlf", arrived, activated, preferred_element_type=jnp.float32)
-    joined = lax.psum_scatter(
-        jnp.concatenate([gate_part, up_part, down_part], axis=2)
-        .reshape(lax.axis_size("dp") * own_rows, local_count * 3 * hidden_width)
-        .astype(jnp.bfloat16),
-        "dp",
-        scatter_dimension=0,
-        tiled=True,
-    ).astype(jnp.float32)
+    if local_count == 1:
+        flat = (sender_count * slot_count, -1)
+        partials = weight_grads(
+            row_block.reshape(flat),
+            arrived.reshape(flat),
+            gate_delta.reshape(flat),
+            up_delta.reshape(flat),
+            activated.reshape(flat),
+        )
+    else:
+        gate_part = jnp.einsum("slnd,slnf->dlf", row_block, gate_delta, preferred_element_type=jnp.float32)
+        up_part = jnp.einsum("slnd,slnf->dlf", row_block, up_delta, preferred_element_type=jnp.float32)
+        down_part = jnp.einsum("slnd,slnf->dlf", arrived, activated, preferred_element_type=jnp.float32)
+        partials = (
+            jnp.concatenate([gate_part, up_part, down_part], axis=2)
+            .reshape(lax.axis_size("dp") * own_rows, local_count * 3 * hidden_width)
+            .astype(jnp.bfloat16)
+        )
+    joined = lax.psum_scatter(partials, "dp", scatter_dimension=0, tiled=True).astype(jnp.float32)
     triple_view = joined.reshape(-1, local_count, 3, hidden_width)
     grad_gate = jnp.transpose(triple_view[:, :, 0, :], (1, 0, 2))
     grad_up = jnp.transpose(triple_view[:, :, 1, :], (1, 0, 2))

time: 250 us -> 250 us (level)
  Pallas kernels: 0 us -> 11.1 us
  local copies, waits for them, and re-layouts: 22 us -> 15.5 us
  other arithmetic: 9.66 us -> 6.32 us
    unnamed x31 -> x27, local copies, waits for them, and re-layouts: 19.9 us -> 3.63 us
    pallas_call x0 -> x1, Pallas kernels: none -> 11.1 us  [weight_grads(): pl.pallas_call(weight_grad_kernel, grid=(width // tile,), in_specs=[pl.Bl...]
    another operation x0 -> x3, local copies, waits for them, and re-layouts: none -> 7.43 us  [the longest x1 2.59 us: on_device(): arrived.reshape(flat)]
    dot_general x3 -> x0, matrix products: 5.52 us -> none  [the longest x1 1.85 us: on_device(): jnp.einsum('slnd,slnf->dlf', arrived, activated, preferred_element_type=j...]
    convert_element_type x1 -> x0, other arithmetic: 4.49 us -> none  [on_device(): joined = lax.psum_scatter(jnp.concatenate([gate_part, up_part, down_part]...]
  transfers between devices with their start and end apart: 20 -> 20, of which waited for: 10 -> 9; matrix products, arithmetic and copies ran while one was open for 8% -> 8% of each run, Pallas kernels for 0% -> 0%
where the time goes in v4:
time: 250 us
  blocking collectives  81.1 us (32%)
  waiting for transfers between devices  56.9 us (23%)
  starting transfers between devices  34.6 us (14%)
  matrix products  30 us (12%)
  local copies, waits for them, and re-layouts  15.5 us (6%)
  between operations  14.3 us (6%)
  Pallas kernels  11.1 us (4%)
  other arithmetic  6.32 us (3%)
    all_to_all x1, blocking collectives, on_device(): lax.all_to_all(jnp.concatenate([outgoing, grad_rows], axis=1), 'expert',...  81.1 us
    all_to_all x1, waiting for transfers between devices, on_device(): lax.all_to_all(expert_out.reshape(flat_rows), 'expert', split_axis=0, con...  34.3 us
    ppermute x17, starting transfers between devices, group_sum(): got.append(lax.ppermute(value, axis, pairs))  25.8 us
    ppermute x17, waiting for transfers between devices, group_sum(): got.append(lax.ppermute(value, axis, pairs))  20.2 us
    pallas_call x1, Pallas kernels, weight_grads(): pl.pallas_call(weight_grad_kernel, grid=(width // tile,), in_specs=[pl.Bl...  11.1 us
  transfers between devices with their start and end apart: 20, of which 9 were waited for; matrix products, arithmetic and copies ran while one was open for 8% of the time, Pallas kernels for 0%

profile of v4, /device:TPU:1, one launch (start us, length us, event | category | flops | bytes accessed | tf_op | source)
XLA Modules:
  0.0 249.7 jit_solution(4982239339228410016)
XLA Ops:
  8.1 1.7 fusion.30
  11.5 1.7 convolution_convert_fusion
  14.3 81.1 %all_to_all.15 = bf16[8,96,2048]{2,1,0:T(8,128)(2,1)S(1)} all-to-all(bf16[8,96,2048]{2,1,0:T(8,128)(2,1)S(1)} %pad_maximum_fusion), channel_id=1, replica_groups=mesh['dp'=32,'expert'=8] {'expert'}, dimensions={0} | all-to-all | bytes 6291456 | tf_op jit(solution)/shard_map/all_to_all | solution.py:94
  95.3 2.3 fusion.46
  97.9 2.6 %copy.35 = bf16[384,2048]{0,1:T(8,128)(2,1)} copy(bf16[384,2048]{1,0:T(8,128)(2,1)} %bitcast.104) | data formatting | bytes 3145728 | tf_op jit(solution)/shard_map/reshape;reshape | solution.py:129
  100.5 2.6 %copy.34 = bf16[384,2048]{0,1:T(8,128)(2,1)} copy(bf16[384,2048]{1,0:T(8,128)(2,1)} %bitcast.103) | data formatting | bytes 3145728 | tf_op jit(solution)/shard_map/reshape;reshape | solution.py:128
  103.1 3.9 %fusion.21 = f32[8,1,48,768]{3,2,0,1:T(8,128)S(1)} fusion(bf16[1,2048,768]{2,1,0:T(8,128)(2,1)} %param.13, bf16[8,96,2048]{2,1,0:T(8,128)(2,1)} %copy-done.1), kind=kOutput, calls=%fused_computation.24 | convolution fusion | flops 1207959552 | bytes 5898240 | tf_op jit(solution)/shard_map/slnd,ldf->slnf/dot_general | solution.py:103
  108.8 2.7 %multiply_convert_fusion.2 = (bf16[8,1,48,768]{3,2,0,1:T(8,128)(2,1)S(1)}, bf16[8,1,48,768]{3,2,0,1:T(8,128)(2,1)S(1)}, bf16[8,1,48,768]{3,2,0,1:T(8,128)(2,1)}) fusion(f32[8,1,48,768]{3,2,0,1:T(8,128)S(1)} %fusion.24, f32[8,1,48,768]{3,2,0,1:T(8,128)S(1)} %fusion.21, bf16[1,2048,768]{2,1,0:T(8,128)(2,1)S(1)} %copy-done, bf16[8,96,2048]{2,1,0:T(8,128)(2,1)S(1)} %copy-done.2), kind=kOutput, calls=%fused_computation.28 | convolution fusion | flops 1212383232 | bytes 8847360 | tf_op jit(solution)/shard_map/slnd,ldf->slnf/dot_general | solution.py:100
  113.4 11.1 %shard_map.127 = bf16[2048,2304]{1,0:T(8,128)(2,1)} custom-call(bf16[2048,384]{1,0:T(8,128)(2,1)} %bitcast.101, bf16[2048,384]{1,0:T(8,128)(2,1)} %bitcast.100, bf16[384,1536]{1,0:T(8,128)(2,1)} %pad_maximum_fusion.1.deltas_ref, bf16[384,768]{1,0:T(8,128)(2,1)} %bitcast.106), custom_call_target="tpu_custom_call" | custom-call | tf_op jit(solution)/shard_map/pallas_call | solution.py:49
  124.6 4.7 %fusion.14 = bf16[8,48,2048]{2,1,0:T(8,128)(2,1)} fusion(bf16[1,2048,768]{2,1,0:T(8,128)(2,1)} %param.14, bf16[8,1,48,768]{3,2,0,1:T(8,128)(2,1)} %get-tuple-element.28), kind=kOutput, calls=%fused_computation.15 | convolution fusion | flops 1208745984 | bytes 5308416 | tf_op jit(solution)/shard_map/slnf,ldf->slnd/dot_general | solution.py:108
  129.2 4.3 %all-to-all-start.1 = ((bf16[8,48,2048]{2,1,0:T(8,128)(2,1)}), bf16[8,48,2048]{2,1,0:T(8,128)(2,1)}, u32[]{:S(2)}, u32[]{:S(2)}) async-start(bf16[8,48,2048]{2,1,0:T(8,128)(2,1)} %fusion.14), calls=%async_computation.1 | async-start | bytes 3145728 | tf_op jit(solution)/shard_map/all_to_all | solution.py:112
  133.6 3.5 %fusion.4 = f32[8,48,2048]{2,1,0:T(8,128)S(1)} fusion(bf16[1,2048,768]{2,1,0:T(8,128)(2,1)} %param.13, bf16[8,1,48,768]{3,2,0,1:T(8,128)(2,1)} %copy-done.8), kind=kOutput, calls=%fused_computation.5 | convolution fusion | flops 1207959552 | bytes 6881280 | tf_op jit(solution)/shard_map/slnf,ldf->slnd/dot_general | solution.py:120
  137.1 2.6 %add_convert_fusion = bf16[8,48,2048]{2,1,0:T(8,128)(2,1)} fusion(f32[8,48,2048]{2,1,0:T(8,128)S(1)} %fusion.4, bf16[1,2048,768]{2,1,0:T(8,128)(2,1)S(1)} %copy-done, bf16[8,1,48,768]{3,2,0,1:T(8,128)(2,1)S(1)} %copy-done.7), kind=kOutput, calls=%fused_computation.13 | convolution fusion | flops 1209532416 | bytes 8454144 | tf_op jit(solution)/shard_map/slnf,ldf->slnd/dot_general | solution.py:119
  139.7 34.3 %all-to-all-done.1 = bf16[8,48,2048]{2,1,0:T(8,128)(2,1)} async-done(((bf16[8,48,2048]{2,1,0:T(8,128)(2,1)}), bf16[8,48,2048]{2,1,0:T(8,128)(2,1)}, u32[]{:S(2)}, u32[]{:S(2)}) %all-to-all-start.1) | async-done | bytes 1572896 | tf_op jit(solution)/shard_map/all_to_all | solution.py:112
  174.0 4.5 %all-to-all-start.2 = ((bf16[8,48,2048]{2,1,0:T(8,128)(2,1)}), bf16[8,48,2048]{2,1,0:T(8,128)(2,1)}, u32[]{:S(2)}, u32[]{:S(2)}) async-start(bf16[8,48,2048]{2,1,0:T(8,128)(2,1)} %add_convert_fusion), calls=%async_computation.2 | async-start | bytes 3145728 | tf_op jit(solution)/shard_map/all_to_all | solution.py:122
  178.5 2.6 %fusion.39 = f32[384,2048]{1,0:T(8,128)S(1)} fusion(bf16[384,2048]{1,0:T(8,128)(2,1)} %bitcast.20, s32[384]{0:T(512)S(1)} %bitcast.109), kind=kOutput, calls=%fused_computation.50 | convolution fusion | flops 604127232 | bytes 4720128 | tf_op jit(solution)/shard_map/dot_general | solution.py:150
  182.9 3.1 %collective-permute-start.6 = (f32[2048,8]{0,1:T(8,128)S(1)}, f32[2048,8]{0,1:T(8,128)S(1)}, u32[]{:S(2)}, u32[]{:S(2)}) collective-permute-start(f32[2048,8]{0,1:T(8,128)S(1)} %convolution_bitcast_fusion), channel_id=1, source_target_pairs={{0,56},{8,48},{16,40},{24,32},{32,24},{40,16},{48,8},{56,0},{64,12... | collective-permute-start | bytes 196616 | tf_op jit(solution)/shard_map/ppermute | solution.py:19
  186.3 1.7 collective-permute-start.4
  191.3 4.7 %collective-permute-done.5 = f32[2048,8]{0,1:T(8,128)S(1)} collective-permute-done((f32[2048,8]{0,1:T(8,128)S(1)}, f32[2048,8]{0,1:T(8,128)S(1)}, u32[]{:S(2)}, u32[]{:S(2)}) %collective-permute-start.5) | collective-permute-done | bytes 65568 | tf_op jit(solution)/shard_map/ppermute | solution.py:19
  196.3 3.1 %collective-permute-done.2 = f32[2048,8]{0,1:T(8,128)S(1)} collective-permute-done((f32[2048,8]{0,1:T(8,128)S(1)}, f32[2048,8]{0,1:T(8,128)S(1)}, u32[]{:S(2)}, u32[]{:S(2)}) %collective-permute-start.2) | collective-permute-done | bytes 65568 | tf_op jit(solution)/shard_map/ppermute | solution.py:19
  199.4 2.2 collective-permute-done.1
  201.7 2.9 %collective-permute-start.9 = (f32[2048,8]{0,1:T(8,128)S(1)}, f32[2048,8]{0,1:T(8,128)S(1)}, u32[]{:S(2)}, u32[]{:S(2)}) collective-permute-start(f32[2048,8]{0,1:T(8,128)S(1)} %add_add_fusion.2), channel_id=1, source_target_pairs={{0,192},{8,200},{16,208},{24,216},{32,224},{40,232},{48,240},{56,2... | collective-permute-start | bytes 196616 | tf_op jit(solution)/shard_map/ppermute | solution.py:19
  206.6 2.6 %collective-permute-done.8 = f32[2048,8]{0,1:T(8,128)S(1)} collective-permute-done((f32[2048,8]{0,1:T(8,128)S(1)}, f32[2048,8]{0,1:T(8,128)S(1)}, u32[]{:S(2)}, u32[]{:S(2)}) %collective-permute-start.8) | collective-permute-done | bytes 65568 | tf_op jit(solution)/shard_map/ppermute | solution.py:19
  209.2 3.3 %collective-permute-start.16 = (f32[2048,8]{0,1:T(8,128)S(1)}, f32[2048,8]{0,1:T(8,128)S(1)}, u32[]{:S(2)}, u32[]{:S(2)}) collective-permute-start(f32[2048,8]{0,1:T(8,128)S(1)} %add_add_fusion.1), channel_id=1, source_target_pairs={{0,7},{1,6},{2,5},{3,4},{4,3},{5,2},{6,1},{7,0},{8,15},{9,14},{10,... | collective-permute-start | bytes 196616 | tf_op jit(solution)/shard_map/ppermute | solution.py:19
  214.1 2.4 all-to-all-done.2
  216.5 2.5 fusion.38
  220.2 4.6 %collective-permute-start.13 = (f32[2048,8]{0,1:T(8,128)S(1)}, f32[2048,8]{0,1:T(8,128)S(1)}, u32[]{:S(2)}, u32[]{:S(2)}) collective-permute-start(f32[2048,8]{0,1:T(8,128)S(1)} %add_add_fusion.1), channel_id=1, source_target_pairs={{0,4},{1,5},{2,6},{3,7},{4,0},{5,1},{6,2},{7,3},{8,12},{9,13},{10,... | collective-permute-start | bytes 196616 | tf_op jit(solution)/shard_map/ppermute | solution.py:19
  225.9 2.5 collective-permute-start.10
  228.4 1.8 fusion.17
  230.2 5.5 %collective-permute-done.11 = f32[2048,8]{0,1:T(8,128)S(1)} collective-permute-done((f32[2048,8]{0,1:T(8,128)S(1)}, f32[2048,8]{0,1:T(8,128)S(1)}, u32[]{:S(2)}, u32[]{:S(2)}) %collective-permute-start.11) | collective-permute-done | bytes 65568 | tf_op jit(solution)/shard_map/ppermute | solution.py:19
  236.4 2.2 reshape.176
  238.5 2.2 slice_bitcast_fusion
  (71 shorter events, 22.2 us)
Async XLA Ops:
  7.2 101.6 %copy-start = (bf16[1,2048,768]{2,1,0:T(8,128)(2,1)S(1)}, bf16[1,2048,768]{2,1,0:T(8,128)(2,1)}, u32[]{:S(2)}) copy-start(bf16[1,2048,768]{2,1,0:T(8,128)(2,1)} %param.12) | copy-start | bytes 9437188
  7.2 229.2 %reduce-scatter.2.cloned.1.call-start = ((), (), s32[]{:S(2)}) async-start(), calls=%async_computation.4 | async-start | bytes 9732096 | tf_op jit(solution)/shard_map/reduce_scatter | solution.py:143
  7.2 6.0 %copy-start.4 = (bf16[128,2048]{1,0:T(8,128)(2,1)S(1)}, bf16[128,2048]{1,0:T(8,128)(2,1)}, u32[]{:S(2)}) copy-start(bf16[128,2048]{1,0:T(8,128)(2,1)} %param.15) | copy-start | bytes 1572868
  95.3 2.6 %copy-start.1 = (bf16[8,96,2048]{2,1,0:T(8,128)(2,1)}, bf16[8,96,2048]{2,1,0:T(8,128)(2,1)S(1)}, u32[]{:S(2)}) copy-start(bf16[8,96,2048]{2,1,0:T(8,128)(2,1)S(1)} %all_to_all.15) | copy-start | bytes 9437188
  103.1 3.9 %copy-start.2 = (bf16[8,96,2048]{2,1,0:T(8,128)(2,1)S(1)}, bf16[8,96,2048]{2,1,0:T(8,128)(2,1)}, u32[]{:S(2)}) copy-start(bf16[8,96,2048]{2,1,0:T(8,128)(2,1)} %copy-done.1) | copy-start | bytes 9437188
  103.1 4.3 %copy-start.11 = (bf16[1,2048,768]{2,1,0:T(8,128)(2,1)S(1)}, bf16[1,2048,768]{2,1,0:T(8,128)(2,1)}, u32[]{:S(2)}) copy-start(bf16[1,2048,768]{2,1,0:T(8,128)(2,1)} %param.14) | copy-start | bytes 9437188
  111.5 0.8 copy-start.6
  111.5 2.0 copy-start.8
  129.2 44.7 %all-to-all-start.1 = ((bf16[8,48,2048]{2,1,0:T(8,128)(2,1)}), bf16[8,48,2048]{2,1,0:T(8,128)(2,1)}, u32[]{:S(2)}, u32[]{:S(2)}) async-start(bf16[8,48,2048]{2,1,0:T(8,128)(2,1)} %fusion.14), calls=%async_computation.1 | async-start | bytes 3145728 | tf_op jit(solution)/shard_map/all_to_all | solution.py:112
  133.5 3.6 %copy-start.7 = (bf16[8,1,48,768]{3,2,0,1:T(8,128)(2,1)S(1)}, bf16[8,1,48,768]{3,2,0,1:T(8,128)(2,1)}, u32[]{:S(2)}) copy-start(bf16[8,1,48,768]{3,2,0,1:T(8,128)(2,1)} %copy-done.6) | copy-start | bytes 1769476
  174.0 42.5 %all-to-all-start.2 = ((bf16[8,48,2048]{2,1,0:T(8,128)(2,1)}), bf16[8,48,2048]{2,1,0:T(8,128)(2,1)}, u32[]{:S(2)}, u32[]{:S(2)}) async-start(bf16[8,48,2048]{2,1,0:T(8,128)(2,1)} %add_convert_fusion), calls=%async_computation.2 | async-start | bytes 3145728 | tf_op jit(solution)/shard_map/all_to_all | solution.py:122
  178.5 2.7 %copy-start.5 = (bf16[128,2048]{1,0:T(8,128)(2,1)S(1)}, bf16[128,2048]{1,0:T(8,128)(2,1)}, u32[]{:S(2)}) copy-start(bf16[128,2048]{1,0:T(8,128)(2,1)} %param.15) | copy-start | bytes 1572868
  181.1 1.5 copy-start.10
  181.1 1.5 copy-start.3
  182.9 7.6 %collective-permute-start.6 = (f32[2048,8]{0,1:T(8,128)S(1)}, f32[2048,8]{0,1:T(8,128)S(1)}, u32[]{:S(2)}, u32[]{:S(2)}) collective-permute-start(f32[2048,8]{0,1:T(8,128)S(1)} %convolution_bitcast_fusion), channel_id=1, source_target_pairs={{0,56},{8,48},{16,40},{24,32},{32,24},{40,16},{48,8},{56,0},{64,12... | collective-permute-start | bytes 196616 | tf_op jit(solution)/shard_map/ppermute | solution.py:19
  186.1 9.9 %collective-permute-start.5 = (f32[2048,8]{0,1:T(8,128)S(1)}, f32[2048,8]{0,1:T(8,128)S(1)}, u32[]{:S(2)}, u32[]{:S(2)}) collective-permute-start(f32[2048,8]{0,1:T(8,128)S(1)} %convolution_bitcast_fusion), channel_id=1, source_target_pairs={{0,48},{8,56},{16,32},{24,40},{32,16},{40,24},{48,0},{56,8},{64,11... | collective-permute-start | bytes 196616 | tf_op jit(solution)/shard_map/ppermute | solution.py:19
  186.3 10.0 %collective-permute-start.4 = (f32[2048,8]{0,1:T(8,128)S(1)}, f32[2048,8]{0,1:T(8,128)S(1)}, u32[]{:S(2)}, u32[]{:S(2)}) collective-permute-start(f32[2048,8]{0,1:T(8,128)S(1)} %convolution_bitcast_fusion), channel_id=1, source_target_pairs={{0,40},{8,32},{16,56},{24,48},{32,8},{40,0},{48,24},{56,16},{64,10... | collective-permute-start | bytes 196616 | tf_op jit(solution)/shard_map/ppermute | solution.py:19
  187.9 8.4 %collective-permute-start.3 = (f32[2048,8]{0,1:T(8,128)S(1)}, f32[2048,8]{0,1:T(8,128)S(1)}, u32[]{:S(2)}, u32[]{:S(2)}) collective-permute-start(f32[2048,8]{0,1:T(8,128)S(1)} %convolution_bitcast_fusion), channel_id=1, source_target_pairs={{0,32},{8,40},{16,48},{24,56},{32,0},{40,8},{48,16},{56,24},{64,96... | collective-permute-start | bytes 196616 | tf_op jit(solution)/shard_map/ppermute | solution.py:19
  189.4 10.0 %collective-permute-start.2 = (f32[2048,8]{0,1:T(8,128)S(1)}, f32[2048,8]{0,1:T(8,128)S(1)}, u32[]{:S(2)}, u32[]{:S(2)}) collective-permute-start(f32[2048,8]{0,1:T(8,128)S(1)} %convolution_bitcast_fusion), channel_id=1, source_target_pairs={{0,24},{8,16},{16,8},{24,0},{32,56},{40,48},{48,40},{56,32},{64,88... | collective-permute-start | bytes 196616 | tf_op jit(solution)/shard_map/ppermute | solution.py:19
  190.5 11.1 %collective-permute-start.1 = (f32[2048,8]{0,1:T(8,128)S(1)}, f32[2048,8]{0,1:T(8,128)S(1)}, u32[]{:S(2)}, u32[]{:S(2)}) collective-permute-start(f32[2048,8]{0,1:T(8,128)S(1)} %convolution_bitcast_fusion), channel_id=1, source_target_pairs={{0,16},{8,24},{16,0},{24,8},{32,48},{40,56},{48,32},{56,40},{64,80... | collective-permute-start | bytes 196616 | tf_op jit(solution)/shard_map/ppermute | solution.py:19
  195.9 5.7 %collective-permute-start = (f32[2048,8]{0,1:T(8,128)S(1)}, f32[2048,8]{0,1:T(8,128)S(1)}, u32[]{:S(2)}, u32[]{:S(2)}) collective-permute-start(f32[2048,8]{0,1:T(8,128)S(1)} %convolution_bitcast_fusion), channel_id=1, source_target_pairs={{0,8},{8,0},{16,24},{24,16},{32,40},{40,32},{48,56},{56,48},{64,72... | collective-permute-start | bytes 196616 | tf_op jit(solution)/shard_map/ppermute | solution.py:19
  201.7 4.9 %collective-permute-start.9 = (f32[2048,8]{0,1:T(8,128)S(1)}, f32[2048,8]{0,1:T(8,128)S(1)}, u32[]{:S(2)}, u32[]{:S(2)}) collective-permute-start(f32[2048,8]{0,1:T(8,128)S(1)} %add_add_fusion.2), channel_id=1, source_target_pairs={{0,192},{8,200},{16,208},{24,216},{32,224},{40,232},{48,240},{56,2... | collective-permute-start | bytes 196616 | tf_op jit(solution)/shard_map/ppermute | solution.py:19
  204.5 4.6 %collective-permute-start.8 = (f32[2048,8]{0,1:T(8,128)S(1)}, f32[2048,8]{0,1:T(8,128)S(1)}, u32[]{:S(2)}, u32[]{:S(2)}) collective-permute-start(f32[2048,8]{0,1:T(8,128)S(1)} %add_add_fusion.2), channel_id=1, source_target_pairs={{0,128},{8,136},{16,144},{24,152},{32,160},{40,168},{48,176},{56,1... | collective-permute-start | bytes 196616 | tf_op jit(solution)/shard_map/ppermute | solution.py:19
  205.1 4.1 %collective-permute-start.7 = (f32[2048,8]{0,1:T(8,128)S(1)}, f32[2048,8]{0,1:T(8,128)S(1)}, u32[]{:S(2)}, u32[]{:S(2)}) collective-permute-start(f32[2048,8]{0,1:T(8,128)S(1)} %add_add_fusion.2), channel_id=1, source_target_pairs={{0,64},{8,72},{16,80},{24,88},{32,96},{40,104},{48,112},{56,120},{... | collective-permute-start | bytes 196616 | tf_op jit(solution)/shard_map/ppermute | solution.py:19
  209.2 15.9 %collective-permute-start.16 = (f32[2048,8]{0,1:T(8,128)S(1)}, f32[2048,8]{0,1:T(8,128)S(1)}, u32[]{:S(2)}, u32[]{:S(2)}) collective-permute-start(f32[2048,8]{0,1:T(8,128)S(1)} %add_add_fusion.1), channel_id=1, source_target_pairs={{0,7},{1,6},{2,5},{3,4},{4,3},{5,2},{6,1},{7,0},{8,15},{9,14},{10,... | collective-permute-start | bytes 196616 | tf_op jit(solution)/shard_map/ppermute | solution.py:19
  212.5 13.4 %collective-permute-start.15 = (f32[2048,8]{0,1:T(8,128)S(1)}, f32[2048,8]{0,1:T(8,128)S(1)}, u32[]{:S(2)}, u32[]{:S(2)}) collective-permute-start(f32[2048,8]{0,1:T(8,128)S(1)} %add_add_fusion.1), channel_id=1, source_target_pairs={{0,6},{1,7},{2,4},{3,5},{4,2},{5,3},{6,0},{7,1},{8,14},{9,15},{10,... | collective-permute-start | bytes 196616 | tf_op jit(solution)/shard_map/ppermute | solution.py:19
  216.5 11.9 %copy-start.9 = (f32[2048,8]{0,1:T(8,128)S(1)}, f32[2048,8]{0,1:T(8,128)}, u32[]{:S(2)}) copy-start(f32[2048,8]{0,1:T(8,128)} %param.11) | copy-start | bytes 196612
  219.0 11.2 %collective-permute-start.14 = (f32[2048,8]{0,1:T(8,128)S(1)}, f32[2048,8]{0,1:T(8,128)S(1)}, u32[]{:S(2)}, u32[]{:S(2)}) collective-permute-start(f32[2048,8]{0,1:T(8,128)S(1)} %add_add_fusion.1), channel_id=1, source_target_pairs={{0,5},{1,4},{2,7},{3,6},{4,1},{5,0},{6,3},{7,2},{8,13},{9,12},{10,... | collective-permute-start | bytes 196616 | tf_op jit(solution)/shard_map/ppermute | solution.py:19
  220.2 10.0 %collective-permute-start.13 = (f32[2048,8]{0,1:T(8,128)S(1)}, f32[2048,8]{0,1:T(8,128)S(1)}, u32[]{:S(2)}, u32[]{:S(2)}) collective-permute-start(f32[2048,8]{0,1:T(8,128)S(1)} %add_add_fusion.1), channel_id=1, source_target_pairs={{0,4},{1,5},{2,6},{3,7},{4,0},{5,1},{6,2},{7,3},{8,12},{9,13},{10,... | collective-permute-start | bytes 196616 | tf_op jit(solution)/shard_map/ppermute | solution.py:19
  224.8 5.4 %collective-permute-start.12 = (f32[2048,8]{0,1:T(8,128)S(1)}, f32[2048,8]{0,1:T(8,128)S(1)}, u32[]{:S(2)}, u32[]{:S(2)}) collective-permute-start(f32[2048,8]{0,1:T(8,128)S(1)} %add_add_fusion.1), channel_id=1, source_target_pairs={{0,3},{1,2},{2,1},{3,0},{4,7},{5,6},{6,5},{7,4},{8,11},{9,10},{10,... | collective-permute-start | bytes 196616 | tf_op jit(solution)/shard_map/ppermute | solution.py:19
  225.1 10.6 %collective-permute-start.11 = (f32[2048,8]{0,1:T(8,128)S(1)}, f32[2048,8]{0,1:T(8,128)S(1)}, u32[]{:S(2)}, u32[]{:S(2)}) collective-permute-start(f32[2048,8]{0,1:T(8,128)S(1)} %add_add_fusion.1), channel_id=1, source_target_pairs={{0,2},{1,3},{2,0},{3,1},{4,6},{5,7},{6,4},{7,5},{8,10},{9,11},{10,... | collective-permute-start | bytes 196616 | tf_op jit(solution)/shard_map/ppermute | solution.py:19
  225.9 9.8 %collective-permute-start.10 = (f32[2048,8]{0,1:T(8,128)S(1)}, f32[2048,8]{0,1:T(8,128)S(1)}, u32[]{:S(2)}, u32[]{:S(2)}) collective-permute-start(f32[2048,8]{0,1:T(8,128)S(1)} %add_add_fusion.1), channel_id=1, source_target_pairs={{0,1},{1,0},{2,3},{3,2},{4,5},{5,4},{6,7},{7,6},{8,9},{9,8},{10,11... | collective-permute-start | bytes 196616 | tf_op jit(solution)/shard_map/ppermute | solution.py:19
Sparse Core Ops, SparseCore 0:
  124.7 104.9 reduce-scatter.1

commit v5 on v4

--- a/solution.py
+++ b/solution.py
@@ -32,10 +32,11 @@
     return value
 
 
-def weight_grad_kernel(rows_t_ref, grads_t_ref, deltas_ref, act_ref, out_ref):
+def weight_grad_kernel(rows_ref, grads_ref, deltas_ref, act_ref, out_ref):
     split = deltas_ref.shape[1]
-    both = jnp.dot(rows_t_ref[...], deltas_ref[...], preferred_element_type=jnp.float32)
-    down = jnp.dot(grads_t_ref[...], act_ref[...], preferred_element_type=jnp.float32)
+    inner = (((0,), (0,)), ((), ()))
+    both = lax.dot_general(rows_ref[...], deltas_ref[...], inner, preferred_element_type=jnp.float32)
+    down = lax.dot_general(grads_ref[...], act_ref[...], inner, preferred_element_type=jnp.float32)
     out_ref[:, :split] = both.astype(out_ref.dtype)
     out_ref[:, split:] = down.astype(out_ref.dtype)
 
@@ -45,19 +46,19 @@
     count = rows.shape[0]
     hidden = activated.shape[1]
     deltas = jnp.concatenate([gate_delta, up_delta], axis=1)
-    tile = 256
+    tile = 512
     return pl.pallas_call(
         weight_grad_kernel,
         grid=(width // tile,),
         in_specs=[
-            pl.BlockSpec((tile, count), lambda i: (i, 0)),
-            pl.BlockSpec((tile, count), lambda i: (i, 0)),
+            pl.BlockSpec((count, tile), lambda i: (0, i)),
+            pl.BlockSpec((count, tile), lambda i: (0, i)),
             pl.BlockSpec((count, 2 * hidden), lambda i: (0, 0)),
             pl.BlockSpec((count, hidden), lambda i: (0, 0)),
         ],
         out_specs=pl.BlockSpec((tile, 3 * hidden), lambda i: (i, 0)),
         out_shape=jax.ShapeDtypeStruct((width, 3 * hidden), jnp.bfloat16),
-    )(rows.T, grads.T, deltas, activated)
+    )(rows, grads, deltas, activated)
 
 
 def on_device(tokens, expert_ids, slot_index, w_router, w_gate, w_up, w_down, grad_out):

time: 250 us -> 241 us (0.964)
  local copies, waits for them, and re-layouts: 15.5 us -> 10 us
  matrix products: 30 us -> 27.5 us
    another operation x2 -> x0, local copies, waits for them, and re-layouts: 5.18 us -> none  [the longest x1 2.59 us: on_device(): arrived.reshape(flat)]
where the time goes in v5:
time: 241 us; the launch traced here: 240 us
  blocking collectives  81.3 us (34%)
  waiting for transfers between devices  56.9 us (24%)
  starting transfers between devices  34.6 us (14%)
  matrix products  27.5 us (11%)
  between operations  14.3 us (6%)
  local copies, waits for them, and re-layouts  10 us (4%)
  Pallas kernels  9.27 us (4%)
  other arithmetic  6.32 us (3%)
    all_to_all x1, blocking collectives, on_device(): lax.all_to_all(jnp.concatenate([outgoing, grad_rows], axis=1), 'expert',...  81.3 us
    all_to_all x1, waiting for transfers between devices, on_device(): lax.all_to_all(expert_out.reshape(flat_rows), 'expert', split_axis=0, con...  34.3 us
    ppermute x17, starting transfers between devices, group_sum(): got.append(lax.ppermute(value, axis, pairs))  25.8 us
    ppermute x17, waiting for transfers between devices, group_sum(): got.append(lax.ppermute(value, axis, pairs))  20.2 us
    pallas_call x1, Pallas kernels, weight_grads(): pl.pallas_call(weight_grad_kernel, grid=(width // tile,), in_specs=[pl.Bl...  9.27 us
  transfers between devices with their start and end apart: 20, of which 9 were waited for; matrix products, arithmetic and copies ran while one was open for 8% of the time, Pallas kernels for 0%

profile of v5, /device:TPU:1, one launch (start us, length us, event | category | flops | bytes accessed | tf_op | source)
XLA Modules:
  0.0 240.2 jit_solution(9905250233925395996)
XLA Ops:
  8.1 1.7 fusion.30
  11.5 1.7 convolution_convert_fusion
  14.3 81.3 %all_to_all.15 = bf16[8,96,2048]{2,1,0:T(8,128)(2,1)S(1)} all-to-all(bf16[8,96,2048]{2,1,0:T(8,128)(2,1)S(1)} %pad_maximum_fusion), channel_id=1, replica_groups=mesh['dp'=32,'expert'=8] {'expert'}, dimensions={0} | all-to-all | bytes 6291456 | tf_op jit(solution)/shard_map/all_to_all | solution.py:95
  95.6 1.4 fusion.21
  98.9 2.6 %multiply_convert_fusion.2 = (bf16[8,1,48,768]{3,2,0,1:T(8,128)(2,1)S(1)}, bf16[8,1,48,768]{3,2,0,1:T(8,128)(2,1)S(1)}, bf16[8,1,48,768]{3,2,0,1:T(8,128)(2,1)}) fusion(f32[8,1,48,768]{3,2,0,1:T(8,128)S(1)} %fusion.24, f32[8,1,48,768]{3,2,0,1:T(8,128)S(1)} %fusion.21, bf16[1,2048,768]{2,1,0:T(8,128)(2,1)S(1)} %copy-done, ...), kind=kOutput, calls=%fused_computation.28 | convolution fusion | flops 1212383232 | bytes 8847360 | tf_op jit(solution)/shard_map/slnd,ldf->slnf/dot_general | solution.py:101
  103.8 2.0 fusion.46
  105.8 9.3 %shard_map.127 = bf16[2048,2304]{1,0:T(8,128)(2,1)} custom-call(bf16[384,2048]{1,0:T(8,128)(2,1)} %bitcast.99, bf16[384,2048]{1,0:T(8,128)(2,1)} %bitcast.98, bf16[384,1536]{1,0:T(8,128)(2,1)} %pad_maximum_fusion.1.deltas_ref, bf16[384,768]{1,0:T(8,128)(2,1)} %bitcast.102), custom_call_target="tpu_custom_call" | custom-call | tf_op jit(solution)/shard_map/pallas_call | solution.py:50
  115.1 4.7 %fusion.14 = bf16[8,48,2048]{2,1,0:T(8,128)(2,1)} fusion(bf16[1,2048,768]{2,1,0:T(8,128)(2,1)} %param.14, bf16[8,1,48,768]{3,2,0,1:T(8,128)(2,1)} %get-tuple-element.28), kind=kOutput, calls=%fused_computation.15 | convolution fusion | flops 1208745984 | bytes 5308416 | tf_op jit(solution)/shard_map/slnf,ldf->slnd/dot_general | solution.py:109
  119.7 4.3 %all-to-all-start.1 = ((bf16[8,48,2048]{2,1,0:T(8,128)(2,1)}), bf16[8,48,2048]{2,1,0:T(8,128)(2,1)}, u32[]{:S(2)}, u32[]{:S(2)}) async-start(bf16[8,48,2048]{2,1,0:T(8,128)(2,1)} %fusion.14), calls=%async_computation.1 | async-start | bytes 3145728 | tf_op jit(solution)/shard_map/all_to_all | solution.py:113
  124.0 3.5 %fusion.4 = f32[8,48,2048]{2,1,0:T(8,128)S(1)} fusion(bf16[1,2048,768]{2,1,0:T(8,128)(2,1)} %param.13, bf16[8,1,48,768]{3,2,0,1:T(8,128)(2,1)} %copy-done.6), kind=kOutput, calls=%fused_computation.5 | convolution fusion | flops 1207959552 | bytes 6881280 | tf_op jit(solution)/shard_map/slnf,ldf->slnd/dot_general | solution.py:121
  127.6 2.6 %add_convert_fusion = bf16[8,48,2048]{2,1,0:T(8,128)(2,1)} fusion(f32[8,48,2048]{2,1,0:T(8,128)S(1)} %fusion.4, bf16[1,2048,768]{2,1,0:T(8,128)(2,1)S(1)} %copy-done, bf16[8,1,48,768]{3,2,0,1:T(8,128)(2,1)S(1)} %copy-done.5), kind=kOutput, calls=%fused_computation.13 | convolution fusion | flops 1209532416 | bytes 8454144 | tf_op jit(solution)/shard_map/slnf,ldf->slnd/dot_general | solution.py:120
  130.2 34.3 %all-to-all-done.1 = bf16[8,48,2048]{2,1,0:T(8,128)(2,1)} async-done(((bf16[8,48,2048]{2,1,0:T(8,128)(2,1)}), bf16[8,48,2048]{2,1,0:T(8,128)(2,1)}, u32[]{:S(2)}, u32[]{:S(2)}) %all-to-all-start.1) | async-done | bytes 1572896 | tf_op jit(solution)/shard_map/all_to_all | solution.py:113
  164.5 4.5 %all-to-all-start.2 = ((bf16[8,48,2048]{2,1,0:T(8,128)(2,1)}), bf16[8,48,2048]{2,1,0:T(8,128)(2,1)}, u32[]{:S(2)}, u32[]{:S(2)}) async-start(bf16[8,48,2048]{2,1,0:T(8,128)(2,1)} %add_convert_fusion), calls=%async_computation.2 | async-start | bytes 3145728 | tf_op jit(solution)/shard_map/all_to_all | solution.py:123
  169.0 2.6 %fusion.39 = f32[384,2048]{1,0:T(8,128)S(1)} fusion(bf16[384,2048]{1,0:T(8,128)(2,1)} %bitcast.20, s32[384]{0:T(512)S(1)} %bitcast.105), kind=kOutput, calls=%fused_computation.50 | convolution fusion | flops 604127232 | bytes 4720128 | tf_op jit(solution)/shard_map/dot_general | solution.py:151
  173.4 3.1 %collective-permute-start.6 = (f32[2048,8]{0,1:T(8,128)S(1)}, f32[2048,8]{0,1:T(8,128)S(1)}, u32[]{:S(2)}, u32[]{:S(2)}) collective-permute-start(f32[2048,8]{0,1:T(8,128)S(1)} %convolution_bitcast_fusion), channel_id=1, source_target_pairs={{0,56},{8,48},{16,40},{24,32},{32,24},{40,16},{48,8},{56,0},{64,12... | collective-permute-start | bytes 196616 | tf_op jit(solution)/shard_map/ppermute | solution.py:19
  176.7 1.7 collective-permute-start.4
  178.4 1.5 collective-permute-start.3
  181.7 4.6 %collective-permute-done.5 = f32[2048,8]{0,1:T(8,128)S(1)} collective-permute-done((f32[2048,8]{0,1:T(8,128)S(1)}, f32[2048,8]{0,1:T(8,128)S(1)}, u32[]{:S(2)}, u32[]{:S(2)}) %collective-permute-start.5) | collective-permute-done | bytes 65568 | tf_op jit(solution)/shard_map/ppermute | solution.py:19
  186.8 3.1 %collective-permute-done.2 = f32[2048,8]{0,1:T(8,128)S(1)} collective-permute-done((f32[2048,8]{0,1:T(8,128)S(1)}, f32[2048,8]{0,1:T(8,128)S(1)}, u32[]{:S(2)}, u32[]{:S(2)}) %collective-permute-start.2) | collective-permute-done | bytes 65568 | tf_op jit(solution)/shard_map/ppermute | solution.py:19
  189.9 2.2 collective-permute-done.1
  192.1 2.9 %collective-permute-start.9 = (f32[2048,8]{0,1:T(8,128)S(1)}, f32[2048,8]{0,1:T(8,128)S(1)}, u32[]{:S(2)}, u32[]{:S(2)}) collective-permute-start(f32[2048,8]{0,1:T(8,128)S(1)} %add_add_fusion.2), channel_id=1, source_target_pairs={{0,192},{8,200},{16,208},{24,216},{32,224},{40,232},{48,240},{56,2... | collective-permute-start | bytes 196616 | tf_op jit(solution)/shard_map/ppermute | solution.py:19
  197.1 2.6 %collective-permute-done.8 = f32[2048,8]{0,1:T(8,128)S(1)} collective-permute-done((f32[2048,8]{0,1:T(8,128)S(1)}, f32[2048,8]{0,1:T(8,128)S(1)}, u32[]{:S(2)}, u32[]{:S(2)}) %collective-permute-start.8) | collective-permute-done | bytes 65568 | tf_op jit(solution)/shard_map/ppermute | solution.py:19
  199.7 3.3 %collective-permute-start.16 = (f32[2048,8]{0,1:T(8,128)S(1)}, f32[2048,8]{0,1:T(8,128)S(1)}, u32[]{:S(2)}, u32[]{:S(2)}) collective-permute-start(f32[2048,8]{0,1:T(8,128)S(1)} %add_add_fusion.1), channel_id=1, source_target_pairs={{0,7},{1,6},{2,5},{3,4},{4,3},{5,2},{6,1},{7,0},{8,15},{9,14},{10,... | collective-permute-start | bytes 196616 | tf_op jit(solution)/shard_map/ppermute | solution.py:19
  203.0 1.6 collective-permute-start.15
  204.5 2.4 %all-to-all-done.2 = bf16[8,48,2048]{2,1,0:T(8,128)(2,1)} async-done(((bf16[8,48,2048]{2,1,0:T(8,128)(2,1)}), bf16[8,48,2048]{2,1,0:T(8,128)(2,1)}, u32[]{:S(2)}, u32[]{:S(2)}) %all-to-all-start.2) | async-done | bytes 1572896 | tf_op jit(solution)/shard_map/all_to_all | solution.py:123
  207.0 2.5 %fusion.38 = f32[384,2048]{1,0:T(8,128)S(1)} fusion(bf16[384,2048]{1,0:T(8,128)(2,1)} %bitcast.32, s32[384]{0:T(512)S(1)} %bitcast.106), kind=kOutput, calls=%fused_computation.49 | convolution fusion | flops 604127232 | bytes 4720128 | tf_op jit(solution)/shard_map/dot_general | solution.py:154
  210.6 4.7 %collective-permute-start.13 = (f32[2048,8]{0,1:T(8,128)S(1)}, f32[2048,8]{0,1:T(8,128)S(1)}, u32[]{:S(2)}, u32[]{:S(2)}) collective-permute-start(f32[2048,8]{0,1:T(8,128)S(1)} %add_add_fusion.1), channel_id=1, source_target_pairs={{0,4},{1,5},{2,6},{3,7},{4,0},{5,1},{6,2},{7,3},{8,12},{9,13},{10,... | collective-permute-start | bytes 196616 | tf_op jit(solution)/shard_map/ppermute | solution.py:19
  216.4 2.5 %collective-permute-start.10 = (f32[2048,8]{0,1:T(8,128)S(1)}, f32[2048,8]{0,1:T(8,128)S(1)}, u32[]{:S(2)}, u32[]{:S(2)}) collective-permute-start(f32[2048,8]{0,1:T(8,128)S(1)} %add_add_fusion.1), channel_id=1, source_target_pairs={{0,1},{1,0},{2,3},{3,2},{4,5},{5,4},{6,7},{7,6},{8,9},{9,8},{10,11... | collective-permute-start | bytes 196616 | tf_op jit(solution)/shard_map/ppermute | solution.py:19
  218.9 1.8 fusion.17
  220.7 5.5 %collective-permute-done.11 = f32[2048,8]{0,1:T(8,128)S(1)} collective-permute-done((f32[2048,8]{0,1:T(8,128)S(1)}, f32[2048,8]{0,1:T(8,128)S(1)}, u32[]{:S(2)}, u32[]{:S(2)}) %collective-permute-start.11) | collective-permute-done | bytes 65568 | tf_op jit(solution)/shard_map/ppermute | solution.py:19
  226.9 2.2 reshape.176
  229.0 2.2 slice_bitcast_fusion
  (67 shorter events, 19.1 us)
Async XLA Ops:
  7.2 91.8 %copy-start = (bf16[1,2048,768]{2,1,0:T(8,128)(2,1)S(1)}, bf16[1,2048,768]{2,1,0:T(8,128)(2,1)}, u32[]{:S(2)}) copy-start(bf16[1,2048,768]{2,1,0:T(8,128)(2,1)} %param.12) | copy-start | bytes 9437188
  7.2 219.7 %reduce-scatter.2.cloned.1.call-start = ((), (), s32[]{:S(2)}) async-start(), calls=%async_computation.4 | async-start | bytes 9732096 | tf_op jit(solution)/shard_map/reduce_scatter | solution.py:144
  7.2 6.0 %copy-start.2 = (bf16[128,2048]{1,0:T(8,128)(2,1)S(1)}, bf16[128,2048]{1,0:T(8,128)(2,1)}, u32[]{:S(2)}) copy-start(bf16[128,2048]{1,0:T(8,128)(2,1)} %param.15) | copy-start | bytes 1572868
  14.3 81.4 %copy-start.10 = (bf16[1,2048,768]{2,1,0:T(8,128)(2,1)S(1)}, bf16[1,2048,768]{2,1,0:T(8,128)(2,1)}, u32[]{:S(2)}) copy-start(bf16[1,2048,768]{2,1,0:T(8,128)(2,1)} %param.13) | copy-start | bytes 9437188
  95.6 1.9 copy-start.9
  101.6 0.8 copy-start.4
  101.6 1.0 copy-start.6
  119.7 44.7 %all-to-all-start.1 = ((bf16[8,48,2048]{2,1,0:T(8,128)(2,1)}), bf16[8,48,2048]{2,1,0:T(8,128)(2,1)}, u32[]{:S(2)}, u32[]{:S(2)}) async-start(bf16[8,48,2048]{2,1,0:T(8,128)(2,1)} %fusion.14), calls=%async_computation.1 | async-start | bytes 3145728 | tf_op jit(solution)/shard_map/all_to_all | solution.py:113
  124.0 3.6 %copy-start.5 = (bf16[8,1,48,768]{3,2,0,1:T(8,128)(2,1)S(1)}, bf16[8,1,48,768]{3,2,0,1:T(8,128)(2,1)}, u32[]{:S(2)}) copy-start(bf16[8,1,48,768]{3,2,0,1:T(8,128)(2,1)} %copy-done.4) | copy-start | bytes 1769476
  164.5 42.5 %all-to-all-start.2 = ((bf16[8,48,2048]{2,1,0:T(8,128)(2,1)}), bf16[8,48,2048]{2,1,0:T(8,128)(2,1)}, u32[]{:S(2)}, u32[]{:S(2)}) async-start(bf16[8,48,2048]{2,1,0:T(8,128)(2,1)} %add_convert_fusion), calls=%async_computation.2 | async-start | bytes 3145728 | tf_op jit(solution)/shard_map/all_to_all | solution.py:123
  168.9 2.7 %copy-start.3 = (bf16[128,2048]{1,0:T(8,128)(2,1)S(1)}, bf16[128,2048]{1,0:T(8,128)(2,1)}, u32[]{:S(2)}) copy-start(bf16[128,2048]{1,0:T(8,128)(2,1)} %param.15) | copy-start | bytes 1572868
  171.6 1.5 copy-start.8
  171.6 1.5 copy-start.1
  173.4 7.6 %collective-permute-start.6 = (f32[2048,8]{0,1:T(8,128)S(1)}, f32[2048,8]{0,1:T(8,128)S(1)}, u32[]{:S(2)}, u32[]{:S(2)}) collective-permute-start(f32[2048,8]{0,1:T(8,128)S(1)} %convolution_bitcast_fusion), channel_id=1, source_target_pairs={{0,56},{8,48},{16,40},{24,32},{32,24},{40,16},{48,8},{56,0},{64,12... | collective-permute-start | bytes 196616 | tf_op jit(solution)/shard_map/ppermute | solution.py:19
  176.5 9.9 %collective-permute-start.5 = (f32[2048,8]{0,1:T(8,128)S(1)}, f32[2048,8]{0,1:T(8,128)S(1)}, u32[]{:S(2)}, u32[]{:S(2)}) collective-permute-start(f32[2048,8]{0,1:T(8,128)S(1)} %convolution_bitcast_fusion), channel_id=1, source_target_pairs={{0,48},{8,56},{16,32},{24,40},{32,16},{40,24},{48,0},{56,8},{64,11... | collective-permute-start | bytes 196616 | tf_op jit(solution)/shard_map/ppermute | solution.py:19
  176.7 10.0 %collective-permute-start.4 = (f32[2048,8]{0,1:T(8,128)S(1)}, f32[2048,8]{0,1:T(8,128)S(1)}, u32[]{:S(2)}, u32[]{:S(2)}) collective-permute-start(f32[2048,8]{0,1:T(8,128)S(1)} %convolution_bitcast_fusion), channel_id=1, source_target_pairs={{0,40},{8,32},{16,56},{24,48},{32,8},{40,0},{48,24},{56,16},{64,10... | collective-permute-start | bytes 196616 | tf_op jit(solution)/shard_map/ppermute | solution.py:19
  178.4 8.3 %collective-permute-start.3 = (f32[2048,8]{0,1:T(8,128)S(1)}, f32[2048,8]{0,1:T(8,128)S(1)}, u32[]{:S(2)}, u32[]{:S(2)}) collective-permute-start(f32[2048,8]{0,1:T(8,128)S(1)} %convolution_bitcast_fusion), channel_id=1, source_target_pairs={{0,32},{8,40},{16,48},{24,56},{32,0},{40,8},{48,16},{56,24},{64,96... | collective-permute-start | bytes 196616 | tf_op jit(solution)/shard_map/ppermute | solution.py:19
  179.9 10.0 %collective-permute-start.2 = (f32[2048,8]{0,1:T(8,128)S(1)}, f32[2048,8]{0,1:T(8,128)S(1)}, u32[]{:S(2)}, u32[]{:S(2)}) collective-permute-start(f32[2048,8]{0,1:T(8,128)S(1)} %convolution_bitcast_fusion), channel_id=1, source_target_pairs={{0,24},{8,16},{16,8},{24,0},{32,56},{40,48},{48,40},{56,32},{64,88... | collective-permute-start | bytes 196616 | tf_op jit(solution)/shard_map/ppermute | solution.py:19
  181.0 11.1 %collective-permute-start.1 = (f32[2048,8]{0,1:T(8,128)S(1)}, f32[2048,8]{0,1:T(8,128)S(1)}, u32[]{:S(2)}, u32[]{:S(2)}) collective-permute-start(f32[2048,8]{0,1:T(8,128)S(1)} %convolution_bitcast_fusion), channel_id=1, source_target_pairs={{0,16},{8,24},{16,0},{24,8},{32,48},{40,56},{48,32},{56,40},{64,80... | collective-permute-start | bytes 196616 | tf_op jit(solution)/shard_map/ppermute | solution.py:19
  186.4 5.7 %collective-permute-start = (f32[2048,8]{0,1:T(8,128)S(1)}, f32[2048,8]{0,1:T(8,128)S(1)}, u32[]{:S(2)}, u32[]{:S(2)}) collective-permute-start(f32[2048,8]{0,1:T(8,128)S(1)} %convolution_bitcast_fusion), channel_id=1, source_target_pairs={{0,8},{8,0},{16,24},{24,16},{32,40},{40,32},{48,56},{56,48},{64,72... | collective-permute-start | bytes 196616 | tf_op jit(solution)/shard_map/ppermute | solution.py:19
  192.1 4.9 %collective-permute-start.9 = (f32[2048,8]{0,1:T(8,128)S(1)}, f32[2048,8]{0,1:T(8,128)S(1)}, u32[]{:S(2)}, u32[]{:S(2)}) collective-permute-start(f32[2048,8]{0,1:T(8,128)S(1)} %add_add_fusion.2), channel_id=1, source_target_pairs={{0,192},{8,200},{16,208},{24,216},{32,224},{40,232},{48,240},{56,2... | collective-permute-start | bytes 196616 | tf_op jit(solution)/shard_map/ppermute | solution.py:19
  195.0 4.6 %collective-permute-start.8 = (f32[2048,8]{0,1:T(8,128)S(1)}, f32[2048,8]{0,1:T(8,128)S(1)}, u32[]{:S(2)}, u32[]{:S(2)}) collective-permute-start(f32[2048,8]{0,1:T(8,128)S(1)} %add_add_fusion.2), channel_id=1, source_target_pairs={{0,128},{8,136},{16,144},{24,152},{32,160},{40,168},{48,176},{56,1... | collective-permute-start | bytes 196616 | tf_op jit(solution)/shard_map/ppermute | solution.py:19
  195.6 4.1 %collective-permute-start.7 = (f32[2048,8]{0,1:T(8,128)S(1)}, f32[2048,8]{0,1:T(8,128)S(1)}, u32[]{:S(2)}, u32[]{:S(2)}) collective-permute-start(f32[2048,8]{0,1:T(8,128)S(1)} %add_add_fusion.2), channel_id=1, source_target_pairs={{0,64},{8,72},{16,80},{24,88},{32,96},{40,104},{48,112},{56,120},{... | collective-permute-start | bytes 196616 | tf_op jit(solution)/shard_map/ppermute | solution.py:19
  199.7 15.9 %collective-permute-start.16 = (f32[2048,8]{0,1:T(8,128)S(1)}, f32[2048,8]{0,1:T(8,128)S(1)}, u32[]{:S(2)}, u32[]{:S(2)}) collective-permute-start(f32[2048,8]{0,1:T(8,128)S(1)} %add_add_fusion.1), channel_id=1, source_target_pairs={{0,7},{1,6},{2,5},{3,4},{4,3},{5,2},{6,1},{7,0},{8,15},{9,14},{10,... | collective-permute-start | bytes 196616 | tf_op jit(solution)/shard_map/ppermute | solution.py:19
  203.0 13.4 %collective-permute-start.15 = (f32[2048,8]{0,1:T(8,128)S(1)}, f32[2048,8]{0,1:T(8,128)S(1)}, u32[]{:S(2)}, u32[]{:S(2)}) collective-permute-start(f32[2048,8]{0,1:T(8,128)S(1)} %add_add_fusion.1), channel_id=1, source_target_pairs={{0,6},{1,7},{2,4},{3,5},{4,2},{5,3},{6,0},{7,1},{8,14},{9,15},{10,... | collective-permute-start | bytes 196616 | tf_op jit(solution)/shard_map/ppermute | solution.py:19
  207.0 11.9 %copy-start.7 = (f32[2048,8]{0,1:T(8,128)S(1)}, f32[2048,8]{0,1:T(8,128)}, u32[]{:S(2)}) copy-start(f32[2048,8]{0,1:T(8,128)} %param.11) | copy-start | bytes 196612
  209.5 11.2 %collective-permute-start.14 = (f32[2048,8]{0,1:T(8,128)S(1)}, f32[2048,8]{0,1:T(8,128)S(1)}, u32[]{:S(2)}, u32[]{:S(2)}) collective-permute-start(f32[2048,8]{0,1:T(8,128)S(1)} %add_add_fusion.1), channel_id=1, source_target_pairs={{0,5},{1,4},{2,7},{3,6},{4,1},{5,0},{6,3},{7,2},{8,13},{9,12},{10,... | collective-permute-start | bytes 196616 | tf_op jit(solution)/shard_map/ppermute | solution.py:19
  210.6 10.1 %collective-permute-start.13 = (f32[2048,8]{0,1:T(8,128)S(1)}, f32[2048,8]{0,1:T(8,128)S(1)}, u32[]{:S(2)}, u32[]{:S(2)}) collective-permute-start(f32[2048,8]{0,1:T(8,128)S(1)} %add_add_fusion.1), channel_id=1, source_target_pairs={{0,4},{1,5},{2,6},{3,7},{4,0},{5,1},{6,2},{7,3},{8,12},{9,13},{10,... | collective-permute-start | bytes 196616 | tf_op jit(solution)/shard_map/ppermute | solution.py:19
  215.3 5.4 %collective-permute-start.12 = (f32[2048,8]{0,1:T(8,128)S(1)}, f32[2048,8]{0,1:T(8,128)S(1)}, u32[]{:S(2)}, u32[]{:S(2)}) collective-permute-start(f32[2048,8]{0,1:T(8,128)S(1)} %add_add_fusion.1), channel_id=1, source_target_pairs={{0,3},{1,2},{2,1},{3,0},{4,7},{5,6},{6,5},{7,4},{8,11},{9,10},{10,... | collective-permute-start | bytes 196616 | tf_op jit(solution)/shard_map/ppermute | solution.py:19
  215.6 10.6 %collective-permute-start.11 = (f32[2048,8]{0,1:T(8,128)S(1)}, f32[2048,8]{0,1:T(8,128)S(1)}, u32[]{:S(2)}, u32[]{:S(2)}) collective-permute-start(f32[2048,8]{0,1:T(8,128)S(1)} %add_add_fusion.1), channel_id=1, source_target_pairs={{0,2},{1,3},{2,0},{3,1},{4,6},{5,7},{6,4},{7,5},{8,10},{9,11},{10,... | collective-permute-start | bytes 196616 | tf_op jit(solution)/shard_map/ppermute | solution.py:19
  216.4 9.8 %collective-permute-start.10 = (f32[2048,8]{0,1:T(8,128)S(1)}, f32[2048,8]{0,1:T(8,128)S(1)}, u32[]{:S(2)}, u32[]{:S(2)}) collective-permute-start(f32[2048,8]{0,1:T(8,128)S(1)} %add_add_fusion.1), channel_id=1, source_target_pairs={{0,1},{1,0},{2,3},{3,2},{4,5},{5,4},{6,7},{7,6},{8,9},{9,8},{10,11... | collective-permute-start | bytes 196616 | tf_op jit(solution)/shard_map/ppermute | solution.py:19
Sparse Core Ops, SparseCore 0:
  115.2 104.9 reduce-scatter.1

commit v6 on v5

--- a/solution.py
+++ b/solution.py
@@ -32,33 +32,27 @@
     return value
 
 
-def weight_grad_kernel(rows_ref, grads_ref, deltas_ref, act_ref, out_ref):
-    split = deltas_ref.shape[1]
+def outer_kernel(rows_ref, deltas_ref, out_ref):
     inner = (((0,), (0,)), ((), ()))
-    both = lax.dot_general(rows_ref[...], deltas_ref[...], inner, preferred_element_type=jnp.float32)
-    down = lax.dot_general(grads_ref[...], act_ref[...], inner, preferred_element_type=jnp.float32)
-    out_ref[:, :split] = both.astype(out_ref.dtype)
-    out_ref[:, split:] = down.astype(out_ref.dtype)
+    out_ref[...] = lax.dot_general(
+        rows_ref[...], deltas_ref[...], inner, preferred_element_type=jnp.float32
+    ).astype(out_ref.dtype)
 
 
-def weight_grads(rows, grads, gate_delta, up_delta, activated):
-    width = rows.shape[1]
-    count = rows.shape[0]
-    hidden = activated.shape[1]
-    deltas = jnp.concatenate([gate_delta, up_delta], axis=1)
+def outer_bf16(rows, deltas):
+    count, width = rows.shape
+    cols = deltas.shape[1]
     tile = 512
     return pl.pallas_call(
-        weight_grad_kernel,
+        outer_kernel,
         grid=(width // tile,),
         in_specs=[
             pl.BlockSpec((count, tile), lambda i: (0, i)),
-            pl.BlockSpec((count, tile), lambda i: (0, i)),
-            pl.BlockSpec((count, 2 * hidden), lambda i: (0, 0)),
-            pl.BlockSpec((count, hidden), lambda i: (0, 0)),
+            pl.BlockSpec((count, cols), lambda i: (0, 0)),
         ],
-        out_specs=pl.BlockSpec((tile, 3 * hidden), lambda i: (i, 0)),
-        out_shape=jax.ShapeDtypeStruct((width, 3 * hidden), jnp.bfloat16),
-    )(rows, grads, deltas, activated)
+        out_specs=pl.BlockSpec((tile, cols), lambda i: (i, 0)),
+        out_shape=jax.ShapeDtypeStruct((width, cols), jnp.bfloat16),
+    )(rows, deltas)
 
 
 def on_device(tokens, expert_ids, slot_index, w_router, w_gate, w_up, w_down, grad_out):
@@ -125,13 +119,16 @@
     )
     if local_count == 1:
         flat = (sender_count * slot_count, -1)
-        partials = weight_grads(
-            row_block.reshape(flat),
-            arrived.reshape(flat),
-            gate_delta.reshape(flat),
-            up_delta.reshape(flat),
-            activated.reshape(flat),
-        )
+        down_sum = lax.psum_scatter(
+            outer_bf16(arrived.reshape(flat), activated.reshape(flat)), "dp", scatter_dimension=0, tiled=True
+        ).astype(jnp.float32)
+        deltas = jnp.concatenate([gate_delta.reshape(flat), up_delta.reshape(flat)], axis=1)
+        gate_up_sum = lax.psum_scatter(
+            outer_bf16(row_block.reshape(flat), deltas), "dp", scatter_dimension=0, tiled=True
+        ).astype(jnp.float32)
+        grad_gate = gate_up_sum[None, :, :hidden_width]
+        grad_up = gate_up_sum[None, :, hidden_width:]
+        grad_down = down_sum[None]
     else:
         gate_part = jnp.einsum("slnd,slnf->dlf", row_block, gate_delta, preferred_element_type=jnp.float32)
         up_part = jnp.einsum("slnd,slnf->dlf", row_block, up_delta, preferred_element_type=jnp.float32)
@@ -141,11 +138,11 @@
             .reshape(lax.axis_size("dp") * own_rows, local_count * 3 * hidden_width)
             .astype(jnp.bfloat16)
         )
-    joined = lax.psum_scatter(partials, "dp", scatter_dimension=0, tiled=True).astype(jnp.float32)
-    triple_view = joined.reshape(-1, local_count, 3, hidden_width)
-    grad_gate = jnp.transpose(triple_view[:, :, 0, :], (1, 0, 2))
-    grad_up = jnp.transpose(triple_view[:, :, 1, :], (1, 0, 2))
-    grad_down = jnp.transpose(triple_view[:, :, 2, :], (1, 0, 2))
+        joined = lax.psum_scatter(partials, "dp", scatter_dimension=0, tiled=True).astype(jnp.float32)
+        triple_view = joined.reshape(-1, local_count, 3, hidden_width)
+        grad_gate = jnp.transpose(triple_view[:, :, 0, :], (1, 0, 2))
+        grad_up = jnp.transpose(triple_view[:, :, 1, :], (1, 0, 2))
+        grad_down = jnp.transpose(triple_view[:, :, 2, :], (1, 0, 2))
     choice_rows = jnp.transpose(chosen, (1, 0, 2)).reshape(choice_count * tok_count, slot_total)
     choice_rows = choice_rows.astype(jnp.bfloat16)
     got_rows = jnp.dot(

time: 241 us -> 303 us (1.26)
  waiting for transfers between devices: 56.9 us -> 115 us
  local copies, waits for them, and re-layouts: 10 us -> 4.34 us
  other arithmetic: 6.32 us -> 10 us
  Pallas kernels: 9.27 us -> 12.3 us
    reduce_scatter x1 -> x2, waiting for transfers between devices: 0.01 us -> 62.8 us  [the longest x1 62.8 us: on_device(): lax.psum_scatter(outer_bf16(row_block.reshape(flat), deltas), 'dp', scatt...]
    ppermute x17, waiting for transfers between devices: 20.2 us -> 11.2 us  [group_sum(): got.append(lax.ppermute(value, axis, pairs))]
    all_to_all x1, waiting for transfers between devices: 2.42 us -> 6.98 us  [on_device(): lax.all_to_all(row_grad.reshape(flat_rows), 'expert', split_axis=0, conca...]
    pallas_call x1 -> x2, Pallas kernels: 9.27 us -> 12.3 us  [outer_bf16(): pl.pallas_call(outer_kernel, grid=(width // tile,), in_specs=[pl.BlockSpe...]
  transfers between devices with their start and end apart: 20 -> 21, of which waited for: 9 -> 9; matrix products, arithmetic and copies ran while one was open for 8% -> 8% of each run, Pallas kernels for 0% -> 2%
where the time goes in v6:
time: 303 us; the launch traced here: 302 us
  waiting for transfers between devices  115 us (38%)
  blocking collectives  81.1 us (27%)
  starting transfers between devices  36.6 us (12%)
  matrix products  27.9 us (9%)
  between operations  14.3 us (5%)
  Pallas kernels  12.3 us (4%)
  other arithmetic  10 us (3%)
  local copies, waits for them, and re-layouts  4.34 us (1%)
    all_to_all x1, blocking collectives, on_device(): lax.all_to_all(jnp.concatenate([outgoing, grad_rows], axis=1), 'expert',...  81.1 us
    reduce_scatter x1, waiting for transfers between devices, on_device(): lax.psum_scatter(outer_bf16(row_block.reshape(flat), deltas), 'dp', scatt...  62.8 us
    all_to_all x1, waiting for transfers between devices, on_device(): lax.all_to_all(expert_out.reshape(flat_rows), 'expert', split_axis=0, con...  34.2 us
    ppermute x17, starting transfers between devices, group_sum(): got.append(lax.ppermute(value, axis, pairs))  27.8 us
    pallas_call x2, Pallas kernels, outer_bf16(): pl.pallas_call(outer_kernel, grid=(width // tile,), in_specs=[pl.BlockSpe...  12.3 us
    ppermute x17, waiting for transfers between devices, group_sum(): got.append(lax.ppermute(value, axis, pairs))  11.2 us
    all_to_all x1, waiting for transfers between devices, on_device(): lax.all_to_all(row_grad.reshape(flat_rows), 'expert', split_axis=0, conca...  6.98 us
  transfers between devices with their start and end apart: 21, of which 9 were waited for; matrix products, arithmetic and copies ran while one was open for 8% of the time, Pallas kernels for 2%

profile of v6, /device:TPU:1, one launch (start us, length us, event | category | flops | bytes accessed | tf_op | source)
XLA Modules:
  0.0 301.8 jit_solution(15439984974579862838)
XLA Ops:
  8.1 1.7 fusion.30
  11.5 1.7 convolution_convert_fusion
  14.3 81.1 %all_to_all.15 = bf16[8,96,2048]{2,1,0:T(8,128)(2,1)S(1)} all-to-all(bf16[8,96,2048]{2,1,0:T(8,128)(2,1)S(1)} %pad_maximum_fusion), channel_id=1, replica_groups=mesh['dp'=32,'expert'=8] {'expert'}, dimensions={0} | all-to-all | bytes 6291456 | tf_op jit(solution)/shard_map/all_to_all | solution.py:89
  95.3 2.0 fusion.46
  101.7 3.0 %multiply_convert_fusion.2 = (bf16[8,1,48,768]{3,2,0,1:T(8,128)(2,1)}, bf16[8,1,48,768]{3,2,0,1:T(8,128)(2,1)}, bf16[8,1,48,768]{3,2,0,1:T(8,128)(2,1)}) fusion(f32[8,1,48,768]{3,2,0,1:T(8,128)S(1)} %fusion.24, f32[8,1,48,768]{3,2,0,1:T(8,128)S(1)} %fusion.21, bf16[1,2048,768]{2,1,0:T(8,128)(2,1)S(1)} %copy-done, bf16[8,96,2048]{2,1,0:T(8,128)(2,1)S(1)} %all_to_all.15), kind=kOutput, calls=%fused_computation.28 | convolution fusion | flops 1212383232 | bytes 8847360 | tf_op jit(solution)/shard_map/slnd,ldf->slnf/dot_general | solution.py:95
  104.7 5.3 %shard_map.128 = bf16[2048,768]{1,0:T(8,128)(2,1)} custom-call(bf16[384,2048]{1,0:T(8,128)(2,1)} %bitcast.102, bf16[384,768]{1,0:T(8,128)(2,1)} %bitcast.105), custom_call_target="tpu_custom_call" | custom-call | tf_op jit(solution)/shard_map/pallas_call | solution.py:46
  110.1 2.3 pad_maximum_fusion.1.deltas_ref
  112.4 7.0 %shard_map.127 = bf16[2048,1536]{1,0:T(8,128)(2,1)} custom-call(bf16[384,2048]{1,0:T(8,128)(2,1)} %bitcast.101, bf16[384,1536]{1,0:T(8,128)(2,1)} %pad_maximum_fusion.1.deltas_ref), custom_call_target="tpu_custom_call" | custom-call | tf_op jit(solution)/shard_map/pallas_call | solution.py:46
  119.5 4.7 %fusion.14 = bf16[8,48,2048]{2,1,0:T(8,128)(2,1)} fusion(bf16[1,2048,768]{2,1,0:T(8,128)(2,1)} %param.14, bf16[8,1,48,768]{3,2,0,1:T(8,128)(2,1)} %get-tuple-element.16), kind=kOutput, calls=%fused_computation.15 | convolution fusion | flops 1208745984 | bytes 5308416 | tf_op jit(solution)/shard_map/slnf,ldf->slnd/dot_general | solution.py:103
  124.2 4.3 %all-to-all-start.1 = ((bf16[8,48,2048]{2,1,0:T(8,128)(2,1)}), bf16[8,48,2048]{2,1,0:T(8,128)(2,1)}, u32[]{:S(2)}, u32[]{:S(2)}) async-start(bf16[8,48,2048]{2,1,0:T(8,128)(2,1)} %fusion.14), calls=%async_computation.1 | async-start | bytes 3145728 | tf_op jit(solution)/shard_map/all_to_all | solution.py:107
  128.5 3.6 %fusion.4 = f32[8,48,2048]{2,1,0:T(8,128)S(1)} fusion(bf16[1,2048,768]{2,1,0:T(8,128)(2,1)} %param.13, bf16[8,1,48,768]{3,2,0,1:T(8,128)(2,1)} %get-tuple-element.15), kind=kOutput, calls=%fused_computation.5 | convolution fusion | flops 1207959552 | bytes 6881280 | tf_op jit(solution)/shard_map/slnf,ldf->slnd/dot_general | solution.py:115
  132.2 2.6 add_convert_fusion
  134.8 34.2 %all-to-all-done.1 = bf16[8,48,2048]{2,1,0:T(8,128)(2,1)} async-done(((bf16[8,48,2048]{2,1,0:T(8,128)(2,1)}), bf16[8,48,2048]{2,1,0:T(8,128)(2,1)}, u32[]{:S(2)}, u32[]{:S(2)}) %all-to-all-start.1) | async-done | bytes 1572896 | tf_op jit(solution)/shard_map/all_to_all | solution.py:107
  168.9 4.5 %all-to-all-start.2 = ((bf16[8,48,2048]{2,1,0:T(8,128)(2,1)}), bf16[8,48,2048]{2,1,0:T(8,128)(2,1)}, u32[]{:S(2)}, u32[]{:S(2)}) async-start(bf16[8,48,2048]{2,1,0:T(8,128)(2,1)} %add_convert_fusion), calls=%async_computation.2 | async-start | bytes 3145728 | tf_op jit(solution)/shard_map/all_to_all | solution.py:117
  173.5 2.5 fusion.39
  177.8 3.2 %collective-permute-start.6 = (f32[2048,8]{0,1:T(8,128)S(1)}, f32[2048,8]{0,1:T(8,128)S(1)}, u32[]{:S(2)}, u32[]{:S(2)}) collective-permute-start(f32[2048,8]{0,1:T(8,128)S(1)} %convolution_bitcast_fusion), channel_id=1, source_target_pairs={{0,56},{8,48},{16,40},{24,32},{32,24},{40,16},{48,8},{56,0},{64,12... | collective-permute-start | bytes 196616 | tf_op jit(solution)/shard_map/ppermute | solution.py:19
  181.0 1.8 collective-permute-start.4
  186.0 2.0 collective-permute-done.5
  188.0 2.0 collective-permute-start
  192.4 2.5 collective-permute-start.9
  195.7 1.6 collective-permute-done.9
  197.3 2.4 collective-permute-done.8
  199.7 1.9 collective-permute-start.16
  201.6 2.8 collective-permute-start.15
  204.4 7.0 %all-to-all-done.2 = bf16[8,48,2048]{2,1,0:T(8,128)(2,1)} async-done(((bf16[8,48,2048]{2,1,0:T(8,128)(2,1)}), bf16[8,48,2048]{2,1,0:T(8,128)(2,1)}, u32[]{:S(2)}, u32[]{:S(2)}) %all-to-all-start.2) | async-done | bytes 1572896 | tf_op jit(solution)/shard_map/all_to_all | solution.py:117
  211.4 2.5 fusion.38
  215.1 4.8 %collective-permute-start.13 = (f32[2048,8]{0,1:T(8,128)S(1)}, f32[2048,8]{0,1:T(8,128)S(1)}, u32[]{:S(2)}, u32[]{:S(2)}) collective-permute-start(f32[2048,8]{0,1:T(8,128)S(1)} %add_add_fusion.1), channel_id=1, source_target_pairs={{0,4},{1,5},{2,6},{3,7},{4,0},{5,1},{6,2},{7,3},{8,12},{9,13},{10,... | collective-permute-start | bytes 196616 | tf_op jit(solution)/shard_map/ppermute | solution.py:19
  220.9 2.6 collective-permute-start.10
  223.4 1.8 fusion.17
  225.3 2.9 collective-permute-done.11
  228.8 1.6 bitcast_convert_fusion
  230.4 62.8 %reduce-scatter.3.cloned.1.call-done = bf16[64,1536]{1,0:T(8,128)(2,1)} async-done(((bf16[2048,1536]{1,0:T(8,128)(2,1)}), bf16[64,1536]{1,0:T(8,128)(2,1)}) %reduce-scatter.3.cloned.1.call-update) | async-done | bytes 196624 | tf_op jit(solution)/shard_map/reduce_scatter | solution.py:126
  (65 shorter events, 20.8 us)
Async XLA Ops:
  7.2 94.5 %copy-start = (bf16[1,2048,768]{2,1,0:T(8,128)(2,1)S(1)}, bf16[1,2048,768]{2,1,0:T(8,128)(2,1)}, u32[]{:S(2)}) copy-start(bf16[1,2048,768]{2,1,0:T(8,128)(2,1)} %param.12) | copy-start | bytes 9437188
  7.2 221.6 %reduce-scatter.5.cloned.1.call-start = ((), (), s32[]{:S(2)}) async-start(), calls=%async_computation.6 | async-start | bytes 3244032 | tf_op jit(solution)/shard_map/reduce_scatter | solution.py:122
  7.2 6.0 %copy-start.2 = (bf16[128,2048]{1,0:T(8,128)(2,1)S(1)}, bf16[128,2048]{1,0:T(8,128)(2,1)}, u32[]{:S(2)}) copy-start(bf16[128,2048]{1,0:T(8,128)(2,1)} %param.15) | copy-start | bytes 1572868
  95.3 3.0 %copy-start.8 = (bf16[1,2048,768]{2,1,0:T(8,128)(2,1)S(1)}, bf16[1,2048,768]{2,1,0:T(8,128)(2,1)}, u32[]{:S(2)}) copy-start(bf16[1,2048,768]{2,1,0:T(8,128)(2,1)} %param.13) | copy-start | bytes 9437188
  98.4 1.9 copy-start.7
  110.1 183.2 %reduce-scatter.3.cloned.1.call-start = ((), (), s32[]{:S(2)}) async-start(), calls=%async_computation.5 | async-start | bytes 6488064 | tf_op jit(solution)/shard_map/reduce_scatter | solution.py:126
  124.2 44.7 %all-to-all-start.1 = ((bf16[8,48,2048]{2,1,0:T(8,128)(2,1)}), bf16[8,48,2048]{2,1,0:T(8,128)(2,1)}, u32[]{:S(2)}, u32[]{:S(2)}) async-start(bf16[8,48,2048]{2,1,0:T(8,128)(2,1)} %fusion.14), calls=%async_computation.1 | async-start | bytes 3145728 | tf_op jit(solution)/shard_map/all_to_all | solution.py:107
  128.5 3.6 %copy-start.4 = (bf16[8,1,48,768]{3,2,0,1:T(8,128)(2,1)S(1)}, bf16[8,1,48,768]{3,2,0,1:T(8,128)(2,1)}, u32[]{:S(2)}) copy-start(bf16[8,1,48,768]{3,2,0,1:T(8,128)(2,1)} %get-tuple-element.14) | copy-start | bytes 1769476
  168.9 42.5 %all-to-all-start.2 = ((bf16[8,48,2048]{2,1,0:T(8,128)(2,1)}), bf16[8,48,2048]{2,1,0:T(8,128)(2,1)}, u32[]{:S(2)}, u32[]{:S(2)}) async-start(bf16[8,48,2048]{2,1,0:T(8,128)(2,1)} %add_convert_fusion), calls=%async_computation.2 | async-start | bytes 3145728 | tf_op jit(solution)/shard_map/all_to_all | solution.py:117
  173.4 2.5 copy-start.3
  176.0 1.5 copy-start.6
  176.0 1.5 copy-start.1
  177.8 6.9 %collective-permute-start.6 = (f32[2048,8]{0,1:T(8,128)S(1)}, f32[2048,8]{0,1:T(8,128)S(1)}, u32[]{:S(2)}, u32[]{:S(2)}) collective-permute-start(f32[2048,8]{0,1:T(8,128)S(1)} %convolution_bitcast_fusion), channel_id=1, source_target_pairs={{0,56},{8,48},{16,40},{24,32},{32,24},{40,16},{48,8},{56,0},{64,12... | collective-permute-start | bytes 196616 | tf_op jit(solution)/shard_map/ppermute | solution.py:19
  181.0 7.0 %collective-permute-start.5 = (f32[2048,8]{0,1:T(8,128)S(1)}, f32[2048,8]{0,1:T(8,128)S(1)}, u32[]{:S(2)}, u32[]{:S(2)}) collective-permute-start(f32[2048,8]{0,1:T(8,128)S(1)} %convolution_bitcast_fusion), channel_id=1, source_target_pairs={{0,48},{8,56},{16,32},{24,40},{32,16},{40,24},{48,0},{56,8},{64,11... | collective-permute-start | bytes 196616 | tf_op jit(solution)/shard_map/ppermute | solution.py:19
  181.0 9.1 %collective-permute-start.4 = (f32[2048,8]{0,1:T(8,128)S(1)}, f32[2048,8]{0,1:T(8,128)S(1)}, u32[]{:S(2)}, u32[]{:S(2)}) collective-permute-start(f32[2048,8]{0,1:T(8,128)S(1)} %convolution_bitcast_fusion), channel_id=1, source_target_pairs={{0,40},{8,32},{16,56},{24,48},{32,8},{40,0},{48,24},{56,16},{64,10... | collective-permute-start | bytes 196616 | tf_op jit(solution)/shard_map/ppermute | solution.py:19
  182.8 7.2 %collective-permute-start.3 = (f32[2048,8]{0,1:T(8,128)S(1)}, f32[2048,8]{0,1:T(8,128)S(1)}, u32[]{:S(2)}, u32[]{:S(2)}) collective-permute-start(f32[2048,8]{0,1:T(8,128)S(1)} %convolution_bitcast_fusion), channel_id=1, source_target_pairs={{0,32},{8,40},{16,48},{24,56},{32,0},{40,8},{48,16},{56,24},{64,96... | collective-permute-start | bytes 196616 | tf_op jit(solution)/shard_map/ppermute | solution.py:19
  184.4 6.6 %collective-permute-start.2 = (f32[2048,8]{0,1:T(8,128)S(1)}, f32[2048,8]{0,1:T(8,128)S(1)}, u32[]{:S(2)}, u32[]{:S(2)}) collective-permute-start(f32[2048,8]{0,1:T(8,128)S(1)} %convolution_bitcast_fusion), channel_id=1, source_target_pairs={{0,24},{8,16},{16,8},{24,0},{32,56},{40,48},{48,40},{56,32},{64,88... | collective-permute-start | bytes 196616 | tf_op jit(solution)/shard_map/ppermute | solution.py:19
  184.7 7.6 %collective-permute-start.1 = (f32[2048,8]{0,1:T(8,128)S(1)}, f32[2048,8]{0,1:T(8,128)S(1)}, u32[]{:S(2)}, u32[]{:S(2)}) collective-permute-start(f32[2048,8]{0,1:T(8,128)S(1)} %convolution_bitcast_fusion), channel_id=1, source_target_pairs={{0,16},{8,24},{16,0},{24,8},{32,48},{40,56},{48,32},{56,40},{64,80... | collective-permute-start | bytes 196616 | tf_op jit(solution)/shard_map/ppermute | solution.py:19
  188.0 4.3 %collective-permute-start = (f32[2048,8]{0,1:T(8,128)S(1)}, f32[2048,8]{0,1:T(8,128)S(1)}, u32[]{:S(2)}, u32[]{:S(2)}) collective-permute-start(f32[2048,8]{0,1:T(8,128)S(1)} %convolution_bitcast_fusion), channel_id=1, source_target_pairs={{0,8},{8,0},{16,24},{24,16},{32,40},{40,32},{48,56},{56,48},{64,72... | collective-permute-start | bytes 196616 | tf_op jit(solution)/shard_map/ppermute | solution.py:19
  192.4 4.9 %collective-permute-start.9 = (f32[2048,8]{0,1:T(8,128)S(1)}, f32[2048,8]{0,1:T(8,128)S(1)}, u32[]{:S(2)}, u32[]{:S(2)}) collective-permute-start(f32[2048,8]{0,1:T(8,128)S(1)} %add_add_fusion.2), channel_id=1, source_target_pairs={{0,192},{8,200},{16,208},{24,216},{32,224},{40,232},{48,240},{56,2... | collective-permute-start | bytes 196616 | tf_op jit(solution)/shard_map/ppermute | solution.py:19
  194.9 4.9 %collective-permute-start.8 = (f32[2048,8]{0,1:T(8,128)S(1)}, f32[2048,8]{0,1:T(8,128)S(1)}, u32[]{:S(2)}, u32[]{:S(2)}) collective-permute-start(f32[2048,8]{0,1:T(8,128)S(1)} %add_add_fusion.2), channel_id=1, source_target_pairs={{0,128},{8,136},{16,144},{24,152},{32,160},{40,168},{48,176},{56,1... | collective-permute-start | bytes 196616 | tf_op jit(solution)/shard_map/ppermute | solution.py:19
  195.4 4.3 %collective-permute-start.7 = (f32[2048,8]{0,1:T(8,128)S(1)}, f32[2048,8]{0,1:T(8,128)S(1)}, u32[]{:S(2)}, u32[]{:S(2)}) collective-permute-start(f32[2048,8]{0,1:T(8,128)S(1)} %add_add_fusion.2), channel_id=1, source_target_pairs={{0,64},{8,72},{16,80},{24,88},{32,96},{40,104},{48,112},{56,120},{... | collective-permute-start | bytes 196616 | tf_op jit(solution)/shard_map/ppermute | solution.py:19
  199.7 20.4 %collective-permute-start.16 = (f32[2048,8]{0,1:T(8,128)S(1)}, f32[2048,8]{0,1:T(8,128)S(1)}, u32[]{:S(2)}, u32[]{:S(2)}) collective-permute-start(f32[2048,8]{0,1:T(8,128)S(1)} %add_add_fusion.1), channel_id=1, source_target_pairs={{0,7},{1,6},{2,5},{3,4},{4,3},{5,2},{6,1},{7,0},{8,15},{9,14},{10,... | collective-permute-start | bytes 196616 | tf_op jit(solution)/shard_map/ppermute | solution.py:19
  201.6 19.2 %collective-permute-start.15 = (f32[2048,8]{0,1:T(8,128)S(1)}, f32[2048,8]{0,1:T(8,128)S(1)}, u32[]{:S(2)}, u32[]{:S(2)}) collective-permute-start(f32[2048,8]{0,1:T(8,128)S(1)} %add_add_fusion.1), channel_id=1, source_target_pairs={{0,6},{1,7},{2,4},{3,5},{4,2},{5,3},{6,0},{7,1},{8,14},{9,15},{10,... | collective-permute-start | bytes 196616 | tf_op jit(solution)/shard_map/ppermute | solution.py:19
  211.4 12.0 %copy-start.5 = (f32[2048,8]{0,1:T(8,128)S(1)}, f32[2048,8]{0,1:T(8,128)}, u32[]{:S(2)}) copy-start(f32[2048,8]{0,1:T(8,128)} %param.11) | copy-start | bytes 196612
  213.9 11.4 %collective-permute-start.14 = (f32[2048,8]{0,1:T(8,128)S(1)}, f32[2048,8]{0,1:T(8,128)S(1)}, u32[]{:S(2)}, u32[]{:S(2)}) collective-permute-start(f32[2048,8]{0,1:T(8,128)S(1)} %add_add_fusion.1), channel_id=1, source_target_pairs={{0,5},{1,4},{2,7},{3,6},{4,1},{5,0},{6,3},{7,2},{8,13},{9,12},{10,... | collective-permute-start | bytes 196616 | tf_op jit(solution)/shard_map/ppermute | solution.py:19
  215.1 10.2 %collective-permute-start.13 = (f32[2048,8]{0,1:T(8,128)S(1)}, f32[2048,8]{0,1:T(8,128)S(1)}, u32[]{:S(2)}, u32[]{:S(2)}) collective-permute-start(f32[2048,8]{0,1:T(8,128)S(1)} %add_add_fusion.1), channel_id=1, source_target_pairs={{0,4},{1,5},{2,6},{3,7},{4,0},{5,1},{6,2},{7,3},{8,12},{9,13},{10,... | collective-permute-start | bytes 196616 | tf_op jit(solution)/shard_map/ppermute | solution.py:19
  219.9 5.4 %collective-permute-start.12 = (f32[2048,8]{0,1:T(8,128)S(1)}, f32[2048,8]{0,1:T(8,128)S(1)}, u32[]{:S(2)}, u32[]{:S(2)}) collective-permute-start(f32[2048,8]{0,1:T(8,128)S(1)} %add_add_fusion.1), channel_id=1, source_target_pairs={{0,3},{1,2},{2,1},{3,0},{4,7},{5,6},{6,5},{7,4},{8,11},{9,10},{10,... | collective-permute-start | bytes 196616 | tf_op jit(solution)/shard_map/ppermute | solution.py:19
  220.1 8.0 %collective-permute-start.11 = (f32[2048,8]{0,1:T(8,128)S(1)}, f32[2048,8]{0,1:T(8,128)S(1)}, u32[]{:S(2)}, u32[]{:S(2)}) collective-permute-start(f32[2048,8]{0,1:T(8,128)S(1)} %add_add_fusion.1), channel_id=1, source_target_pairs={{0,2},{1,3},{2,0},{3,1},{4,6},{5,7},{6,4},{7,5},{8,10},{9,11},{10,... | collective-permute-start | bytes 196616 | tf_op jit(solution)/shard_map/ppermute | solution.py:19
  220.9 7.3 %collective-permute-start.10 = (f32[2048,8]{0,1:T(8,128)S(1)}, f32[2048,8]{0,1:T(8,128)S(1)}, u32[]{:S(2)}, u32[]{:S(2)}) collective-permute-start(f32[2048,8]{0,1:T(8,128)S(1)} %add_add_fusion.1), channel_id=1, source_target_pairs={{0,1},{1,0},{2,3},{3,2},{4,5},{5,4},{6,7},{7,6},{8,9},{9,8},{10,11... | collective-permute-start | bytes 196616 | tf_op jit(solution)/shard_map/ppermute | solution.py:19
Sparse Core Ops, SparseCore 0:
  110.2 86.3 reduce-scatter.4
  200.6 92.6 reduce-scatter.2

commit v7 on v5

--- a/solution.py
+++ b/solution.py
@@ -59,6 +59,24 @@
         out_specs=pl.BlockSpec((tile, 3 * hidden), lambda i: (i, 0)),
         out_shape=jax.ShapeDtypeStruct((width, 3 * hidden), jnp.bfloat16),
     )(rows, grads, deltas, activated)
+
+
+def halving_scatter(parts, axis):
+    size = lax.axis_size(axis)
+    me = lax.axis_index(axis)
+    rows = parts.shape[0] // size
+    acc = parts.reshape(size, rows, parts.shape[1]).astype(jnp.float32)
+    bits = (size - 1).bit_length()
+    for bit in range(bits):
+        cur = acc.reshape(size >> (bit + 1), 2, rows, parts.shape[1])
+        mine = (me >> bit) & 1
+        keep = lax.dynamic_index_in_dim(cur, mine, axis=1, keepdims=False)
+        send = lax.dynamic_index_in_dim(cur, 1 - mine, axis=1, keepdims=False)
+        if bit < 3:
+            send = send.astype(jnp.bfloat16)
+        pairs = [(i, i ^ (1 << bit)) for i in range(size)]
+        acc = keep + lax.ppermute(send, axis, pairs).astype(jnp.float32)
+    return acc.reshape(rows, parts.shape[1])
 
 
 def on_device(tokens, expert_ids, slot_index, w_router, w_gate, w_up, w_down, grad_out):
@@ -141,7 +159,7 @@
             .reshape(lax.axis_size("dp") * own_rows, local_count * 3 * hidden_width)
             .astype(jnp.bfloat16)
         )
-    joined = lax.psum_scatter(partials, "dp", scatter_dimension=0, tiled=True).astype(jnp.float32)
+    joined = halving_scatter(partials, "dp")
     triple_view = joined.reshape(-1, local_count, 3, hidden_width)
     grad_gate = jnp.transpose(triple_view[:, :, 0, :], (1, 0, 2))
     grad_up = jnp.transpose(triple_view[:, :, 1, :], (1, 0, 2))

time: 241 us -> 325 us (1.35); the launches traced: 240 us -> 320 us
  waiting for transfers between devices: 56.9 us -> 164 us
  blocking collectives: 81.3 us -> 0 us
  other arithmetic: 6.32 us -> 37.8 us
  local copies, waits for them, and re-layouts: 10 us -> 26.7 us
  starting transfers between devices: 34.6 us -> 50.5 us
  between operations: 14.3 us -> 0.95 us
  matrix products: 27.5 us -> 30.8 us
    all_to_all x1 -> x0, blocking collectives: 81.3 us -> none  [on_device(): lax.all_to_all(jnp.concatenate([outgoing, grad_rows], axis=1), 'expert',...]
    all_to_all x0 -> x1, waiting for transfers between devices: none -> 74.4 us  [on_device(): lax.all_to_all(jnp.concatenate([outgoing, grad_rows], axis=1), 'expert',...]
    ppermute x0 -> x5, waiting for transfers between devices: none -> 63.5 us  [halving_scatter(): acc = keep + lax.ppermute(send, axis, pairs).astype(jnp.float32)]
    all_to_all x1, waiting for transfers between devices: 34.3 us -> 0.01 us  [on_device(): lax.all_to_all(expert_out.reshape(flat_rows), 'expert', split_axis=0, con...]
    add x0 -> x5, other arithmetic: none -> 17.3 us  [halving_scatter(): acc = keep + lax.ppermute(send, axis, pairs).astype(jnp.float32)]
    convert_element_type x0 -> x1, other arithmetic: none -> 12.6 us  [halving_scatter(): acc = parts.reshape(size, rows, parts.shape[1]).astype(jnp.float32)]
    convert_element_type x0 -> x3, local copies, waits for them, and re-layouts: none -> 11.8 us  [halving_scatter(): send = send.astype(jnp.bfloat16)]
    all_to_all x0 -> x1, starting transfers between devices: none -> 9.01 us  [on_device(): lax.all_to_all(jnp.concatenate([outgoing, grad_rows], axis=1), 'expert',...]
  transfers between devices with their start and end apart: 20 -> 25, of which waited for: 9 -> 10; matrix products, arithmetic and copies ran while one was open for 8% -> 8% of each run, Pallas kernels for 0% -> 0%
where the time goes in v7:
time: 325 us; the launch traced here: 320 us
  waiting for transfers between devices  164 us (50%)
  starting transfers between devices  50.5 us (16%)
  other arithmetic  37.8 us (12%)
  matrix products  30.8 us (9%)
  local copies, waits for them, and re-layouts  26.7 us (8%)
  Pallas kernels  9.18 us (3%)
    all_to_all x1, waiting for transfers between devices, on_device(): lax.all_to_all(jnp.concatenate([outgoing, grad_rows], axis=1), 'expert',...  74.4 us
    ppermute x5, waiting for transfers between devices, halving_scatter(): acc = keep + lax.ppermute(send, axis, pairs).astype(jnp.float32)  63.5 us
    ppermute x17, starting transfers between devices, group_sum(): got.append(lax.ppermute(value, axis, pairs))  24.7 us
    ppermute x17, waiting for transfers between devices, group_sum(): got.append(lax.ppermute(value, axis, pairs))  22.5 us
    add x5, other arithmetic, halving_scatter(): acc = keep + lax.ppermute(send, axis, pairs).astype(jnp.float32)  17.3 us
    convert_element_type x1, other arithmetic, halving_scatter(): acc = parts.reshape(size, rows, parts.shape[1]).astype(jnp.float32)  12.6 us
    convert_element_type x3, local copies, waits for them, and re-layouts, halving_scatter(): send = send.astype(jnp.bfloat16)  11.8 us
    pallas_call x1, Pallas kernels, weight_grads(): pl.pallas_call(weight_grad_kernel, grid=(width // tile,), in_specs=[pl.Bl...  9.18 us
  transfers between devices with their start and end apart: 25, of which 10 were waited for; matrix products, arithmetic and copies ran while one was open for 8% of the time, Pallas kernels for 0%

profile of v7, /device:TPU:1, one launch (start us, length us, event | category | flops | bytes accessed | tf_op | source)
XLA Modules:
  0.0 319.7 jit_solution(14153394643729890810)
XLA Ops:
  9.3 9.0 %all-to-all-start = ((bf16[8,96,2048]{2,1,0:T(8,128)(2,1)}), bf16[8,96,2048]{2,1,0:T(8,128)(2,1)}, u32[]{:S(2)}, u32[]{:S(2)}) async-start(bf16[8,96,2048]{2,1,0:T(8,128)(2,1)} %pad_maximum_fusion), calls=%async_computation | async-start | bytes 6291456 | tf_op jit(solution)/shard_map/all_to_all | solution.py:113
  18.3 74.4 %all-to-all-done = bf16[8,96,2048]{2,1,0:T(8,128)(2,1)} async-done(((bf16[8,96,2048]{2,1,0:T(8,128)(2,1)}), bf16[8,96,2048]{2,1,0:T(8,128)(2,1)}, u32[]{:S(2)}, u32[]{:S(2)}) %all-to-all-start) | async-done | bytes 3145760 | tf_op jit(solution)/shard_map/all_to_all | solution.py:113
  92.6 3.9 %fusion.26 = f32[8,1,48,768]{3,2,0,1:T(8,128)S(1)} fusion(bf16[1,2048,768]{2,1,0:T(8,128)(2,1)} %param.14, bf16[8,96,2048]{2,1,0:T(8,128)(2,1)} %all-to-all-done), kind=kOutput, calls=%fused_computation.33 | convolution fusion | flops 1207959552 | bytes 5898240 | tf_op jit(solution)/shard_map/slnd,ldf->slnf/dot_general | solution.py:134
  96.6 2.8 fusion.23
  99.4 4.0 %multiply_convert_fusion.2 = (bf16[8,1,48,768]{3,2,0,1:T(8,128)(2,1)S(1)}, bf16[8,1,48,768]{3,2,0,1:T(8,128)(2,1)S(1)}, bf16[8,1,48,768]{3,2,0,1:T(8,128)(2,1)}) fusion(f32[8,1,48,768]{3,2,0,1:T(8,128)S(1)} %fusion.26, f32[8,1,48,768]{3,2,0,1:T(8,128)S(1)} %fusion.23, bf16[1,2048,768]{2,1,0:T(8,128)(2,1)S(1)} %copy-done, bf16[8,96,2048]{2,1,0:T(8,128)(2,1)} %all-to-all-done), kind=kOutput, calls=%fused_computation.39 | convolution fusion | flops 1212383232 | bytes 8847360 | tf_op jit(solution)/shard_map/slnd,ldf->slnf/dot_general | solution.py:119
  105.5 4.0 %fusion.49 = (bf16[8,48,2048]{2,1,0:T(8,128)(2,1)}, bf16[8,48,2048]{2,1,0:T(8,128)(2,1)}) fusion(bf16[8,96,2048]{2,1,0:T(8,128)(2,1)} %all-to-all-done), kind=kLoop, calls=%fused_computation.90 | loop fusion | bytes 6291456 | tf_op jit(solution)/shard_map/slice | solution.py:118
  109.5 9.2 %shard_map.127 = bf16[2048,2304]{1,0:T(8,128)(2,1)} custom-call(bf16[384,2048]{1,0:T(8,128)(2,1)} %bitcast.131, bf16[384,2048]{1,0:T(8,128)(2,1)} %bitcast.130, bf16[384,1536]{1,0:T(8,128)(2,1)} %pad_maximum_fusion.1.deltas_ref, bf16[384,768]{1,0:T(8,128)(2,1)} %bitcast.134), custom_call_target="tpu_custom_call" | custom-call | tf_op jit(solution)/shard_map/pallas_call | solution.py:50
  118.7 12.6 %convert.1 = f32[16,2,64,2304]{3,2,1,0:T(8,128)} convert(bf16[16,2,64,2304]{3,2,1,0:T(8,128)(2,1)} %bitcast.123) | non-fusion elementwise | flops 4718592 | bytes 28311552 | tf_op jit(solution)/shard_map/convert_element_type | solution.py:68
  131.2 6.5 %fusion = bf16[16,64,2304]{2,1,0:T(8,128)(2,1)} fusion(f32[16,2,64,2304]{3,2,1,0:T(8,128)} %convert.1, s32[]{:T(128)S(6)} %select_n.51), kind=kLoop, calls=%fused_computation.2 | loop fusion | bytes 9437188 | tf_op jit(solution)/shard_map/convert_element_type | solution.py:76
  138.2 7.9 %collective-permute-done.17 = bf16[16,64,2304]{2,1,0:T(8,128)(2,1)} collective-permute-done((bf16[16,64,2304]{2,1,0:T(8,128)(2,1)}, bf16[16,64,2304]{2,1,0:T(8,128)(2,1)}, u32[]{:S(2)}, u32[]{:S(2)}) %collective-permute-start.17) | collective-permute-done | bytes 4718624 | tf_op jit(solution)/shard_map/ppermute | solution.py:78
  146.1 9.9 %bitcast_add_fusion = f32[16,64,2304]{2,1,0:T(8,128)} fusion(bf16[16,64,2304]{2,1,0:T(8,128)(2,1)} %collective-permute-done.17, f32[16,2,64,2304]{3,2,1,0:T(8,128)} %convert.1, s32[]{:T(128)S(6)} %select_n.50), kind=kLoop, calls=%fused_computation.1 | loop fusion | flops 4718592 | bytes 23592964 | tf_op jit(solution)/shard_map/add | solution.py:78
  156.0 4.2 %fusion.19 = bf16[8,64,2304]{2,1,0:T(8,128)(2,1)} fusion(f32[8,2,64,2304]{3,2,1,0:T(8,128)} %bitcast.124, s32[]{:T(128)S(6)} %select_n.53), kind=kLoop, calls=%fused_computation.24 | loop fusion | bytes 4718596 | tf_op jit(solution)/shard_map/convert_element_type | solution.py:76
  161.5 2.7 fusion.15
  164.1 4.3 %all-to-all-start.1 = ((bf16[8,48,2048]{2,1,0:T(8,128)(2,1)}), bf16[8,48,2048]{2,1,0:T(8,128)(2,1)}, u32[]{:S(2)}, u32[]{:S(2)}) async-start(bf16[8,48,2048]{2,1,0:T(8,128)(2,1)} %fusion.15), calls=%async_computation.1 | async-start | bytes 3145728 | tf_op jit(solution)/shard_map/all_to_all | solution.py:131
  168.4 3.5 %fusion.5 = f32[8,48,2048]{2,1,0:T(8,128)S(1)} fusion(bf16[1,2048,768]{2,1,0:T(8,128)(2,1)} %param.13, bf16[8,1,48,768]{3,2,0,1:T(8,128)(2,1)} %copy-done.11), kind=kOutput, calls=%fused_computation.10 | convolution fusion | flops 1207959552 | bytes 6881280 | tf_op jit(solution)/shard_map/slnf,ldf->slnd/dot_general | solution.py:139
  172.0 2.6 add_convert_fusion
  174.6 38.3 %collective-permute-done.18 = bf16[8,64,2304]{2,1,0:T(8,128)(2,1)} collective-permute-done((bf16[8,64,2304]{2,1,0:T(8,128)(2,1)}, bf16[8,64,2304]{2,1,0:T(8,128)(2,1)}, u32[]{:S(2)}, u32[]{:S(2)}) %collective-permute-start.18) | collective-permute-done | bytes 2359328 | tf_op jit(solution)/shard_map/ppermute | solution.py:78
  212.9 3.5 %bitcast_add_fusion.1 = f32[8,64,2304]{2,1,0:T(8,128)S(1)} fusion(bf16[8,64,2304]{2,1,0:T(8,128)(2,1)} %collective-permute-done.18, f32[8,2,64,2304]{3,2,1,0:T(8,128)} %bitcast.125, s32[]{:T(128)S(6)} %select_n.52), kind=kLoop, calls=%fused_computation.3 | loop fusion | flops 2359296 | bytes 11796484 | tf_op jit(solution)/shard_map/add | solution.py:78
  219.7 2.9 collective-permute-start.19
  222.6 4.3 %all-to-all-start.2 = ((bf16[8,48,2048]{2,1,0:T(8,128)(2,1)}), bf16[8,48,2048]{2,1,0:T(8,128)(2,1)}, u32[]{:S(2)}, u32[]{:S(2)}) async-start(bf16[8,48,2048]{2,1,0:T(8,128)(2,1)} %add_convert_fusion), calls=%async_computation.2 | async-start | bytes 3145728 | tf_op jit(solution)/shard_map/all_to_all | solution.py:141
  227.0 2.5 fusion.42
  232.2 3.6 %collective-permute-start.6 = (f32[2048,8]{0,1:T(8,128)S(1)}, f32[2048,8]{0,1:T(8,128)S(1)}, u32[]{:S(2)}, u32[]{:S(2)}) collective-permute-start(f32[2048,8]{0,1:T(8,128)S(1)} %convolution_bitcast_fusion), channel_id=1, source_target_pairs={{0,56},{8,48},{16,40},{24,32},{32,24},{40,16},{48,8},{56,0},{64,12... | collective-permute-start | bytes 196616 | tf_op jit(solution)/shard_map/ppermute | solution.py:19
  237.6 10.2 %collective-permute-done.19 = bf16[4,64,2304]{2,1,0:T(8,128)(2,1)} collective-permute-done((bf16[4,64,2304]{2,1,0:T(8,128)(2,1)}, bf16[4,64,2304]{2,1,0:T(8,128)(2,1)}, u32[]{:S(2)}, u32[]{:S(2)}) %collective-permute-start.19) | collective-permute-done | bytes 1179680 | tf_op jit(solution)/shard_map/ppermute | solution.py:78
  250.7 2.9 collective-permute-done.5
  258.2 2.8 collective-permute-start.8
  261.9 3.4 %all-to-all-done.2 = bf16[8,48,2048]{2,1,0:T(8,128)(2,1)} async-done(((bf16[8,48,2048]{2,1,0:T(8,128)(2,1)}), bf16[8,48,2048]{2,1,0:T(8,128)(2,1)}, u32[]{:S(2)}, u32[]{:S(2)}) %all-to-all-start.2) | async-done | bytes 1572896 | tf_op jit(solution)/shard_map/all_to_all | solution.py:141
  265.2 2.6 fusion.41
  267.8 19.0 %collective-permute-done.8 = f32[2048,8]{0,1:T(8,128)S(1)} collective-permute-done((f32[2048,8]{0,1:T(8,128)S(1)}, f32[2048,8]{0,1:T(8,128)S(1)}, u32[]{:S(2)}, u32[]{:S(2)}) %collective-permute-start.8) | collective-permute-done | bytes 65568 | tf_op jit(solution)/shard_map/ppermute | solution.py:19
  287.1 2.5 collective-permute-start.16
  290.7 5.2 %collective-permute-start.14 = (f32[2048,8]{0,1:T(8,128)S(1)}, f32[2048,8]{0,1:T(8,128)S(1)}, u32[]{:S(2)}, u32[]{:S(2)}) collective-permute-start(f32[2048,8]{0,1:T(8,128)S(1)} %add_add_fusion.1), channel_id=1, source_target_pairs={{0,5},{1,4},{2,7},{3,6},{4,1},{5,0},{6,3},{7,2},{8,13},{9,12},{10,... | collective-permute-start | bytes 196616 | tf_op jit(solution)/shard_map/ppermute | solution.py:19
  305.1 7.0 %collective-permute-done.21 = f32[1,64,2304]{2,1,0:T(8,128)S(1)} collective-permute-done((f32[1,64,2304]{2,1,0:T(8,128)S(1)}, f32[1,64,2304]{2,1,0:T(8,128)S(1)}, u32[]{:S(2)}, u32[]{:S(2)}) %collective-permute-start.21) | collective-permute-done | bytes 589856 | tf_op jit(solution)/shard_map/ppermute | solution.py:78
  315.3 2.3 slice_bitcast_fusion
  (96 shorter events, 44.2 us)
Async XLA Ops:
  0.6 98.7 %copy-start = (bf16[1,2048,768]{2,1,0:T(8,128)(2,1)S(1)}, bf16[1,2048,768]{2,1,0:T(8,128)(2,1)}, u32[]{:S(2)}) copy-start(bf16[1,2048,768]{2,1,0:T(8,128)(2,1)} %param.12) | copy-start | bytes 9437188
  0.6 5.9 %copy-start.6 = (bf16[128,2048]{1,0:T(8,128)(2,1)S(1)}, bf16[128,2048]{1,0:T(8,128)(2,1)}, u32[]{:S(2)}) copy-start(bf16[128,2048]{1,0:T(8,128)(2,1)} %param.15) | copy-start | bytes 1572868
  9.3 83.4 %all-to-all-start = ((bf16[8,96,2048]{2,1,0:T(8,128)(2,1)}), bf16[8,96,2048]{2,1,0:T(8,128)(2,1)}, u32[]{:S(2)}, u32[]{:S(2)}) async-start(bf16[8,96,2048]{2,1,0:T(8,128)(2,1)} %pad_maximum_fusion), calls=%async_computation | async-start | bytes 6291456 | tf_op jit(solution)/shard_map/all_to_all | solution.py:113
  137.7 8.4 %collective-permute-start.17 = (bf16[16,64,2304]{2,1,0:T(8,128)(2,1)}, bf16[16,64,2304]{2,1,0:T(8,128)(2,1)}, u32[]{:S(2)}, u32[]{:S(2)}) collective-permute-start(bf16[16,64,2304]{2,1,0:T(8,128)(2,1)} %fusion), channel_id=1, source_target_pairs={{0,8},{8,0},{16,24},{24,16},{32,40},{40,32},{48,56},{56,48},{64,72... | collective-permute-start | bytes 14155784 | tf_op jit(solution)/shard_map/ppermute | solution.py:78
  156.0 5.5 %copy-start.8 = (bf16[8,1,48,768]{3,2,0,1:T(8,128)(2,1)S(1)}, bf16[8,1,48,768]{3,2,0,1:T(8,128)(2,1)}, u32[]{:S(2)}) copy-start(bf16[8,1,48,768]{3,2,0,1:T(8,128)(2,1)} %get-tuple-element.46) | copy-start | bytes 1769476
  156.0 5.5 %copy-start.14 = (bf16[1,2048,768]{2,1,0:T(8,128)(2,1)S(1)}, bf16[1,2048,768]{2,1,0:T(8,128)(2,1)}, u32[]{:S(2)}) copy-start(bf16[1,2048,768]{2,1,0:T(8,128)(2,1)} %param.14) | copy-start | bytes 9437188
  160.2 52.8 %collective-permute-start.18 = (bf16[8,64,2304]{2,1,0:T(8,128)(2,1)}, bf16[8,64,2304]{2,1,0:T(8,128)(2,1)}, u32[]{:S(2)}, u32[]{:S(2)}) collective-permute-start(bf16[8,64,2304]{2,1,0:T(8,128)(2,1)} %fusion.19), channel_id=1, source_target_pairs={{0,16},{8,24},{16,0},{24,8},{32,48},{40,56},{48,32},{56,40},{64,80... | collective-permute-start | bytes 7077896 | tf_op jit(solution)/shard_map/ppermute | solution.py:78
  164.1 58.5 %all-to-all-start.1 = ((bf16[8,48,2048]{2,1,0:T(8,128)(2,1)}), bf16[8,48,2048]{2,1,0:T(8,128)(2,1)}, u32[]{:S(2)}, u32[]{:S(2)}) async-start(bf16[8,48,2048]{2,1,0:T(8,128)(2,1)} %fusion.15), calls=%async_computation.1 | async-start | bytes 3145728 | tf_op jit(solution)/shard_map/all_to_all | solution.py:131
  219.7 28.2 %collective-permute-start.19 = (bf16[4,64,2304]{2,1,0:T(8,128)(2,1)}, bf16[4,64,2304]{2,1,0:T(8,128)(2,1)}, u32[]{:S(2)}, u32[]{:S(2)}) collective-permute-start(bf16[4,64,2304]{2,1,0:T(8,128)(2,1)} %fusion.29), channel_id=1, source_target_pairs={{0,32},{8,40},{16,48},{24,56},{32,0},{40,8},{48,16},{56,24},{64,96... | collective-permute-start | bytes 3538952 | tf_op jit(solution)/shard_map/ppermute | solution.py:78
  222.6 42.6 %all-to-all-start.2 = ((bf16[8,48,2048]{2,1,0:T(8,128)(2,1)}), bf16[8,48,2048]{2,1,0:T(8,128)(2,1)}, u32[]{:S(2)}, u32[]{:S(2)}) async-start(bf16[8,48,2048]{2,1,0:T(8,128)(2,1)} %add_convert_fusion), calls=%async_computation.2 | async-start | bytes 3145728 | tf_op jit(solution)/shard_map/all_to_all | solution.py:141
  229.6 19.6 %copy-start.2 = (f32[8,64,2304]{2,1,0:T(8,128)S(1)}, f32[8,64,2304]{2,1,0:T(8,128)}, u32[]{:S(2)}) copy-start(f32[8,64,2304]{2,1,0:T(8,128)} %copy-done.1) | copy-start | bytes 14155780
  231.4 22.3 %collective-permute-start.5 = (f32[2048,8]{0,1:T(8,128)S(1)}, f32[2048,8]{0,1:T(8,128)S(1)}, u32[]{:S(2)}, u32[]{:S(2)}) collective-permute-start(f32[2048,8]{0,1:T(8,128)S(1)} %convolution_bitcast_fusion), channel_id=1, source_target_pairs={{0,48},{8,56},{16,32},{24,40},{32,16},{40,24},{48,0},{56,8},{64,11... | collective-permute-start | bytes 196616 | tf_op jit(solution)/shard_map/ppermute | solution.py:19
  232.2 23.1 %collective-permute-start.6 = (f32[2048,8]{0,1:T(8,128)S(1)}, f32[2048,8]{0,1:T(8,128)S(1)}, u32[]{:S(2)}, u32[]{:S(2)}) collective-permute-start(f32[2048,8]{0,1:T(8,128)S(1)} %convolution_bitcast_fusion), channel_id=1, source_target_pairs={{0,56},{8,48},{16,40},{24,32},{32,24},{40,16},{48,8},{56,0},{64,12... | collective-permute-start | bytes 196616 | tf_op jit(solution)/shard_map/ppermute | solution.py:19
  235.8 20.7 %collective-permute-start.3 = (f32[2048,8]{0,1:T(8,128)S(1)}, f32[2048,8]{0,1:T(8,128)S(1)}, u32[]{:S(2)}, u32[]{:S(2)}) collective-permute-start(f32[2048,8]{0,1:T(8,128)S(1)} %convolution_bitcast_fusion), channel_id=1, source_target_pairs={{0,32},{8,40},{16,48},{24,56},{32,0},{40,8},{48,16},{56,24},{64,96... | collective-permute-start | bytes 196616 | tf_op jit(solution)/shard_map/ppermute | solution.py:19
  235.8 21.9 %collective-permute-start.4 = (f32[2048,8]{0,1:T(8,128)S(1)}, f32[2048,8]{0,1:T(8,128)S(1)}, u32[]{:S(2)}, u32[]{:S(2)}) collective-permute-start(f32[2048,8]{0,1:T(8,128)S(1)} %convolution_bitcast_fusion), channel_id=1, source_target_pairs={{0,40},{8,32},{16,56},{24,48},{32,8},{40,0},{48,24},{56,16},{64,10... | collective-permute-start | bytes 196616 | tf_op jit(solution)/shard_map/ppermute | solution.py:19
  247.9 9.8 %collective-permute-start.1 = (f32[2048,8]{0,1:T(8,128)S(1)}, f32[2048,8]{0,1:T(8,128)S(1)}, u32[]{:S(2)}, u32[]{:S(2)}) collective-permute-start(f32[2048,8]{0,1:T(8,128)S(1)} %convolution_bitcast_fusion), channel_id=1, source_target_pairs={{0,16},{8,24},{16,0},{24,8},{32,48},{40,56},{48,32},{56,40},{64,80... | collective-permute-start | bytes 196616 | tf_op jit(solution)/shard_map/ppermute | solution.py:19
  253.6 4.5 %collective-permute-start.2 = (f32[2048,8]{0,1:T(8,128)S(1)}, f32[2048,8]{0,1:T(8,128)S(1)}, u32[]{:S(2)}, u32[]{:S(2)}) collective-permute-start(f32[2048,8]{0,1:T(8,128)S(1)} %convolution_bitcast_fusion), channel_id=1, source_target_pairs={{0,24},{8,16},{16,8},{24,0},{32,56},{40,48},{48,40},{56,32},{64,88... | collective-permute-start | bytes 196616 | tf_op jit(solution)/shard_map/ppermute | solution.py:19
  255.3 2.8 collective-permute-start
  256.5 39.5 %collective-permute-start.20 = (f32[2,64,2304]{2,1,0:T(8,128)}, f32[2,64,2304]{2,1,0:T(8,128)}, u32[]{:S(2)}, u32[]{:S(2)}) collective-permute-start(f32[2,64,2304]{2,1,0:T(8,128)} %dynamic-slice_bitcast_fusion), channel_id=1, source_target_pairs={{0,64},{8,72},{16,80},{24,88},{32,96},{40,104},{48,112},{56,120},{... | collective-permute-start | bytes 3538952 | tf_op jit(solution)/shard_map/ppermute | solution.py:78
  258.2 28.7 %collective-permute-start.8 = (f32[2048,8]{0,1:T(8,128)S(1)}, f32[2048,8]{0,1:T(8,128)S(1)}, u32[]{:S(2)}, u32[]{:S(2)}) collective-permute-start(f32[2048,8]{0,1:T(8,128)S(1)} %add_add_fusion.2), channel_id=1, source_target_pairs={{0,128},{8,136},{16,144},{24,152},{32,160},{40,168},{48,176},{56,1... | collective-permute-start | bytes 196616 | tf_op jit(solution)/shard_map/ppermute | solution.py:19
  261.0 25.9 %collective-permute-start.9 = (f32[2048,8]{0,1:T(8,128)S(1)}, f32[2048,8]{0,1:T(8,128)S(1)}, u32[]{:S(2)}, u32[]{:S(2)}) collective-permute-start(f32[2048,8]{0,1:T(8,128)S(1)} %add_add_fusion.2), channel_id=1, source_target_pairs={{0,192},{8,200},{16,208},{24,216},{32,224},{40,232},{48,240},{56,2... | collective-permute-start | bytes 196616 | tf_op jit(solution)/shard_map/ppermute | solution.py:19
  261.9 25.0 %collective-permute-start.7 = (f32[2048,8]{0,1:T(8,128)S(1)}, f32[2048,8]{0,1:T(8,128)S(1)}, u32[]{:S(2)}, u32[]{:S(2)}) collective-permute-start(f32[2048,8]{0,1:T(8,128)S(1)} %add_add_fusion.2), channel_id=1, source_target_pairs={{0,64},{8,72},{16,80},{24,88},{32,96},{40,104},{48,112},{56,120},{... | collective-permute-start | bytes 196616 | tf_op jit(solution)/shard_map/ppermute | solution.py:19
  265.2 30.7 %copy-start.4 = (f32[4,64,2304]{2,1,0:T(8,128)S(1)}, f32[4,64,2304]{2,1,0:T(8,128)}, u32[]{:S(2)}) copy-start(f32[4,64,2304]{2,1,0:T(8,128)} %copy-done.3) | copy-start | bytes 7077892
  286.9 15.5 %copy-start.12 = (f32[2048,8]{0,1:T(8,128)S(1)}, f32[2048,8]{0,1:T(8,128)}, u32[]{:S(2)}) copy-start(f32[2048,8]{0,1:T(8,128)} %param.11) | copy-start | bytes 196612
  286.9 10.5 %collective-permute-start.15 = (f32[2048,8]{0,1:T(8,128)S(1)}, f32[2048,8]{0,1:T(8,128)S(1)}, u32[]{:S(2)}, u32[]{:S(2)}) collective-permute-start(f32[2048,8]{0,1:T(8,128)S(1)} %add_add_fusion.1), channel_id=1, source_target_pairs={{0,6},{1,7},{2,4},{3,5},{4,2},{5,3},{6,0},{7,1},{8,14},{9,15},{10,... | collective-permute-start | bytes 196616 | tf_op jit(solution)/shard_map/ppermute | solution.py:19
  287.1 11.8 %collective-permute-start.16 = (f32[2048,8]{0,1:T(8,128)S(1)}, f32[2048,8]{0,1:T(8,128)S(1)}, u32[]{:S(2)}, u32[]{:S(2)}) collective-permute-start(f32[2048,8]{0,1:T(8,128)S(1)} %add_add_fusion.1), channel_id=1, source_target_pairs={{0,7},{1,6},{2,5},{3,4},{4,3},{5,2},{6,1},{7,0},{8,15},{9,14},{10,... | collective-permute-start | bytes 196616 | tf_op jit(solution)/shard_map/ppermute | solution.py:19
  289.6 10.6 %collective-permute-start.13 = (f32[2048,8]{0,1:T(8,128)S(1)}, f32[2048,8]{0,1:T(8,128)S(1)}, u32[]{:S(2)}, u32[]{:S(2)}) collective-permute-start(f32[2048,8]{0,1:T(8,128)S(1)} %add_add_fusion.1), channel_id=1, source_target_pairs={{0,4},{1,5},{2,6},{3,7},{4,0},{5,1},{6,2},{7,3},{8,12},{9,13},{10,... | collective-permute-start | bytes 196616 | tf_op jit(solution)/shard_map/ppermute | solution.py:19
  290.7 13.7 %collective-permute-start.14 = (f32[2048,8]{0,1:T(8,128)S(1)}, f32[2048,8]{0,1:T(8,128)S(1)}, u32[]{:S(2)}, u32[]{:S(2)}) collective-permute-start(f32[2048,8]{0,1:T(8,128)S(1)} %add_add_fusion.1), channel_id=1, source_target_pairs={{0,5},{1,4},{2,7},{3,6},{4,1},{5,0},{6,3},{7,2},{8,13},{9,12},{10,... | collective-permute-start | bytes 196616 | tf_op jit(solution)/shard_map/ppermute | solution.py:19
  295.9 8.5 %collective-permute-start.11 = (f32[2048,8]{0,1:T(8,128)S(1)}, f32[2048,8]{0,1:T(8,128)S(1)}, u32[]{:S(2)}, u32[]{:S(2)}) collective-permute-start(f32[2048,8]{0,1:T(8,128)S(1)} %add_add_fusion.1), channel_id=1, source_target_pairs={{0,2},{1,3},{2,0},{3,1},{4,6},{5,7},{6,4},{7,5},{8,10},{9,11},{10,... | collective-permute-start | bytes 196616 | tf_op jit(solution)/shard_map/ppermute | solution.py:19
  297.4 7.0 %collective-permute-start.12 = (f32[2048,8]{0,1:T(8,128)S(1)}, f32[2048,8]{0,1:T(8,128)S(1)}, u32[]{:S(2)}, u32[]{:S(2)}) collective-permute-start(f32[2048,8]{0,1:T(8,128)S(1)} %add_add_fusion.1), channel_id=1, source_target_pairs={{0,3},{1,2},{2,1},{3,0},{4,7},{5,6},{6,5},{7,4},{8,11},{9,10},{10,... | collective-permute-start | bytes 196616 | tf_op jit(solution)/shard_map/ppermute | solution.py:19
  298.9 5.5 %collective-permute-start.10 = (f32[2048,8]{0,1:T(8,128)S(1)}, f32[2048,8]{0,1:T(8,128)S(1)}, u32[]{:S(2)}, u32[]{:S(2)}) collective-permute-start(f32[2048,8]{0,1:T(8,128)S(1)} %add_add_fusion.1), channel_id=1, source_target_pairs={{0,1},{1,0},{2,3},{3,2},{4,5},{5,4},{6,7},{7,6},{8,9},{9,8},{10,11... | collective-permute-start | bytes 196616 | tf_op jit(solution)/shard_map/ppermute | solution.py:19
  300.2 11.9 %collective-permute-start.21 = (f32[1,64,2304]{2,1,0:T(8,128)S(1)}, f32[1,64,2304]{2,1,0:T(8,128)S(1)}, u32[]{:S(2)}, u32[]{:S(2)}) collective-permute-start(f32[1,64,2304]{2,1,0:T(8,128)S(1)} %constant_dynamic-slice_fusion), channel_id=1, source_target_pairs={{0,128},{8,136},{16,144},{24,152},{32,160},{40,168},{48,176},{56,1... | collective-permute-start | bytes 1769480 | tf_op jit(solution)/shard_map/ppermute | solution.py:78
  (9 other events, 24.2 us)

commit v8 on v5

--- a/solution.py
+++ b/solution.py
@@ -32,33 +32,33 @@
     return value
 
 
-def weight_grad_kernel(rows_ref, grads_ref, deltas_ref, act_ref, out_ref):
-    split = deltas_ref.shape[1]
+def weight_grad_kernel(rows_ref, grads_ref, gate_ref, up_ref, act_ref, out_ref):
+    split = gate_ref.shape[1]
     inner = (((0,), (0,)), ((), ()))
-    both = lax.dot_general(rows_ref[...], deltas_ref[...], inner, preferred_element_type=jnp.float32)
-    down = lax.dot_general(grads_ref[...], act_ref[...], inner, preferred_element_type=jnp.float32)
-    out_ref[:, :split] = both.astype(out_ref.dtype)
-    out_ref[:, split:] = down.astype(out_ref.dtype)
+    rows = rows_ref[...]
+    for col, (lhs, rhs) in enumerate(((rows, gate_ref), (rows, up_ref), (grads_ref[...], act_ref))):
+        part = lax.dot_general(lhs, rhs[...], inner, preferred_element_type=jnp.float32)
+        out_ref[:, col * split : (col + 1) * split] = part.astype(out_ref.dtype)
 
 
 def weight_grads(rows, grads, gate_delta, up_delta, activated):
     width = rows.shape[1]
     count = rows.shape[0]
     hidden = activated.shape[1]
-    deltas = jnp.concatenate([gate_delta, up_delta], axis=1)
-    tile = 512
+    tile = 1024
     return pl.pallas_call(
         weight_grad_kernel,
         grid=(width // tile,),
         in_specs=[
             pl.BlockSpec((count, tile), lambda i: (0, i)),
             pl.BlockSpec((count, tile), lambda i: (0, i)),
-            pl.BlockSpec((count, 2 * hidden), lambda i: (0, 0)),
+            pl.BlockSpec((count, hidden), lambda i: (0, 0)),
+            pl.BlockSpec((count, hidden), lambda i: (0, 0)),
             pl.BlockSpec((count, hidden), lambda i: (0, 0)),
         ],
         out_specs=pl.BlockSpec((tile, 3 * hidden), lambda i: (i, 0)),
         out_shape=jax.ShapeDtypeStruct((width, 3 * hidden), jnp.bfloat16),
-    )(rows, grads, deltas, activated)
+    )(rows, grads, gate_delta, up_delta, activated)
 
 
 def on_device(tokens, expert_ids, slot_index, w_router, w_gate, w_up, w_down, grad_out):

time: 241 us -> 241 us (level)
  transfers between devices with their start and end apart: 20 -> 20, of which waited for: 9 -> 12; matrix products, arithmetic and copies ran while one was open for 8% -> 8% of each run, Pallas kernels for 0% -> 0%
where the time goes in v8:
time: 241 us; the launch traced here: 240 us
  blocking collectives  81.1 us (34%)
  waiting for transfers between devices  57.5 us (24%)
  starting transfers between devices  34.4 us (14%)
  matrix products  27.8 us (12%)
  between operations  14.3 us (6%)
  local copies, waits for them, and re-layouts  10.1 us (4%)
  Pallas kernels  9.4 us (4%)
  other arithmetic  5.01 us (2%)
    all_to_all x1, blocking collectives, on_device(): lax.all_to_all(jnp.concatenate([outgoing, grad_rows], axis=1), 'expert',...  81.1 us
    all_to_all x1, waiting for transfers between devices, on_device(): lax.all_to_all(expert_out.reshape(flat_rows), 'expert', split_axis=0, con...  34.3 us
    ppermute x17, starting transfers between devices, group_sum(): got.append(lax.ppermute(value, axis, pairs))  25.6 us
    ppermute x17, waiting for transfers between devices, group_sum(): got.append(lax.ppermute(value, axis, pairs))  20.3 us
    pallas_call x1, Pallas kernels, weight_grads(): pl.pallas_call(weight_grad_kernel, grid=(width // tile,), in_specs=[pl.Bl...  9.4 us
  transfers between devices with their start and end apart: 20, of which 12 were waited for; matrix products, arithmetic and copies ran while one was open for 8% of the time, Pallas kernels for 0%

profile of v8, /device:TPU:1, one launch (start us, length us, event | category | flops | bytes accessed | tf_op | source)
XLA Modules:
  0.0 239.6 jit_solution(7952229041092502791)
XLA Ops:
  7.2 1.7 fusion.30
  11.4 1.7 convolution_convert_fusion
  14.1 81.1 %all_to_all.15 = bf16[8,96,2048]{2,1,0:T(8,128)(2,1)S(1)} all-to-all(bf16[8,96,2048]{2,1,0:T(8,128)(2,1)S(1)} %pad_maximum_fusion), channel_id=1, replica_groups=mesh['dp'=32,'expert'=8] {'expert'}, dimensions={0} | all-to-all | bytes 6291456 | tf_op jit(solution)/shard_map/all_to_all | solution.py:95
  95.2 2.0 fusion.46
  100.1 1.4 fusion.24
  101.6 3.0 %multiply_convert_fusion.2 = (bf16[8,1,48,768]{3,2,0,1:T(8,128)(2,1)}, bf16[8,1,48,768]{3,2,0,1:T(8,128)(2,1)}, bf16[8,1,48,768]{3,2,0,1:T(8,128)(2,1)}) fusion(f32[8,1,48,768]{3,2,0,1:T(8,128)S(1)} %fusion.24, f32[8,1,48,768]{3,2,0,1:T(8,128)S(1)} %fusion.21, bf16[1,2048,768]{2,1,0:T(8,128)(2,1)S(1)} %copy-done, bf16[8,96,2048]{2,1,0:T(8,128)(2,1)S(1)} %all_to_all.15), kind=kOutput, calls=%fused_computation.27 | convolution fusion | flops 1212383232 | bytes 8847360 | tf_op jit(solution)/shard_map/slnd,ldf->slnf/dot_general | solution.py:101
  104.6 9.4 %shard_map.127 = bf16[2048,2304]{1,0:T(8,128)(2,1)} custom-call(bf16[384,2048]{1,0:T(8,128)(2,1)} %bitcast.99, bf16[384,2048]{1,0:T(8,128)(2,1)} %bitcast.98, bf16[384,768]{1,0:T(8,128)(2,1)} %bitcast.102, bf16[384,768]{1,0:T(8,128)(2,1)} %bitcast.103, bf16[384,768]{1,0:T(8,128)(2,1)} %bitcast.104), custom_call_target="tpu_custom_call" | custom-call | tf_op jit(solution)/shard_map/pallas_call | solution.py:49
  114.0 4.7 %fusion.14 = bf16[8,48,2048]{2,1,0:T(8,128)(2,1)} fusion(bf16[1,2048,768]{2,1,0:T(8,128)(2,1)} %param.14, bf16[8,1,48,768]{3,2,0,1:T(8,128)(2,1)} %get-tuple-element.28), kind=kOutput, calls=%fused_computation.15 | convolution fusion | flops 1208745984 | bytes 5308416 | tf_op jit(solution)/shard_map/slnf,ldf->slnd/dot_general | solution.py:109
  118.7 4.3 %all-to-all-start.1 = ((bf16[8,48,2048]{2,1,0:T(8,128)(2,1)}), bf16[8,48,2048]{2,1,0:T(8,128)(2,1)}, u32[]{:S(2)}, u32[]{:S(2)}) async-start(bf16[8,48,2048]{2,1,0:T(8,128)(2,1)} %fusion.14), calls=%async_computation.1 | async-start | bytes 3145728 | tf_op jit(solution)/shard_map/all_to_all | solution.py:113
  123.0 3.5 %fusion.4 = f32[8,48,2048]{2,1,0:T(8,128)S(1)} fusion(bf16[1,2048,768]{2,1,0:T(8,128)(2,1)} %param.13, bf16[8,1,48,768]{3,2,0,1:T(8,128)(2,1)} %get-tuple-element.27), kind=kOutput, calls=%fused_computation.5 | convolution fusion | flops 1207959552 | bytes 6881280 | tf_op jit(solution)/shard_map/slnf,ldf->slnd/dot_general | solution.py:121
  126.6 2.6 %add_convert_fusion = bf16[8,48,2048]{2,1,0:T(8,128)(2,1)} fusion(f32[8,48,2048]{2,1,0:T(8,128)S(1)} %fusion.4, bf16[1,2048,768]{2,1,0:T(8,128)(2,1)S(1)} %copy-done, bf16[8,1,48,768]{3,2,0,1:T(8,128)(2,1)S(1)} %copy-done.4), kind=kOutput, calls=%fused_computation.13 | convolution fusion | flops 1209532416 | bytes 8454144 | tf_op jit(solution)/shard_map/slnf,ldf->slnd/dot_general | solution.py:120
  129.1 34.3 %all-to-all-done.1 = bf16[8,48,2048]{2,1,0:T(8,128)(2,1)} async-done(((bf16[8,48,2048]{2,1,0:T(8,128)(2,1)}), bf16[8,48,2048]{2,1,0:T(8,128)(2,1)}, u32[]{:S(2)}, u32[]{:S(2)}) %all-to-all-start.1) | async-done | bytes 1572896 | tf_op jit(solution)/shard_map/all_to_all | solution.py:113
  163.4 4.5 %all-to-all-start.2 = ((bf16[8,48,2048]{2,1,0:T(8,128)(2,1)}), bf16[8,48,2048]{2,1,0:T(8,128)(2,1)}, u32[]{:S(2)}, u32[]{:S(2)}) async-start(bf16[8,48,2048]{2,1,0:T(8,128)(2,1)} %add_convert_fusion), calls=%async_computation.2 | async-start | bytes 3145728 | tf_op jit(solution)/shard_map/all_to_all | solution.py:123
  167.9 2.6 %fusion.39 = f32[384,2048]{1,0:T(8,128)S(1)} fusion(bf16[384,2048]{1,0:T(8,128)(2,1)} %bitcast.20, s32[384]{0:T(512)S(1)} %bitcast.105), kind=kOutput, calls=%fused_computation.49 | convolution fusion | flops 604127232 | bytes 4720128 | tf_op jit(solution)/shard_map/dot_general | solution.py:151
  174.9 2.7 %collective-permute-start.3 = (f32[2048,8]{0,1:T(8,128)S(1)}, f32[2048,8]{0,1:T(8,128)S(1)}, u32[]{:S(2)}, u32[]{:S(2)}) collective-permute-start(f32[2048,8]{0,1:T(8,128)S(1)} %convolution_bitcast_fusion), channel_id=1, source_target_pairs={{0,32},{8,40},{16,48},{24,56},{32,0},{40,8},{48,16},{56,24},{64,96... | collective-permute-start | bytes 196616 | tf_op jit(solution)/shard_map/ppermute | solution.py:19
  178.1 2.5 %collective-permute-start.5 = (f32[2048,8]{0,1:T(8,128)S(1)}, f32[2048,8]{0,1:T(8,128)S(1)}, u32[]{:S(2)}, u32[]{:S(2)}) collective-permute-start(f32[2048,8]{0,1:T(8,128)S(1)} %convolution_bitcast_fusion), channel_id=1, source_target_pairs={{0,48},{8,56},{16,32},{24,40},{32,16},{40,24},{48,0},{56,8},{64,11... | collective-permute-start | bytes 196616 | tf_op jit(solution)/shard_map/ppermute | solution.py:19
  182.1 4.3 %collective-permute-done.3 = f32[2048,8]{0,1:T(8,128)S(1)} collective-permute-done((f32[2048,8]{0,1:T(8,128)S(1)}, f32[2048,8]{0,1:T(8,128)S(1)}, u32[]{:S(2)}, u32[]{:S(2)}) %collective-permute-start.3) | collective-permute-done | bytes 65568 | tf_op jit(solution)/shard_map/ppermute | solution.py:19
  186.4 3.2 %collective-permute-done.4 = f32[2048,8]{0,1:T(8,128)S(1)} collective-permute-done((f32[2048,8]{0,1:T(8,128)S(1)}, f32[2048,8]{0,1:T(8,128)S(1)}, u32[]{:S(2)}, u32[]{:S(2)}) %collective-permute-start.4) | collective-permute-done | bytes 65568 | tf_op jit(solution)/shard_map/ppermute | solution.py:19
  192.1 2.4 %collective-permute-start.8 = (f32[2048,8]{0,1:T(8,128)S(1)}, f32[2048,8]{0,1:T(8,128)S(1)}, u32[]{:S(2)}, u32[]{:S(2)}) collective-permute-start(f32[2048,8]{0,1:T(8,128)S(1)} %add_add_fusion.2), channel_id=1, source_target_pairs={{0,128},{8,136},{16,144},{24,152},{32,160},{40,168},{48,176},{56,1... | collective-permute-start | bytes 196616 | tf_op jit(solution)/shard_map/ppermute | solution.py:19
  195.2 3.1 %collective-permute-done.8 = f32[2048,8]{0,1:T(8,128)S(1)} collective-permute-done((f32[2048,8]{0,1:T(8,128)S(1)}, f32[2048,8]{0,1:T(8,128)S(1)}, u32[]{:S(2)}, u32[]{:S(2)}) %collective-permute-start.8) | collective-permute-done | bytes 65568 | tf_op jit(solution)/shard_map/ppermute | solution.py:19
  199.0 1.9 collective-permute-start.10
  200.9 2.1 collective-permute-start.11
  203.1 2.9 %all-to-all-done.2 = bf16[8,48,2048]{2,1,0:T(8,128)(2,1)} async-done(((bf16[8,48,2048]{2,1,0:T(8,128)(2,1)}), bf16[8,48,2048]{2,1,0:T(8,128)(2,1)}, u32[]{:S(2)}, u32[]{:S(2)}) %all-to-all-start.2) | async-done | bytes 1572896 | tf_op jit(solution)/shard_map/all_to_all | solution.py:123
  205.9 2.4 %fusion.38 = f32[384,2048]{1,0:T(8,128)S(1)} fusion(bf16[384,2048]{1,0:T(8,128)(2,1)} %bitcast.32, s32[384]{0:T(512)S(1)} %bitcast.106), kind=kOutput, calls=%fused_computation.48 | convolution fusion | flops 604127232 | bytes 4720128 | tf_op jit(solution)/shard_map/dot_general | solution.py:154
  208.5 2.5 %collective-permute-start.13 = (f32[2048,8]{0,1:T(8,128)S(1)}, f32[2048,8]{0,1:T(8,128)S(1)}, u32[]{:S(2)}, u32[]{:S(2)}) collective-permute-start(f32[2048,8]{0,1:T(8,128)S(1)} %add_add_fusion.1), channel_id=1, source_target_pairs={{0,4},{1,5},{2,6},{3,7},{4,0},{5,1},{6,2},{7,3},{8,12},{9,13},{10,... | collective-permute-start | bytes 196616 | tf_op jit(solution)/shard_map/ppermute | solution.py:19
  211.0 3.3 %collective-permute-start.14 = (f32[2048,8]{0,1:T(8,128)S(1)}, f32[2048,8]{0,1:T(8,128)S(1)}, u32[]{:S(2)}, u32[]{:S(2)}) collective-permute-start(f32[2048,8]{0,1:T(8,128)S(1)} %add_add_fusion.1), channel_id=1, source_target_pairs={{0,5},{1,4},{2,7},{3,6},{4,1},{5,0},{6,3},{7,2},{8,13},{9,12},{10,... | collective-permute-start | bytes 196616 | tf_op jit(solution)/shard_map/ppermute | solution.py:19
  214.5 2.1 collective-permute-start.16
  216.6 1.8 fusion.17
  218.8 3.4 %collective-permute-done.15 = f32[2048,8]{0,1:T(8,128)S(1)} collective-permute-done((f32[2048,8]{0,1:T(8,128)S(1)}, f32[2048,8]{0,1:T(8,128)S(1)}, u32[]{:S(2)}, u32[]{:S(2)}) %collective-permute-start.15) | collective-permute-done | bytes 65568 | tf_op jit(solution)/shard_map/ppermute | solution.py:19
  222.2 3.4 %collective-permute-done.16 = f32[2048,8]{0,1:T(8,128)S(1)} collective-permute-done((f32[2048,8]{0,1:T(8,128)S(1)}, f32[2048,8]{0,1:T(8,128)S(1)}, u32[]{:S(2)}, u32[]{:S(2)}) %collective-permute-start.16) | collective-permute-done | bytes 65568 | tf_op jit(solution)/shard_map/ppermute | solution.py:19
  226.2 2.2 reshape.176
  228.4 2.3 slice_bitcast_fusion
  (62 shorter events, 20.0 us)
Async XLA Ops:
  7.2 94.4 %copy-start = (bf16[1,2048,768]{2,1,0:T(8,128)(2,1)S(1)}, bf16[1,2048,768]{2,1,0:T(8,128)(2,1)}, u32[]{:S(2)}) copy-start(bf16[1,2048,768]{2,1,0:T(8,128)(2,1)} %param.12) | copy-start | bytes 9437188
  7.2 219.0 %reduce-scatter.2.cloned.1.call-start = ((), (), s32[]{:S(2)}) async-start(), calls=%async_computation.4 | async-start | bytes 9732096 | tf_op jit(solution)/shard_map/reduce_scatter | solution.py:144
  7.2 5.8 %copy-start.2 = (bf16[128,2048]{1,0:T(8,128)(2,1)S(1)}, bf16[128,2048]{1,0:T(8,128)(2,1)}, u32[]{:S(2)}) copy-start(bf16[128,2048]{1,0:T(8,128)(2,1)} %param.15) | copy-start | bytes 1572868
  95.2 3.0 %copy-start.8 = (bf16[1,2048,768]{2,1,0:T(8,128)(2,1)S(1)}, bf16[1,2048,768]{2,1,0:T(8,128)(2,1)}, u32[]{:S(2)}) copy-start(bf16[1,2048,768]{2,1,0:T(8,128)(2,1)} %param.13) | copy-start | bytes 9437188
  98.2 1.9 copy-start.7
  118.7 44.7 %all-to-all-start.1 = ((bf16[8,48,2048]{2,1,0:T(8,128)(2,1)}), bf16[8,48,2048]{2,1,0:T(8,128)(2,1)}, u32[]{:S(2)}, u32[]{:S(2)}) async-start(bf16[8,48,2048]{2,1,0:T(8,128)(2,1)} %fusion.14), calls=%async_computation.1 | async-start | bytes 3145728 | tf_op jit(solution)/shard_map/all_to_all | solution.py:113
  123.0 3.6 %copy-start.4 = (bf16[8,1,48,768]{3,2,0,1:T(8,128)(2,1)S(1)}, bf16[8,1,48,768]{3,2,0,1:T(8,128)(2,1)}, u32[]{:S(2)}) copy-start(bf16[8,1,48,768]{3,2,0,1:T(8,128)(2,1)} %get-tuple-element.26) | copy-start | bytes 1769476
  163.4 42.5 %all-to-all-start.2 = ((bf16[8,48,2048]{2,1,0:T(8,128)(2,1)}), bf16[8,48,2048]{2,1,0:T(8,128)(2,1)}, u32[]{:S(2)}, u32[]{:S(2)}) async-start(bf16[8,48,2048]{2,1,0:T(8,128)(2,1)} %add_convert_fusion), calls=%async_computation.2 | async-start | bytes 3145728 | tf_op jit(solution)/shard_map/all_to_all | solution.py:123
  167.9 2.7 %copy-start.3 = (bf16[128,2048]{1,0:T(8,128)(2,1)S(1)}, bf16[128,2048]{1,0:T(8,128)(2,1)}, u32[]{:S(2)}) copy-start(bf16[128,2048]{1,0:T(8,128)(2,1)} %param.15) | copy-start | bytes 1572868
  170.5 1.5 copy-start.6
  170.5 1.5 copy-start.1
  172.3 5.8 %collective-permute-start = (f32[2048,8]{0,1:T(8,128)S(1)}, f32[2048,8]{0,1:T(8,128)S(1)}, u32[]{:S(2)}, u32[]{:S(2)}) collective-permute-start(f32[2048,8]{0,1:T(8,128)S(1)} %convolution_bitcast_fusion), channel_id=1, source_target_pairs={{0,8},{8,0},{16,24},{24,16},{32,40},{40,32},{48,56},{56,48},{64,72... | collective-permute-start | bytes 196616 | tf_op jit(solution)/shard_map/ppermute | solution.py:19
  173.1 7.5 %collective-permute-start.1 = (f32[2048,8]{0,1:T(8,128)S(1)}, f32[2048,8]{0,1:T(8,128)S(1)}, u32[]{:S(2)}, u32[]{:S(2)}) collective-permute-start(f32[2048,8]{0,1:T(8,128)S(1)} %convolution_bitcast_fusion), channel_id=1, source_target_pairs={{0,16},{8,24},{16,0},{24,8},{32,48},{40,56},{48,32},{56,40},{64,80... | collective-permute-start | bytes 196616 | tf_op jit(solution)/shard_map/ppermute | solution.py:19
  174.2 7.9 %collective-permute-start.2 = (f32[2048,8]{0,1:T(8,128)S(1)}, f32[2048,8]{0,1:T(8,128)S(1)}, u32[]{:S(2)}, u32[]{:S(2)}) collective-permute-start(f32[2048,8]{0,1:T(8,128)S(1)} %convolution_bitcast_fusion), channel_id=1, source_target_pairs={{0,24},{8,16},{16,8},{24,0},{32,56},{40,48},{48,40},{56,32},{64,88... | collective-permute-start | bytes 196616 | tf_op jit(solution)/shard_map/ppermute | solution.py:19
  174.9 11.6 %collective-permute-start.3 = (f32[2048,8]{0,1:T(8,128)S(1)}, f32[2048,8]{0,1:T(8,128)S(1)}, u32[]{:S(2)}, u32[]{:S(2)}) collective-permute-start(f32[2048,8]{0,1:T(8,128)S(1)} %convolution_bitcast_fusion), channel_id=1, source_target_pairs={{0,32},{8,40},{16,48},{24,56},{32,0},{40,8},{48,16},{56,24},{64,96... | collective-permute-start | bytes 196616 | tf_op jit(solution)/shard_map/ppermute | solution.py:19
  177.5 12.1 %collective-permute-start.4 = (f32[2048,8]{0,1:T(8,128)S(1)}, f32[2048,8]{0,1:T(8,128)S(1)}, u32[]{:S(2)}, u32[]{:S(2)}) collective-permute-start(f32[2048,8]{0,1:T(8,128)S(1)} %convolution_bitcast_fusion), channel_id=1, source_target_pairs={{0,40},{8,32},{16,56},{24,48},{32,8},{40,0},{48,24},{56,16},{64,10... | collective-permute-start | bytes 196616 | tf_op jit(solution)/shard_map/ppermute | solution.py:19
  178.1 11.5 %collective-permute-start.5 = (f32[2048,8]{0,1:T(8,128)S(1)}, f32[2048,8]{0,1:T(8,128)S(1)}, u32[]{:S(2)}, u32[]{:S(2)}) collective-permute-start(f32[2048,8]{0,1:T(8,128)S(1)} %convolution_bitcast_fusion), channel_id=1, source_target_pairs={{0,48},{8,56},{16,32},{24,40},{32,16},{40,24},{48,0},{56,8},{64,11... | collective-permute-start | bytes 196616 | tf_op jit(solution)/shard_map/ppermute | solution.py:19
  180.6 10.3 %collective-permute-start.6 = (f32[2048,8]{0,1:T(8,128)S(1)}, f32[2048,8]{0,1:T(8,128)S(1)}, u32[]{:S(2)}, u32[]{:S(2)}) collective-permute-start(f32[2048,8]{0,1:T(8,128)S(1)} %convolution_bitcast_fusion), channel_id=1, source_target_pairs={{0,56},{8,48},{16,40},{24,32},{32,24},{40,16},{48,8},{56,0},{64,12... | collective-permute-start | bytes 196616 | tf_op jit(solution)/shard_map/ppermute | solution.py:19
  190.9 25.7 %copy-start.5 = (f32[2048,8]{0,1:T(8,128)S(1)}, f32[2048,8]{0,1:T(8,128)}, u32[]{:S(2)}) copy-start(f32[2048,8]{0,1:T(8,128)} %param.11) | copy-start | bytes 196612
  190.9 4.2 %collective-permute-start.7 = (f32[2048,8]{0,1:T(8,128)S(1)}, f32[2048,8]{0,1:T(8,128)S(1)}, u32[]{:S(2)}, u32[]{:S(2)}) collective-permute-start(f32[2048,8]{0,1:T(8,128)S(1)} %add_add_fusion.2), channel_id=1, source_target_pairs={{0,64},{8,72},{16,80},{24,88},{32,96},{40,104},{48,112},{56,120},{... | collective-permute-start | bytes 196616 | tf_op jit(solution)/shard_map/ppermute | solution.py:19
  192.1 6.1 %collective-permute-start.8 = (f32[2048,8]{0,1:T(8,128)S(1)}, f32[2048,8]{0,1:T(8,128)S(1)}, u32[]{:S(2)}, u32[]{:S(2)}) collective-permute-start(f32[2048,8]{0,1:T(8,128)S(1)} %add_add_fusion.2), channel_id=1, source_target_pairs={{0,128},{8,136},{16,144},{24,152},{32,160},{40,168},{48,176},{56,1... | collective-permute-start | bytes 196616 | tf_op jit(solution)/shard_map/ppermute | solution.py:19
  194.6 4.5 %collective-permute-start.9 = (f32[2048,8]{0,1:T(8,128)S(1)}, f32[2048,8]{0,1:T(8,128)S(1)}, u32[]{:S(2)}, u32[]{:S(2)}) collective-permute-start(f32[2048,8]{0,1:T(8,128)S(1)} %add_add_fusion.2), channel_id=1, source_target_pairs={{0,192},{8,200},{16,208},{24,216},{32,224},{40,232},{48,240},{56,2... | collective-permute-start | bytes 196616 | tf_op jit(solution)/shard_map/ppermute | solution.py:19
  199.0 15.3 %collective-permute-start.10 = (f32[2048,8]{0,1:T(8,128)S(1)}, f32[2048,8]{0,1:T(8,128)S(1)}, u32[]{:S(2)}, u32[]{:S(2)}) collective-permute-start(f32[2048,8]{0,1:T(8,128)S(1)} %add_add_fusion.1), channel_id=1, source_target_pairs={{0,1},{1,0},{2,3},{3,2},{4,5},{5,4},{6,7},{7,6},{8,9},{9,8},{10,11... | collective-permute-start | bytes 196616 | tf_op jit(solution)/shard_map/ppermute | solution.py:19
  200.9 13.6 %collective-permute-start.11 = (f32[2048,8]{0,1:T(8,128)S(1)}, f32[2048,8]{0,1:T(8,128)S(1)}, u32[]{:S(2)}, u32[]{:S(2)}) collective-permute-start(f32[2048,8]{0,1:T(8,128)S(1)} %add_add_fusion.1), channel_id=1, source_target_pairs={{0,2},{1,3},{2,0},{3,1},{4,6},{5,7},{6,4},{7,5},{8,10},{9,11},{10,... | collective-permute-start | bytes 196616 | tf_op jit(solution)/shard_map/ppermute | solution.py:19
  208.4 10.1 %collective-permute-start.12 = (f32[2048,8]{0,1:T(8,128)S(1)}, f32[2048,8]{0,1:T(8,128)S(1)}, u32[]{:S(2)}, u32[]{:S(2)}) collective-permute-start(f32[2048,8]{0,1:T(8,128)S(1)} %add_add_fusion.1), channel_id=1, source_target_pairs={{0,3},{1,2},{2,1},{3,0},{4,7},{5,6},{6,5},{7,4},{8,11},{9,10},{10,... | collective-permute-start | bytes 196616 | tf_op jit(solution)/shard_map/ppermute | solution.py:19
  208.5 10.0 %collective-permute-start.13 = (f32[2048,8]{0,1:T(8,128)S(1)}, f32[2048,8]{0,1:T(8,128)S(1)}, u32[]{:S(2)}, u32[]{:S(2)}) collective-permute-start(f32[2048,8]{0,1:T(8,128)S(1)} %add_add_fusion.1), channel_id=1, source_target_pairs={{0,4},{1,5},{2,6},{3,7},{4,0},{5,1},{6,2},{7,3},{8,12},{9,13},{10,... | collective-permute-start | bytes 196616 | tf_op jit(solution)/shard_map/ppermute | solution.py:19
  211.0 7.8 %collective-permute-start.14 = (f32[2048,8]{0,1:T(8,128)S(1)}, f32[2048,8]{0,1:T(8,128)S(1)}, u32[]{:S(2)}, u32[]{:S(2)}) collective-permute-start(f32[2048,8]{0,1:T(8,128)S(1)} %add_add_fusion.1), channel_id=1, source_target_pairs={{0,5},{1,4},{2,7},{3,6},{4,1},{5,0},{6,3},{7,2},{8,13},{9,12},{10,... | collective-permute-start | bytes 196616 | tf_op jit(solution)/shard_map/ppermute | solution.py:19
  214.3 7.9 %collective-permute-start.15 = (f32[2048,8]{0,1:T(8,128)S(1)}, f32[2048,8]{0,1:T(8,128)S(1)}, u32[]{:S(2)}, u32[]{:S(2)}) collective-permute-start(f32[2048,8]{0,1:T(8,128)S(1)} %add_add_fusion.1), channel_id=1, source_target_pairs={{0,6},{1,7},{2,4},{3,5},{4,2},{5,3},{6,0},{7,1},{8,14},{9,15},{10,... | collective-permute-start | bytes 196616 | tf_op jit(solution)/shard_map/ppermute | solution.py:19
  214.5 11.0 %collective-permute-start.16 = (f32[2048,8]{0,1:T(8,128)S(1)}, f32[2048,8]{0,1:T(8,128)S(1)}, u32[]{:S(2)}, u32[]{:S(2)}) collective-permute-start(f32[2048,8]{0,1:T(8,128)S(1)} %add_add_fusion.1), channel_id=1, source_target_pairs={{0,7},{1,6},{2,5},{3,4},{4,3},{5,2},{6,1},{7,0},{8,15},{9,14},{10,... | collective-permute-start | bytes 196616 | tf_op jit(solution)/shard_map/ppermute | solution.py:19
Sparse Core Ops, SparseCore 0:
  114.1 105.1 reduce-scatter.1

commit v9 on v5

--- a/solution.py
+++ b/solution.py
@@ -92,12 +92,9 @@
     grad_rows = (gate_of_slot[:, None] * picked_grad).astype(jnp.bfloat16)
     outgoing = outgoing.reshape(expert_count, slot_count, width)
     grad_rows = grad_rows.reshape(expert_count, slot_count, width)
-    both_in = lax.all_to_all(
-        jnp.concatenate([outgoing, grad_rows], axis=1), "expert", split_axis=0, concat_axis=0, tiled=True
-    )
     block_shape = (sender_count, local_count, slot_count, width)
-    row_block = both_in[:, :slot_count].reshape(block_shape)
-    arrived = both_in[:, slot_count:].reshape(block_shape)
+    row_block = lax.all_to_all(outgoing, "expert", split_axis=0, concat_axis=0, tiled=True).reshape(block_shape)
+    arrived = lax.all_to_all(grad_rows, "expert", split_axis=0, concat_axis=0, tiled=True).reshape(block_shape)
     hidden_gate = jnp.einsum(
         "slnd,ldf->slnf", row_block, w_gate, preferred_element_type=jnp.float32
     )

time: 241 us -> 251 us (1.041)
  blocking collectives: 81.3 us -> 0 us
  waiting for transfers between devices: 56.9 us -> 128 us
  starting transfers between devices: 34.6 us -> 48 us
  matrix products: 27.5 us -> 38.3 us
  local copies, waits for them, and re-layouts: 10 us -> 7.34 us
    all_to_all x1 -> x0, blocking collectives: 81.3 us -> none  [on_device(): lax.all_to_all(jnp.concatenate([outgoing, grad_rows], axis=1), 'expert',...]
    all_to_all x0 -> x2, waiting for transfers between devices: none -> 71.1 us  [the longest x1 37.7 us: on_device(): lax.all_to_all(grad_rows, 'expert', split_axis=0, concat_axis=0, tiled=True)]
    all_to_all x0 -> x2, starting transfers between devices: none -> 13.3 us  [the longest x1 9 us: on_device(): lax.all_to_all(grad_rows, 'expert', split_axis=0, concat_axis=0, tiled=True)]
    dot_general x1, matrix products: 1.42 us -> 4.77 us  [on_device(): jnp.einsum('slnd,ldf->slnf', arrived, w_down, preferred_element_type=jnp....]
  transfers between devices with their start and end apart: 20 -> 22, of which waited for: 9 -> 12; matrix products, arithmetic and copies ran while one was open for 8% -> 11% of each run, Pallas kernels for 0% -> 0%
where the time goes in v9:
time: 251 us
  waiting for transfers between devices  128 us (51%)
  starting transfers between devices  48 us (19%)
  matrix products  38.3 us (15%)
  between operations  14.2 us (6%)
  Pallas kernels  9.28 us (4%)
  local copies, waits for them, and re-layouts  7.34 us (3%)
  other arithmetic  5.9 us (2%)
    all_to_all x1, waiting for transfers between devices, on_device(): lax.all_to_all(grad_rows, 'expert', split_axis=0, concat_axis=0, tiled=True)  37.7 us
    all_to_all x1, waiting for transfers between devices, on_device(): lax.all_to_all(expert_out.reshape(flat_rows), 'expert', split_axis=0, con...  34.2 us
    all_to_all x1, waiting for transfers between devices, on_device(): lax.all_to_all(outgoing, 'expert', split_axis=0, concat_axis=0, tiled=True)  33.4 us
    ppermute x17, starting transfers between devices, group_sum(): got.append(lax.ppermute(value, axis, pairs))  25.9 us
    ppermute x17, waiting for transfers between devices, group_sum(): got.append(lax.ppermute(value, axis, pairs))  20.1 us
    pallas_call x1, Pallas kernels, weight_grads(): pl.pallas_call(weight_grad_kernel, grid=(width // tile,), in_specs=[pl.Bl...  9.28 us
    all_to_all x1, starting transfers between devices, on_device(): lax.all_to_all(grad_rows, 'expert', split_axis=0, concat_axis=0, tiled=True)  9 us
  transfers between devices with their start and end apart: 22, of which 12 were waited for; matrix products, arithmetic and copies ran while one was open for 11% of the time, Pallas kernels for 0%

profile of v9, /device:TPU:1, one launch (start us, length us, event | category | flops | bytes accessed | tf_op | source)
XLA Modules:
  0.0 250.6 jit_solution(15201495213753347195)
XLA Ops:
  11.4 2.8 %multiply_convert_fusion = bf16[384,2048]{1,0:T(8,128)(2,1)} fusion(pred[128,384]{1,0:T(8,128)(4,1)S(1)} %fusion.37, bf16[128,2048]{1,0:T(8,128)(2,1)} %param.15, f32[384]{0:T(512)S(1)} %select_reduce_fusion), kind=kOutput, calls=%fused_computation.13 | convolution fusion | flops 202899456 | bytes 2147840 | tf_op jit(solution)/shard_map/dot_general | solution.py:91
  14.3 9.0 %all-to-all-start.2 = ((bf16[8,48,2048]{2,1,0:T(8,128)(2,1)}), bf16[8,48,2048]{2,1,0:T(8,128)(2,1)}, u32[]{:S(2)}, u32[]{:S(2)}) async-start(bf16[8,48,2048]{2,1,0:T(8,128)(2,1)} %bitcast.102), calls=%async_computation.2 | async-start | bytes 3145728 | tf_op jit(solution)/shard_map/all_to_all | solution.py:97
  23.3 2.8 %convolution_convert_fusion = bf16[384,2048]{1,0:T(8,128)(2,1)} fusion(pred[128,384]{1,0:T(8,128)(4,1)S(1)} %fusion.37, bf16[128,2048]{1,0:T(8,128)(2,1)} %param.8), kind=kOutput, calls=%fused_computation.15 | convolution fusion | flops 202113024 | bytes 2146304 | tf_op jit(solution)/shard_map/dot_general | solution.py:90
  26.1 37.7 %all-to-all-done.2 = bf16[8,48,2048]{2,1,0:T(8,128)(2,1)} async-done(((bf16[8,48,2048]{2,1,0:T(8,128)(2,1)}), bf16[8,48,2048]{2,1,0:T(8,128)(2,1)}, u32[]{:S(2)}, u32[]{:S(2)}) %all-to-all-start.2) | async-done | bytes 1572896 | tf_op jit(solution)/shard_map/all_to_all | solution.py:97
  63.8 4.3 %all-to-all-start = ((bf16[8,48,2048]{2,1,0:T(8,128)(2,1)}), bf16[8,48,2048]{2,1,0:T(8,128)(2,1)}, u32[]{:S(2)}, u32[]{:S(2)}) async-start(bf16[8,48,2048]{2,1,0:T(8,128)(2,1)} %bitcast.101), calls=%async_computation | async-start | bytes 3145728 | tf_op jit(solution)/shard_map/all_to_all | solution.py:96
  68.1 4.8 %fusion.24 = f32[8,1,48,768]{3,2,0,1:T(8,128)} fusion(bf16[8,48,2048]{2,1,0:T(8,128)(2,1)} %all-to-all-done.2, bf16[1,2048,768]{2,1,0:T(8,128)(2,1)} %param.14), kind=kOutput, calls=%fused_computation.24 | convolution fusion | flops 1207959552 | bytes 5898240 | tf_op jit(solution)/shard_map/slnd,ldf->slnf/dot_general | solution.py:113
  72.9 33.4 %all-to-all-done = bf16[8,48,2048]{2,1,0:T(8,128)(2,1)} async-done(((bf16[8,48,2048]{2,1,0:T(8,128)(2,1)}), bf16[8,48,2048]{2,1,0:T(8,128)(2,1)}, u32[]{:S(2)}, u32[]{:S(2)}) %all-to-all-start) | async-done | bytes 1572896 | tf_op jit(solution)/shard_map/all_to_all | solution.py:96
  106.3 3.8 %fusion.21 = f32[8,1,48,768]{3,2,0,1:T(8,128)S(1)} fusion(bf16[8,48,2048]{2,1,0:T(8,128)(2,1)} %all-to-all-done, bf16[1,2048,768]{2,1,0:T(8,128)(2,1)} %param.13), kind=kOutput, calls=%fused_computation.23 | convolution fusion | flops 1207959552 | bytes 5898240 | tf_op jit(solution)/shard_map/slnd,ldf->slnf/dot_general | solution.py:101
  110.2 4.0 %multiply_convert_fusion.2 = (bf16[8,1,48,768]{3,2,0,1:T(8,128)(2,1)S(1)}, bf16[8,1,48,768]{3,2,0,1:T(8,128)(2,1)S(1)}, bf16[8,1,48,768]{3,2,0,1:T(8,128)(2,1)}) fusion(f32[8,1,48,768]{3,2,0,1:T(8,128)S(1)} %copy-done.8, f32[8,1,48,768]{3,2,0,1:T(8,128)S(1)} %fusion.21, bf16[8,48,2048]{2,1,0:T(8,128)(2,1)} %all-to-all-done, ...), kind=kOutput, calls=%fused_computation.27 | convolution fusion | flops 1212383232 | bytes 8847360 | tf_op jit(solution)/shard_map/slnd,ldf->slnf/dot_general | solution.py:98
  116.2 9.3 %shard_map.127 = bf16[2048,2304]{1,0:T(8,128)(2,1)} custom-call(bf16[384,2048]{1,0:T(8,128)(2,1)} %bitcast.37.rows_ref, bf16[384,2048]{1,0:T(8,128)(2,1)} %bitcast.38.grads_ref, bf16[384,1536]{1,0:T(8,128)(2,1)} %pad_maximum_fusion.deltas_ref, bf16[384,768]{1,0:T(8,128)(2,1)} %bitcast.103), custom_call_target="tpu_custom_call" | custom-call | tf_op jit(solution)/shard_map/pallas_call | solution.py:50
  125.5 4.7 %fusion.14 = bf16[8,48,2048]{2,1,0:T(8,128)(2,1)} fusion(bf16[1,2048,768]{2,1,0:T(8,128)(2,1)} %param.14, bf16[8,1,48,768]{3,2,0,1:T(8,128)(2,1)} %get-tuple-element.26), kind=kOutput, calls=%fused_computation.14 | convolution fusion | flops 1208745984 | bytes 5308416 | tf_op jit(solution)/shard_map/slnf,ldf->slnd/dot_general | solution.py:106
  130.2 4.3 %all-to-all-start.1 = ((bf16[8,48,2048]{2,1,0:T(8,128)(2,1)}), bf16[8,48,2048]{2,1,0:T(8,128)(2,1)}, u32[]{:S(2)}, u32[]{:S(2)}) async-start(bf16[8,48,2048]{2,1,0:T(8,128)(2,1)} %fusion.14), calls=%async_computation.1 | async-start | bytes 3145728 | tf_op jit(solution)/shard_map/all_to_all | solution.py:110
  134.5 3.6 %fusion.4 = f32[8,48,2048]{2,1,0:T(8,128)S(1)} fusion(bf16[1,2048,768]{2,1,0:T(8,128)(2,1)} %param.13, bf16[8,1,48,768]{3,2,0,1:T(8,128)(2,1)} %copy-done.5), kind=kOutput, calls=%fused_computation.4 | convolution fusion | flops 1207959552 | bytes 6881280 | tf_op jit(solution)/shard_map/slnf,ldf->slnd/dot_general | solution.py:118
  138.1 2.6 %add_convert_fusion = bf16[8,48,2048]{2,1,0:T(8,128)(2,1)} fusion(f32[8,48,2048]{2,1,0:T(8,128)S(1)} %fusion.4, bf16[1,2048,768]{2,1,0:T(8,128)(2,1)S(1)} %copy-done, bf16[8,1,48,768]{3,2,0,1:T(8,128)(2,1)S(1)} %copy-done.4), kind=kOutput, calls=%fused_computation.12 | convolution fusion | flops 1209532416 | bytes 8454144 | tf_op jit(solution)/shard_map/slnf,ldf->slnd/dot_general | solution.py:117
  140.7 34.2 %all-to-all-done.1 = bf16[8,48,2048]{2,1,0:T(8,128)(2,1)} async-done(((bf16[8,48,2048]{2,1,0:T(8,128)(2,1)}), bf16[8,48,2048]{2,1,0:T(8,128)(2,1)}, u32[]{:S(2)}, u32[]{:S(2)}) %all-to-all-start.1) | async-done | bytes 1572896 | tf_op jit(solution)/shard_map/all_to_all | solution.py:110
  174.9 4.5 %all-to-all-start.3 = ((bf16[8,48,2048]{2,1,0:T(8,128)(2,1)}), bf16[8,48,2048]{2,1,0:T(8,128)(2,1)}, u32[]{:S(2)}, u32[]{:S(2)}) async-start(bf16[8,48,2048]{2,1,0:T(8,128)(2,1)} %add_convert_fusion), calls=%async_computation.3 | async-start | bytes 3145728 | tf_op jit(solution)/shard_map/all_to_all | solution.py:120
  179.4 2.9 %fusion.39 = f32[384,2048]{1,0:T(8,128)S(1)} fusion(bf16[384,2048]{1,0:T(8,128)(2,1)} %bitcast.19, s32[384]{0:T(512)S(1)} %bitcast.106), kind=kOutput, calls=%fused_computation.49 | convolution fusion | flops 604127232 | bytes 4720128 | tf_op jit(solution)/shard_map/dot_general | solution.py:148
  184.1 3.0 %collective-permute-start.6 = (f32[2048,8]{0,1:T(8,128)S(1)}, f32[2048,8]{0,1:T(8,128)S(1)}, u32[]{:S(2)}, u32[]{:S(2)}) collective-permute-start(f32[2048,8]{0,1:T(8,128)S(1)} %convolution_bitcast_fusion), channel_id=1, source_target_pairs={{0,56},{8,48},{16,40},{24,32},{32,24},{40,16},{48,8},{56,0},{64,12... | collective-permute-start | bytes 196616 | tf_op jit(solution)/shard_map/ppermute | solution.py:19
  192.3 4.7 %collective-permute-done.5 = f32[2048,8]{0,1:T(8,128)S(1)} collective-permute-done((f32[2048,8]{0,1:T(8,128)S(1)}, f32[2048,8]{0,1:T(8,128)S(1)}, u32[]{:S(2)}, u32[]{:S(2)}) %collective-permute-start.5) | collective-permute-done | bytes 65568 | tf_op jit(solution)/shard_map/ppermute | solution.py:19
  197.4 2.9 %collective-permute-done.2 = f32[2048,8]{0,1:T(8,128)S(1)} collective-permute-done((f32[2048,8]{0,1:T(8,128)S(1)}, f32[2048,8]{0,1:T(8,128)S(1)}, u32[]{:S(2)}, u32[]{:S(2)}) %collective-permute-start.2) | collective-permute-done | bytes 65568 | tf_op jit(solution)/shard_map/ppermute | solution.py:19
  200.4 2.4 collective-permute-done.1
  202.8 2.9 %collective-permute-start.9 = (f32[2048,8]{0,1:T(8,128)S(1)}, f32[2048,8]{0,1:T(8,128)S(1)}, u32[]{:S(2)}, u32[]{:S(2)}) collective-permute-start(f32[2048,8]{0,1:T(8,128)S(1)} %add_add_fusion.2), channel_id=1, source_target_pairs={{0,192},{8,200},{16,208},{24,216},{32,224},{40,232},{48,240},{56,2... | collective-permute-start | bytes 196616 | tf_op jit(solution)/shard_map/ppermute | solution.py:19
  207.8 2.5 collective-permute-done.8
  210.3 3.1 %collective-permute-start.16 = (f32[2048,8]{0,1:T(8,128)S(1)}, f32[2048,8]{0,1:T(8,128)S(1)}, u32[]{:S(2)}, u32[]{:S(2)}) collective-permute-start(f32[2048,8]{0,1:T(8,128)S(1)} %add_add_fusion.1), channel_id=1, source_target_pairs={{0,7},{1,6},{2,5},{3,4},{4,3},{5,2},{6,1},{7,0},{8,15},{9,14},{10,... | collective-permute-start | bytes 196616 | tf_op jit(solution)/shard_map/ppermute | solution.py:19
  213.4 1.9 collective-permute-start.15
  215.3 2.1 all-to-all-done.3
  217.4 2.5 fusion.38
  221.3 4.4 %collective-permute-start.13 = (f32[2048,8]{0,1:T(8,128)S(1)}, f32[2048,8]{0,1:T(8,128)S(1)}, u32[]{:S(2)}, u32[]{:S(2)}) collective-permute-start(f32[2048,8]{0,1:T(8,128)S(1)} %add_add_fusion.1), channel_id=1, source_target_pairs={{0,4},{1,5},{2,6},{3,7},{4,0},{5,1},{6,2},{7,3},{8,12},{9,13},{10,... | collective-permute-start | bytes 196616 | tf_op jit(solution)/shard_map/ppermute | solution.py:19
  226.8 2.5 collective-permute-start.10
  231.2 5.4 %collective-permute-done.11 = f32[2048,8]{0,1:T(8,128)S(1)} collective-permute-done((f32[2048,8]{0,1:T(8,128)S(1)}, f32[2048,8]{0,1:T(8,128)S(1)}, u32[]{:S(2)}, u32[]{:S(2)}) %collective-permute-start.11) | collective-permute-done | bytes 65568 | tf_op jit(solution)/shard_map/ppermute | solution.py:19
  237.3 2.2 reshape.176
  239.4 2.2 slice_bitcast_fusion
  (64 shorter events, 23.2 us)
Async XLA Ops:
  7.2 103.0 %copy-start = (bf16[1,2048,768]{2,1,0:T(8,128)(2,1)S(1)}, bf16[1,2048,768]{2,1,0:T(8,128)(2,1)}, u32[]{:S(2)}) copy-start(bf16[1,2048,768]{2,1,0:T(8,128)(2,1)} %param.12) | copy-start | bytes 9437188
  14.3 49.5 %all-to-all-start.2 = ((bf16[8,48,2048]{2,1,0:T(8,128)(2,1)}), bf16[8,48,2048]{2,1,0:T(8,128)(2,1)}, u32[]{:S(2)}, u32[]{:S(2)}) async-start(bf16[8,48,2048]{2,1,0:T(8,128)(2,1)} %bitcast.102), calls=%async_computation.2 | async-start | bytes 3145728 | tf_op jit(solution)/shard_map/all_to_all | solution.py:97
  63.8 42.5 %all-to-all-start = ((bf16[8,48,2048]{2,1,0:T(8,128)(2,1)}), bf16[8,48,2048]{2,1,0:T(8,128)(2,1)}, u32[]{:S(2)}, u32[]{:S(2)}) async-start(bf16[8,48,2048]{2,1,0:T(8,128)(2,1)} %bitcast.101), calls=%async_computation | async-start | bytes 3145728 | tf_op jit(solution)/shard_map/all_to_all | solution.py:96
  68.1 169.2 %reduce-scatter.2.cloned.1.call-start = ((), (), s32[]{:S(2)}) async-start(), calls=%async_computation.5 | async-start | bytes 9732096 | tf_op jit(solution)/shard_map/reduce_scatter | solution.py:141
  106.3 3.9 %copy-start.8 = (f32[8,1,48,768]{3,2,0,1:T(8,128)S(1)}, f32[8,1,48,768]{3,2,0,1:T(8,128)}, u32[]{:S(2)}) copy-start(f32[8,1,48,768]{3,2,0,1:T(8,128)} %fusion.24) | copy-start | bytes 3538948
  114.2 0.8 copy-start.3
  114.2 2.0 copy-start.5
  130.2 44.7 %all-to-all-start.1 = ((bf16[8,48,2048]{2,1,0:T(8,128)(2,1)}), bf16[8,48,2048]{2,1,0:T(8,128)(2,1)}, u32[]{:S(2)}, u32[]{:S(2)}) async-start(bf16[8,48,2048]{2,1,0:T(8,128)(2,1)} %fusion.14), calls=%async_computation.1 | async-start | bytes 3145728 | tf_op jit(solution)/shard_map/all_to_all | solution.py:110
  134.5 3.6 %copy-start.4 = (bf16[8,1,48,768]{3,2,0,1:T(8,128)(2,1)S(1)}, bf16[8,1,48,768]{3,2,0,1:T(8,128)(2,1)}, u32[]{:S(2)}) copy-start(bf16[8,1,48,768]{3,2,0,1:T(8,128)(2,1)} %copy-done.3) | copy-start | bytes 1769476
  174.9 42.5 %all-to-all-start.3 = ((bf16[8,48,2048]{2,1,0:T(8,128)(2,1)}), bf16[8,48,2048]{2,1,0:T(8,128)(2,1)}, u32[]{:S(2)}, u32[]{:S(2)}) async-start(bf16[8,48,2048]{2,1,0:T(8,128)(2,1)} %add_convert_fusion), calls=%async_computation.3 | async-start | bytes 3145728 | tf_op jit(solution)/shard_map/all_to_all | solution.py:120
  179.4 2.9 %copy-start.2 = (bf16[128,2048]{1,0:T(8,128)(2,1)S(1)}, bf16[128,2048]{1,0:T(8,128)(2,1)}, u32[]{:S(2)}) copy-start(bf16[128,2048]{1,0:T(8,128)(2,1)} %param.15) | copy-start | bytes 1572868
  182.3 1.5 copy-start.7
  182.3 1.5 copy-start.1
  184.1 7.5 %collective-permute-start.6 = (f32[2048,8]{0,1:T(8,128)S(1)}, f32[2048,8]{0,1:T(8,128)S(1)}, u32[]{:S(2)}, u32[]{:S(2)}) collective-permute-start(f32[2048,8]{0,1:T(8,128)S(1)} %convolution_bitcast_fusion), channel_id=1, source_target_pairs={{0,56},{8,48},{16,40},{24,32},{32,24},{40,16},{48,8},{56,0},{64,12... | collective-permute-start | bytes 196616 | tf_op jit(solution)/shard_map/ppermute | solution.py:19
  187.1 9.9 %collective-permute-start.5 = (f32[2048,8]{0,1:T(8,128)S(1)}, f32[2048,8]{0,1:T(8,128)S(1)}, u32[]{:S(2)}, u32[]{:S(2)}) collective-permute-start(f32[2048,8]{0,1:T(8,128)S(1)} %convolution_bitcast_fusion), channel_id=1, source_target_pairs={{0,48},{8,56},{16,32},{24,40},{32,16},{40,24},{48,0},{56,8},{64,11... | collective-permute-start | bytes 196616 | tf_op jit(solution)/shard_map/ppermute | solution.py:19
  187.3 10.1 %collective-permute-start.4 = (f32[2048,8]{0,1:T(8,128)S(1)}, f32[2048,8]{0,1:T(8,128)S(1)}, u32[]{:S(2)}, u32[]{:S(2)}) collective-permute-start(f32[2048,8]{0,1:T(8,128)S(1)} %convolution_bitcast_fusion), channel_id=1, source_target_pairs={{0,40},{8,32},{16,56},{24,48},{32,8},{40,0},{48,24},{56,16},{64,10... | collective-permute-start | bytes 196616 | tf_op jit(solution)/shard_map/ppermute | solution.py:19
  189.1 8.3 %collective-permute-start.3 = (f32[2048,8]{0,1:T(8,128)S(1)}, f32[2048,8]{0,1:T(8,128)S(1)}, u32[]{:S(2)}, u32[]{:S(2)}) collective-permute-start(f32[2048,8]{0,1:T(8,128)S(1)} %convolution_bitcast_fusion), channel_id=1, source_target_pairs={{0,32},{8,40},{16,48},{24,56},{32,0},{40,8},{48,16},{56,24},{64,96... | collective-permute-start | bytes 196616 | tf_op jit(solution)/shard_map/ppermute | solution.py:19
  190.4 9.9 %collective-permute-start.2 = (f32[2048,8]{0,1:T(8,128)S(1)}, f32[2048,8]{0,1:T(8,128)S(1)}, u32[]{:S(2)}, u32[]{:S(2)}) collective-permute-start(f32[2048,8]{0,1:T(8,128)S(1)} %convolution_bitcast_fusion), channel_id=1, source_target_pairs={{0,24},{8,16},{16,8},{24,0},{32,56},{40,48},{48,40},{56,32},{64,88... | collective-permute-start | bytes 196616 | tf_op jit(solution)/shard_map/ppermute | solution.py:19
  191.6 11.2 %collective-permute-start.1 = (f32[2048,8]{0,1:T(8,128)S(1)}, f32[2048,8]{0,1:T(8,128)S(1)}, u32[]{:S(2)}, u32[]{:S(2)}) collective-permute-start(f32[2048,8]{0,1:T(8,128)S(1)} %convolution_bitcast_fusion), channel_id=1, source_target_pairs={{0,16},{8,24},{16,0},{24,8},{32,48},{40,56},{48,32},{56,40},{64,80... | collective-permute-start | bytes 196616 | tf_op jit(solution)/shard_map/ppermute | solution.py:19
  197.0 5.8 %collective-permute-start = (f32[2048,8]{0,1:T(8,128)S(1)}, f32[2048,8]{0,1:T(8,128)S(1)}, u32[]{:S(2)}, u32[]{:S(2)}) collective-permute-start(f32[2048,8]{0,1:T(8,128)S(1)} %convolution_bitcast_fusion), channel_id=1, source_target_pairs={{0,8},{8,0},{16,24},{24,16},{32,40},{40,32},{48,56},{56,48},{64,72... | collective-permute-start | bytes 196616 | tf_op jit(solution)/shard_map/ppermute | solution.py:19
  202.8 5.0 %collective-permute-start.9 = (f32[2048,8]{0,1:T(8,128)S(1)}, f32[2048,8]{0,1:T(8,128)S(1)}, u32[]{:S(2)}, u32[]{:S(2)}) collective-permute-start(f32[2048,8]{0,1:T(8,128)S(1)} %add_add_fusion.2), channel_id=1, source_target_pairs={{0,192},{8,200},{16,208},{24,216},{32,224},{40,232},{48,240},{56,2... | collective-permute-start | bytes 196616 | tf_op jit(solution)/shard_map/ppermute | solution.py:19
  205.7 4.6 %collective-permute-start.8 = (f32[2048,8]{0,1:T(8,128)S(1)}, f32[2048,8]{0,1:T(8,128)S(1)}, u32[]{:S(2)}, u32[]{:S(2)}) collective-permute-start(f32[2048,8]{0,1:T(8,128)S(1)} %add_add_fusion.2), channel_id=1, source_target_pairs={{0,128},{8,136},{16,144},{24,152},{32,160},{40,168},{48,176},{56,1... | collective-permute-start | bytes 196616 | tf_op jit(solution)/shard_map/ppermute | solution.py:19
  206.2 4.1 %collective-permute-start.7 = (f32[2048,8]{0,1:T(8,128)S(1)}, f32[2048,8]{0,1:T(8,128)S(1)}, u32[]{:S(2)}, u32[]{:S(2)}) collective-permute-start(f32[2048,8]{0,1:T(8,128)S(1)} %add_add_fusion.2), channel_id=1, source_target_pairs={{0,64},{8,72},{16,80},{24,88},{32,96},{40,104},{48,112},{56,120},{... | collective-permute-start | bytes 196616 | tf_op jit(solution)/shard_map/ppermute | solution.py:19
  210.3 15.7 %collective-permute-start.16 = (f32[2048,8]{0,1:T(8,128)S(1)}, f32[2048,8]{0,1:T(8,128)S(1)}, u32[]{:S(2)}, u32[]{:S(2)}) collective-permute-start(f32[2048,8]{0,1:T(8,128)S(1)} %add_add_fusion.1), channel_id=1, source_target_pairs={{0,7},{1,6},{2,5},{3,4},{4,3},{5,2},{6,1},{7,0},{8,15},{9,14},{10,... | collective-permute-start | bytes 196616 | tf_op jit(solution)/shard_map/ppermute | solution.py:19
  213.4 13.4 %collective-permute-start.15 = (f32[2048,8]{0,1:T(8,128)S(1)}, f32[2048,8]{0,1:T(8,128)S(1)}, u32[]{:S(2)}, u32[]{:S(2)}) collective-permute-start(f32[2048,8]{0,1:T(8,128)S(1)} %add_add_fusion.1), channel_id=1, source_target_pairs={{0,6},{1,7},{2,4},{3,5},{4,2},{5,3},{6,0},{7,1},{8,14},{9,15},{10,... | collective-permute-start | bytes 196616 | tf_op jit(solution)/shard_map/ppermute | solution.py:19
  217.4 11.9 %copy-start.6 = (f32[2048,8]{0,1:T(8,128)S(1)}, f32[2048,8]{0,1:T(8,128)}, u32[]{:S(2)}) copy-start(f32[2048,8]{0,1:T(8,128)} %param.11) | copy-start | bytes 196612
  219.9 11.2 %collective-permute-start.14 = (f32[2048,8]{0,1:T(8,128)S(1)}, f32[2048,8]{0,1:T(8,128)S(1)}, u32[]{:S(2)}, u32[]{:S(2)}) collective-permute-start(f32[2048,8]{0,1:T(8,128)S(1)} %add_add_fusion.1), channel_id=1, source_target_pairs={{0,5},{1,4},{2,7},{3,6},{4,1},{5,0},{6,3},{7,2},{8,13},{9,12},{10,... | collective-permute-start | bytes 196616 | tf_op jit(solution)/shard_map/ppermute | solution.py:19
  221.3 9.8 %collective-permute-start.13 = (f32[2048,8]{0,1:T(8,128)S(1)}, f32[2048,8]{0,1:T(8,128)S(1)}, u32[]{:S(2)}, u32[]{:S(2)}) collective-permute-start(f32[2048,8]{0,1:T(8,128)S(1)} %add_add_fusion.1), channel_id=1, source_target_pairs={{0,4},{1,5},{2,6},{3,7},{4,0},{5,1},{6,2},{7,3},{8,12},{9,13},{10,... | collective-permute-start | bytes 196616 | tf_op jit(solution)/shard_map/ppermute | solution.py:19
  225.7 5.5 %collective-permute-start.12 = (f32[2048,8]{0,1:T(8,128)S(1)}, f32[2048,8]{0,1:T(8,128)S(1)}, u32[]{:S(2)}, u32[]{:S(2)}) collective-permute-start(f32[2048,8]{0,1:T(8,128)S(1)} %add_add_fusion.1), channel_id=1, source_target_pairs={{0,3},{1,2},{2,1},{3,0},{4,7},{5,6},{6,5},{7,4},{8,11},{9,10},{10,... | collective-permute-start | bytes 196616 | tf_op jit(solution)/shard_map/ppermute | solution.py:19
  226.0 10.6 %collective-permute-start.11 = (f32[2048,8]{0,1:T(8,128)S(1)}, f32[2048,8]{0,1:T(8,128)S(1)}, u32[]{:S(2)}, u32[]{:S(2)}) collective-permute-start(f32[2048,8]{0,1:T(8,128)S(1)} %add_add_fusion.1), channel_id=1, source_target_pairs={{0,2},{1,3},{2,0},{3,1},{4,6},{5,7},{6,4},{7,5},{8,10},{9,11},{10,... | collective-permute-start | bytes 196616 | tf_op jit(solution)/shard_map/ppermute | solution.py:19
  226.8 9.8 %collective-permute-start.10 = (f32[2048,8]{0,1:T(8,128)S(1)}, f32[2048,8]{0,1:T(8,128)S(1)}, u32[]{:S(2)}, u32[]{:S(2)}) collective-permute-start(f32[2048,8]{0,1:T(8,128)S(1)} %add_add_fusion.1), channel_id=1, source_target_pairs={{0,1},{1,0},{2,3},{3,2},{4,5},{5,4},{6,7},{7,6},{8,9},{9,8},{10,11... | collective-permute-start | bytes 196616 | tf_op jit(solution)/shard_map/ppermute | solution.py:19
Sparse Core Ops, SparseCore 0:
  125.6 105.3 reduce-scatter.1

commit v10 on v5

--- a/solution.py
+++ b/solution.py
@@ -141,11 +141,17 @@
             .reshape(lax.axis_size("dp") * own_rows, local_count * 3 * hidden_width)
             .astype(jnp.bfloat16)
         )
-    joined = lax.psum_scatter(partials, "dp", scatter_dimension=0, tiled=True).astype(jnp.float32)
-    triple_view = joined.reshape(-1, local_count, 3, hidden_width)
-    grad_gate = jnp.transpose(triple_view[:, :, 0, :], (1, 0, 2))
-    grad_up = jnp.transpose(triple_view[:, :, 1, :], (1, 0, 2))
-    grad_down = jnp.transpose(triple_view[:, :, 2, :], (1, 0, 2))
+    joined = lax.psum_scatter(partials, "dp", scatter_dimension=0, tiled=True)
+    if local_count == 1:
+        grad_gate, grad_up, grad_down = (
+            joined[None, :, which * hidden_width : (which + 1) * hidden_width].astype(jnp.float32)
+            for which in range(3)
+        )
+    else:
+        triple_view = joined.astype(jnp.float32).reshape(-1, local_count, 3, hidden_width)
+        grad_gate = jnp.transpose(triple_view[:, :, 0, :], (1, 0, 2))
+        grad_up = jnp.transpose(triple_view[:, :, 1, :], (1, 0, 2))
+        grad_down = jnp.transpose(triple_view[:, :, 2, :], (1, 0, 2))
     choice_rows = jnp.transpose(chosen, (1, 0, 2)).reshape(choice_count * tok_count, slot_total)
     choice_rows = choice_rows.astype(jnp.bfloat16)
     got_rows = jnp.dot(

time: 241 us -> 236 us (0.979)
  local copies, waits for them, and re-layouts: 10 us -> 3.55 us
  transfers between devices with their start and end apart: 20 -> 20, of which waited for: 9 -> 9; matrix products, arithmetic and copies ran while one was open for 8% -> 9% of each run, Pallas kernels for 0% -> 0%
where the time goes in v10:
time: 236 us
  blocking collectives  81.3 us (34%)
  waiting for transfers between devices  56.9 us (24%)
  starting transfers between devices  34.6 us (15%)
  matrix products  27.5 us (12%)
  between operations  14.3 us (6%)
  Pallas kernels  9.27 us (4%)
  other arithmetic  8.13 us (3%)
  local copies, waits for them, and re-layouts  3.55 us (2%)
    all_to_all x1, blocking collectives, on_device(): lax.all_to_all(jnp.concatenate([outgoing, grad_rows], axis=1), 'expert',...  81.3 us
    all_to_all x1, waiting for transfers between devices, on_device(): lax.all_to_all(expert_out.reshape(flat_rows), 'expert', split_axis=0, con...  34.3 us
    ppermute x17, starting transfers between devices, group_sum(): got.append(lax.ppermute(value, axis, pairs))  25.8 us
    ppermute x17, waiting for transfers between devices, group_sum(): got.append(lax.ppermute(value, axis, pairs))  20.2 us
    pallas_call x1, Pallas kernels, weight_grads(): pl.pallas_call(weight_grad_kernel, grid=(width // tile,), in_specs=[pl.Bl...  9.27 us
  transfers between devices with their start and end apart: 20, of which 9 were waited for; matrix products, arithmetic and copies ran while one was open for 9% of the time, Pallas kernels for 0%

profile of v10, /device:TPU:1, one launch (start us, length us, event | category | flops | bytes accessed | tf_op | source)
XLA Modules:
  0.0 235.5 jit_solution(10092235966472049588)
XLA Ops:
  8.1 1.7 fusion.30
  11.5 1.7 convolution_convert_fusion
  14.3 81.3 %all_to_all.15 = bf16[8,96,2048]{2,1,0:T(8,128)(2,1)S(1)} all-to-all(bf16[8,96,2048]{2,1,0:T(8,128)(2,1)S(1)} %pad_maximum_fusion), channel_id=1, replica_groups=mesh['dp'=32,'expert'=8] {'expert'}, dimensions={0} | all-to-all | bytes 6291456 | tf_op jit(solution)/shard_map/all_to_all | solution.py:95
  95.6 1.4 fusion.21
  97.5 1.4 fusion.24
  98.9 2.6 %multiply_convert_fusion.2 = (bf16[8,1,48,768]{3,2,0,1:T(8,128)(2,1)S(1)}, bf16[8,1,48,768]{3,2,0,1:T(8,128)(2,1)S(1)}, bf16[8,1,48,768]{3,2,0,1:T(8,128)(2,1)}) fusion(f32[8,1,48,768]{3,2,0,1:T(8,128)S(1)} %fusion.24, f32[8,1,48,768]{3,2,0,1:T(8,128)S(1)} %fusion.21, bf16[1,2048,768]{2,1,0:T(8,128)(2,1)S(1)} %copy-done, ...), kind=kOutput, calls=%fused_computation.28 | convolution fusion | flops 1212383232 | bytes 8847360 | tf_op jit(solution)/shard_map/slnd,ldf->slnf/dot_general | solution.py:101
  103.8 2.0 fusion.49
  105.8 9.3 %shard_map.127 = bf16[2048,2304]{1,0:T(8,128)(2,1)} custom-call(bf16[384,2048]{1,0:T(8,128)(2,1)} %bitcast.108, bf16[384,2048]{1,0:T(8,128)(2,1)} %bitcast.107, bf16[384,1536]{1,0:T(8,128)(2,1)} %pad_maximum_fusion.1.deltas_ref, bf16[384,768]{1,0:T(8,128)(2,1)} %bitcast.111), custom_call_target="tpu_custom_call" | custom-call | tf_op jit(solution)/shard_map/pallas_call | solution.py:50
  115.1 4.7 %fusion.14 = bf16[8,48,2048]{2,1,0:T(8,128)(2,1)} fusion(bf16[1,2048,768]{2,1,0:T(8,128)(2,1)} %param.14, bf16[8,1,48,768]{3,2,0,1:T(8,128)(2,1)} %get-tuple-element.16), kind=kOutput, calls=%fused_computation.15 | convolution fusion | flops 1208745984 | bytes 5308416 | tf_op jit(solution)/shard_map/slnf,ldf->slnd/dot_general | solution.py:109
  119.7 4.3 %all-to-all-start.1 = ((bf16[8,48,2048]{2,1,0:T(8,128)(2,1)}), bf16[8,48,2048]{2,1,0:T(8,128)(2,1)}, u32[]{:S(2)}, u32[]{:S(2)}) async-start(bf16[8,48,2048]{2,1,0:T(8,128)(2,1)} %fusion.14), calls=%async_computation.1 | async-start | bytes 3145728 | tf_op jit(solution)/shard_map/all_to_all | solution.py:113
  124.0 3.5 %fusion.4 = f32[8,48,2048]{2,1,0:T(8,128)S(1)} fusion(bf16[1,2048,768]{2,1,0:T(8,128)(2,1)} %param.13, bf16[8,1,48,768]{3,2,0,1:T(8,128)(2,1)} %copy-done.6), kind=kOutput, calls=%fused_computation.5 | convolution fusion | flops 1207959552 | bytes 6881280 | tf_op jit(solution)/shard_map/slnf,ldf->slnd/dot_general | solution.py:121
  127.6 2.6 %add_convert_fusion = bf16[8,48,2048]{2,1,0:T(8,128)(2,1)} fusion(f32[8,48,2048]{2,1,0:T(8,128)S(1)} %fusion.4, bf16[1,2048,768]{2,1,0:T(8,128)(2,1)S(1)} %copy-done, bf16[8,1,48,768]{3,2,0,1:T(8,128)(2,1)S(1)} %copy-done.5), kind=kOutput, calls=%fused_computation.13 | convolution fusion | flops 1209532416 | bytes 8454144 | tf_op jit(solution)/shard_map/slnf,ldf->slnd/dot_general | solution.py:120
  130.2 34.3 %all-to-all-done.1 = bf16[8,48,2048]{2,1,0:T(8,128)(2,1)} async-done(((bf16[8,48,2048]{2,1,0:T(8,128)(2,1)}), bf16[8,48,2048]{2,1,0:T(8,128)(2,1)}, u32[]{:S(2)}, u32[]{:S(2)}) %all-to-all-start.1) | async-done | bytes 1572896 | tf_op jit(solution)/shard_map/all_to_all | solution.py:113
  164.5 4.5 %all-to-all-start.2 = ((bf16[8,48,2048]{2,1,0:T(8,128)(2,1)}), bf16[8,48,2048]{2,1,0:T(8,128)(2,1)}, u32[]{:S(2)}, u32[]{:S(2)}) async-start(bf16[8,48,2048]{2,1,0:T(8,128)(2,1)} %add_convert_fusion), calls=%async_computation.2 | async-start | bytes 3145728 | tf_op jit(solution)/shard_map/all_to_all | solution.py:123
  169.0 2.6 %fusion.39 = f32[384,2048]{1,0:T(8,128)S(1)} fusion(bf16[384,2048]{1,0:T(8,128)(2,1)} %bitcast.20, s32[384]{0:T(512)S(1)} %bitcast.114), kind=kOutput, calls=%fused_computation.50 | convolution fusion | flops 604127232 | bytes 4720128 | tf_op jit(solution)/shard_map/dot_general | solution.py:157
  173.4 3.1 %collective-permute-start.6 = (f32[2048,8]{0,1:T(8,128)S(1)}, f32[2048,8]{0,1:T(8,128)S(1)}, u32[]{:S(2)}, u32[]{:S(2)}) collective-permute-start(f32[2048,8]{0,1:T(8,128)S(1)} %convolution_bitcast_fusion), channel_id=1, source_target_pairs={{0,56},{8,48},{16,40},{24,32},{32,24},{40,16},{48,8},{56,0},{64,12... | collective-permute-start | bytes 196616 | tf_op jit(solution)/shard_map/ppermute | solution.py:19
  176.7 1.7 collective-permute-start.4
  178.4 1.5 collective-permute-start.3
  181.8 4.7 %collective-permute-done.5 = f32[2048,8]{0,1:T(8,128)S(1)} collective-permute-done((f32[2048,8]{0,1:T(8,128)S(1)}, f32[2048,8]{0,1:T(8,128)S(1)}, u32[]{:S(2)}, u32[]{:S(2)}) %collective-permute-start.5) | collective-permute-done | bytes 65568 | tf_op jit(solution)/shard_map/ppermute | solution.py:19
  186.8 3.1 %collective-permute-done.2 = f32[2048,8]{0,1:T(8,128)S(1)} collective-permute-done((f32[2048,8]{0,1:T(8,128)S(1)}, f32[2048,8]{0,1:T(8,128)S(1)}, u32[]{:S(2)}, u32[]{:S(2)}) %collective-permute-start.2) | collective-permute-done | bytes 65568 | tf_op jit(solution)/shard_map/ppermute | solution.py:19
  189.9 2.2 collective-permute-done.1
  192.1 2.9 %collective-permute-start.9 = (f32[2048,8]{0,1:T(8,128)S(1)}, f32[2048,8]{0,1:T(8,128)S(1)}, u32[]{:S(2)}, u32[]{:S(2)}) collective-permute-start(f32[2048,8]{0,1:T(8,128)S(1)} %add_add_fusion.2), channel_id=1, source_target_pairs={{0,192},{8,200},{16,208},{24,216},{32,224},{40,232},{48,240},{56,2... | collective-permute-start | bytes 196616 | tf_op jit(solution)/shard_map/ppermute | solution.py:19
  197.1 2.6 %collective-permute-done.8 = f32[2048,8]{0,1:T(8,128)S(1)} collective-permute-done((f32[2048,8]{0,1:T(8,128)S(1)}, f32[2048,8]{0,1:T(8,128)S(1)}, u32[]{:S(2)}, u32[]{:S(2)}) %collective-permute-start.8) | collective-permute-done | bytes 65568 | tf_op jit(solution)/shard_map/ppermute | solution.py:19
  199.7 3.3 %collective-permute-start.16 = (f32[2048,8]{0,1:T(8,128)S(1)}, f32[2048,8]{0,1:T(8,128)S(1)}, u32[]{:S(2)}, u32[]{:S(2)}) collective-permute-start(f32[2048,8]{0,1:T(8,128)S(1)} %add_add_fusion.1), channel_id=1, source_target_pairs={{0,7},{1,6},{2,5},{3,4},{4,3},{5,2},{6,1},{7,0},{8,15},{9,14},{10,... | collective-permute-start | bytes 196616 | tf_op jit(solution)/shard_map/ppermute | solution.py:19
  203.0 1.6 collective-permute-start.15
  204.6 2.4 %all-to-all-done.2 = bf16[8,48,2048]{2,1,0:T(8,128)(2,1)} async-done(((bf16[8,48,2048]{2,1,0:T(8,128)(2,1)}), bf16[8,48,2048]{2,1,0:T(8,128)(2,1)}, u32[]{:S(2)}, u32[]{:S(2)}) %all-to-all-start.2) | async-done | bytes 1572896 | tf_op jit(solution)/shard_map/all_to_all | solution.py:123
  207.0 2.5 %fusion.38 = f32[384,2048]{1,0:T(8,128)S(1)} fusion(bf16[384,2048]{1,0:T(8,128)(2,1)} %bitcast.32, s32[384]{0:T(512)S(1)} %bitcast.115), kind=kOutput, calls=%fused_computation.49 | convolution fusion | flops 604127232 | bytes 4720128 | tf_op jit(solution)/shard_map/dot_general | solution.py:160
  210.7 4.6 %collective-permute-start.13 = (f32[2048,8]{0,1:T(8,128)S(1)}, f32[2048,8]{0,1:T(8,128)S(1)}, u32[]{:S(2)}, u32[]{:S(2)}) collective-permute-start(f32[2048,8]{0,1:T(8,128)S(1)} %add_add_fusion.1), channel_id=1, source_target_pairs={{0,4},{1,5},{2,6},{3,7},{4,0},{5,1},{6,2},{7,3},{8,12},{9,13},{10,... | collective-permute-start | bytes 196616 | tf_op jit(solution)/shard_map/ppermute | solution.py:19
  216.4 2.5 %collective-permute-start.10 = (f32[2048,8]{0,1:T(8,128)S(1)}, f32[2048,8]{0,1:T(8,128)S(1)}, u32[]{:S(2)}, u32[]{:S(2)}) collective-permute-start(f32[2048,8]{0,1:T(8,128)S(1)} %add_add_fusion.1), channel_id=1, source_target_pairs={{0,1},{1,0},{2,3},{3,2},{4,5},{5,4},{6,7},{7,6},{8,9},{9,8},{10,11... | collective-permute-start | bytes 196616 | tf_op jit(solution)/shard_map/ppermute | solution.py:19
  218.9 1.9 fusion.17
  220.7 5.5 %collective-permute-done.11 = f32[2048,8]{0,1:T(8,128)S(1)} collective-permute-done((f32[2048,8]{0,1:T(8,128)S(1)}, f32[2048,8]{0,1:T(8,128)S(1)}, u32[]{:S(2)}, u32[]{:S(2)}) %collective-permute-start.11) | collective-permute-done | bytes 65568 | tf_op jit(solution)/shard_map/ppermute | solution.py:19
  226.9 1.8 fusion.42
  (63 shorter events, 15.6 us)
Async XLA Ops:
  7.2 91.8 %copy-start = (bf16[1,2048,768]{2,1,0:T(8,128)(2,1)S(1)}, bf16[1,2048,768]{2,1,0:T(8,128)(2,1)}, u32[]{:S(2)}) copy-start(bf16[1,2048,768]{2,1,0:T(8,128)(2,1)} %param.12) | copy-start | bytes 9437188
  7.2 219.7 %reduce-scatter.2.cloned.1.call-start = ((), (), s32[]{:S(2)}) async-start(), calls=%async_computation.4 | async-start | bytes 9732096 | tf_op jit(solution)/shard_map/reduce_scatter | solution.py:144
  7.2 6.0 %copy-start.2 = (bf16[128,2048]{1,0:T(8,128)(2,1)S(1)}, bf16[128,2048]{1,0:T(8,128)(2,1)}, u32[]{:S(2)}) copy-start(bf16[128,2048]{1,0:T(8,128)(2,1)} %param.15) | copy-start | bytes 1572868
  14.3 81.4 %copy-start.10 = (bf16[1,2048,768]{2,1,0:T(8,128)(2,1)S(1)}, bf16[1,2048,768]{2,1,0:T(8,128)(2,1)}, u32[]{:S(2)}) copy-start(bf16[1,2048,768]{2,1,0:T(8,128)(2,1)} %param.13) | copy-start | bytes 9437188
  95.6 1.9 copy-start.9
  101.6 0.8 copy-start.4
  101.6 1.0 copy-start.6
  119.7 44.7 %all-to-all-start.1 = ((bf16[8,48,2048]{2,1,0:T(8,128)(2,1)}), bf16[8,48,2048]{2,1,0:T(8,128)(2,1)}, u32[]{:S(2)}, u32[]{:S(2)}) async-start(bf16[8,48,2048]{2,1,0:T(8,128)(2,1)} %fusion.14), calls=%async_computation.1 | async-start | bytes 3145728 | tf_op jit(solution)/shard_map/all_to_all | solution.py:113
  124.0 3.6 %copy-start.5 = (bf16[8,1,48,768]{3,2,0,1:T(8,128)(2,1)S(1)}, bf16[8,1,48,768]{3,2,0,1:T(8,128)(2,1)}, u32[]{:S(2)}) copy-start(bf16[8,1,48,768]{3,2,0,1:T(8,128)(2,1)} %copy-done.4) | copy-start | bytes 1769476
  164.5 42.5 %all-to-all-start.2 = ((bf16[8,48,2048]{2,1,0:T(8,128)(2,1)}), bf16[8,48,2048]{2,1,0:T(8,128)(2,1)}, u32[]{:S(2)}, u32[]{:S(2)}) async-start(bf16[8,48,2048]{2,1,0:T(8,128)(2,1)} %add_convert_fusion), calls=%async_computation.2 | async-start | bytes 3145728 | tf_op jit(solution)/shard_map/all_to_all | solution.py:123
  168.9 2.7 %copy-start.3 = (bf16[128,2048]{1,0:T(8,128)(2,1)S(1)}, bf16[128,2048]{1,0:T(8,128)(2,1)}, u32[]{:S(2)}) copy-start(bf16[128,2048]{1,0:T(8,128)(2,1)} %param.15) | copy-start | bytes 1572868
  171.6 1.5 copy-start.8
  171.6 1.5 copy-start.1
  173.4 7.6 %collective-permute-start.6 = (f32[2048,8]{0,1:T(8,128)S(1)}, f32[2048,8]{0,1:T(8,128)S(1)}, u32[]{:S(2)}, u32[]{:S(2)}) collective-permute-start(f32[2048,8]{0,1:T(8,128)S(1)} %convolution_bitcast_fusion), channel_id=1, source_target_pairs={{0,56},{8,48},{16,40},{24,32},{32,24},{40,16},{48,8},{56,0},{64,12... | collective-permute-start | bytes 196616 | tf_op jit(solution)/shard_map/ppermute | solution.py:19
  176.5 9.9 %collective-permute-start.5 = (f32[2048,8]{0,1:T(8,128)S(1)}, f32[2048,8]{0,1:T(8,128)S(1)}, u32[]{:S(2)}, u32[]{:S(2)}) collective-permute-start(f32[2048,8]{0,1:T(8,128)S(1)} %convolution_bitcast_fusion), channel_id=1, source_target_pairs={{0,48},{8,56},{16,32},{24,40},{32,16},{40,24},{48,0},{56,8},{64,11... | collective-permute-start | bytes 196616 | tf_op jit(solution)/shard_map/ppermute | solution.py:19
  176.7 10.0 %collective-permute-start.4 = (f32[2048,8]{0,1:T(8,128)S(1)}, f32[2048,8]{0,1:T(8,128)S(1)}, u32[]{:S(2)}, u32[]{:S(2)}) collective-permute-start(f32[2048,8]{0,1:T(8,128)S(1)} %convolution_bitcast_fusion), channel_id=1, source_target_pairs={{0,40},{8,32},{16,56},{24,48},{32,8},{40,0},{48,24},{56,16},{64,10... | collective-permute-start | bytes 196616 | tf_op jit(solution)/shard_map/ppermute | solution.py:19
  178.4 8.3 %collective-permute-start.3 = (f32[2048,8]{0,1:T(8,128)S(1)}, f32[2048,8]{0,1:T(8,128)S(1)}, u32[]{:S(2)}, u32[]{:S(2)}) collective-permute-start(f32[2048,8]{0,1:T(8,128)S(1)} %convolution_bitcast_fusion), channel_id=1, source_target_pairs={{0,32},{8,40},{16,48},{24,56},{32,0},{40,8},{48,16},{56,24},{64,96... | collective-permute-start | bytes 196616 | tf_op jit(solution)/shard_map/ppermute | solution.py:19
  179.9 10.0 %collective-permute-start.2 = (f32[2048,8]{0,1:T(8,128)S(1)}, f32[2048,8]{0,1:T(8,128)S(1)}, u32[]{:S(2)}, u32[]{:S(2)}) collective-permute-start(f32[2048,8]{0,1:T(8,128)S(1)} %convolution_bitcast_fusion), channel_id=1, source_target_pairs={{0,24},{8,16},{16,8},{24,0},{32,56},{40,48},{48,40},{56,32},{64,88... | collective-permute-start | bytes 196616 | tf_op jit(solution)/shard_map/ppermute | solution.py:19
  181.0 11.1 %collective-permute-start.1 = (f32[2048,8]{0,1:T(8,128)S(1)}, f32[2048,8]{0,1:T(8,128)S(1)}, u32[]{:S(2)}, u32[]{:S(2)}) collective-permute-start(f32[2048,8]{0,1:T(8,128)S(1)} %convolution_bitcast_fusion), channel_id=1, source_target_pairs={{0,16},{8,24},{16,0},{24,8},{32,48},{40,56},{48,32},{56,40},{64,80... | collective-permute-start | bytes 196616 | tf_op jit(solution)/shard_map/ppermute | solution.py:19
  186.4 5.7 %collective-permute-start = (f32[2048,8]{0,1:T(8,128)S(1)}, f32[2048,8]{0,1:T(8,128)S(1)}, u32[]{:S(2)}, u32[]{:S(2)}) collective-permute-start(f32[2048,8]{0,1:T(8,128)S(1)} %convolution_bitcast_fusion), channel_id=1, source_target_pairs={{0,8},{8,0},{16,24},{24,16},{32,40},{40,32},{48,56},{56,48},{64,72... | collective-permute-start | bytes 196616 | tf_op jit(solution)/shard_map/ppermute | solution.py:19
  192.1 4.9 %collective-permute-start.9 = (f32[2048,8]{0,1:T(8,128)S(1)}, f32[2048,8]{0,1:T(8,128)S(1)}, u32[]{:S(2)}, u32[]{:S(2)}) collective-permute-start(f32[2048,8]{0,1:T(8,128)S(1)} %add_add_fusion.2), channel_id=1, source_target_pairs={{0,192},{8,200},{16,208},{24,216},{32,224},{40,232},{48,240},{56,2... | collective-permute-start | bytes 196616 | tf_op jit(solution)/shard_map/ppermute | solution.py:19
  195.0 4.6 %collective-permute-start.8 = (f32[2048,8]{0,1:T(8,128)S(1)}, f32[2048,8]{0,1:T(8,128)S(1)}, u32[]{:S(2)}, u32[]{:S(2)}) collective-permute-start(f32[2048,8]{0,1:T(8,128)S(1)} %add_add_fusion.2), channel_id=1, source_target_pairs={{0,128},{8,136},{16,144},{24,152},{32,160},{40,168},{48,176},{56,1... | collective-permute-start | bytes 196616 | tf_op jit(solution)/shard_map/ppermute | solution.py:19
  195.6 4.1 %collective-permute-start.7 = (f32[2048,8]{0,1:T(8,128)S(1)}, f32[2048,8]{0,1:T(8,128)S(1)}, u32[]{:S(2)}, u32[]{:S(2)}) collective-permute-start(f32[2048,8]{0,1:T(8,128)S(1)} %add_add_fusion.2), channel_id=1, source_target_pairs={{0,64},{8,72},{16,80},{24,88},{32,96},{40,104},{48,112},{56,120},{... | collective-permute-start | bytes 196616 | tf_op jit(solution)/shard_map/ppermute | solution.py:19
  199.7 15.9 %collective-permute-start.16 = (f32[2048,8]{0,1:T(8,128)S(1)}, f32[2048,8]{0,1:T(8,128)S(1)}, u32[]{:S(2)}, u32[]{:S(2)}) collective-permute-start(f32[2048,8]{0,1:T(8,128)S(1)} %add_add_fusion.1), channel_id=1, source_target_pairs={{0,7},{1,6},{2,5},{3,4},{4,3},{5,2},{6,1},{7,0},{8,15},{9,14},{10,... | collective-permute-start | bytes 196616 | tf_op jit(solution)/shard_map/ppermute | solution.py:19
  203.0 13.4 %collective-permute-start.15 = (f32[2048,8]{0,1:T(8,128)S(1)}, f32[2048,8]{0,1:T(8,128)S(1)}, u32[]{:S(2)}, u32[]{:S(2)}) collective-permute-start(f32[2048,8]{0,1:T(8,128)S(1)} %add_add_fusion.1), channel_id=1, source_target_pairs={{0,6},{1,7},{2,4},{3,5},{4,2},{5,3},{6,0},{7,1},{8,14},{9,15},{10,... | collective-permute-start | bytes 196616 | tf_op jit(solution)/shard_map/ppermute | solution.py:19
  207.0 11.9 %copy-start.7 = (f32[2048,8]{0,1:T(8,128)S(1)}, f32[2048,8]{0,1:T(8,128)}, u32[]{:S(2)}) copy-start(f32[2048,8]{0,1:T(8,128)} %param.11) | copy-start | bytes 196612
  209.4 11.3 %collective-permute-start.14 = (f32[2048,8]{0,1:T(8,128)S(1)}, f32[2048,8]{0,1:T(8,128)S(1)}, u32[]{:S(2)}, u32[]{:S(2)}) collective-permute-start(f32[2048,8]{0,1:T(8,128)S(1)} %add_add_fusion.1), channel_id=1, source_target_pairs={{0,5},{1,4},{2,7},{3,6},{4,1},{5,0},{6,3},{7,2},{8,13},{9,12},{10,... | collective-permute-start | bytes 196616 | tf_op jit(solution)/shard_map/ppermute | solution.py:19
  210.7 10.1 %collective-permute-start.13 = (f32[2048,8]{0,1:T(8,128)S(1)}, f32[2048,8]{0,1:T(8,128)S(1)}, u32[]{:S(2)}, u32[]{:S(2)}) collective-permute-start(f32[2048,8]{0,1:T(8,128)S(1)} %add_add_fusion.1), channel_id=1, source_target_pairs={{0,4},{1,5},{2,6},{3,7},{4,0},{5,1},{6,2},{7,3},{8,12},{9,13},{10,... | collective-permute-start | bytes 196616 | tf_op jit(solution)/shard_map/ppermute | solution.py:19
  215.3 5.4 %collective-permute-start.12 = (f32[2048,8]{0,1:T(8,128)S(1)}, f32[2048,8]{0,1:T(8,128)S(1)}, u32[]{:S(2)}, u32[]{:S(2)}) collective-permute-start(f32[2048,8]{0,1:T(8,128)S(1)} %add_add_fusion.1), channel_id=1, source_target_pairs={{0,3},{1,2},{2,1},{3,0},{4,7},{5,6},{6,5},{7,4},{8,11},{9,10},{10,... | collective-permute-start | bytes 196616 | tf_op jit(solution)/shard_map/ppermute | solution.py:19
  215.6 10.6 %collective-permute-start.11 = (f32[2048,8]{0,1:T(8,128)S(1)}, f32[2048,8]{0,1:T(8,128)S(1)}, u32[]{:S(2)}, u32[]{:S(2)}) collective-permute-start(f32[2048,8]{0,1:T(8,128)S(1)} %add_add_fusion.1), channel_id=1, source_target_pairs={{0,2},{1,3},{2,0},{3,1},{4,6},{5,7},{6,4},{7,5},{8,10},{9,11},{10,... | collective-permute-start | bytes 196616 | tf_op jit(solution)/shard_map/ppermute | solution.py:19
  216.4 9.8 %collective-permute-start.10 = (f32[2048,8]{0,1:T(8,128)S(1)}, f32[2048,8]{0,1:T(8,128)S(1)}, u32[]{:S(2)}, u32[]{:S(2)}) collective-permute-start(f32[2048,8]{0,1:T(8,128)S(1)} %add_add_fusion.1), channel_id=1, source_target_pairs={{0,1},{1,0},{2,3},{3,2},{4,5},{5,4},{6,7},{7,6},{8,9},{9,8},{10,11... | collective-permute-start | bytes 196616 | tf_op jit(solution)/shard_map/ppermute | solution.py:19
Sparse Core Ops, SparseCore 0:
  115.2 104.9 reduce-scatter.1
